TPU v7x, 256 devices: a whole 4x4x8 slice. The times are simulated.
256 devices in a mesh: tiles: 64 (over z, x, core), views: 4 (over y).
Axes of the slice: x: 4, y: 4, z: 8, core: 2. Of those that a mesh axis runs over, the one named last changes fastest.
Arguments:
- gaussians: float32 [59, 131072], P(None, 'tiles')
- moment_one: float32 [59, 131072], P(None, 'tiles'), may hold values from -3 to 3
- moment_two: float32 [59, 131072], P(None, 'tiles'), may hold values from 0.01 to 1
- learn_rates: float32 [59], replicated, may hold values from 0.002 to 0.05
- cameras: float32 [16, 12], replicated, as said below
- camera_ids: int32 [4], P('views'), may hold values from 0 to 15
- list_owner: int32 [4, 64, 1024, 1], P('views', 'tiles'), may hold values from 0 to 63; in each aligned block of 1024 rows (0 to 1023, 1024 to 2047, ..., all dimensions but the last counted through in order) at most 32 rows name the same one
- list_index: int32 [4, 64, 1024], P('views', 'tiles'), may hold values from 0 to 2047
- list_length: int32 [4, 64], P('views', 'tiles'), may hold values from 1 to 1024, 32768 in all within a row
- targets: bfloat16 [4, 64, 3, 1024], P('views', 'tiles'), may hold values from 0 to 1
- background: float32 [3], replicated, may hold values from 0.1 to 0.9
Outputs:
- rendered: bfloat16 [4, 64, 3, 1024], P('views', 'tiles')
- new_gaussians: float32 [59, 131072], P(None, 'tiles')
- new_moment_one: float32 [59, 131072], P(None, 'tiles')
- new_moment_two: float32 [59, 131072], P(None, 'tiles')
Inputs may be any that keep to these rules, and one draw needn't show every extreme that they name: `list_owner`: in the list of one device (one camera slot, one tile) no owner is named by more than 32 entries, and some device's list reaches this bound. `cameras`: rotations are proper, and every Gaussian lies in front of every camera.
All inputs are finite; a program needn't handle non-finite values. No bound on the sum of `list_length` on one device may be relied on, other than what follows from the above.
Results may differ from a plain program's by a relative error of at most 0.001.
Values sent between devices are 32-bit elements; how exact they have to be, the bound alone decides.
No kernel may reach another device: no remote copies, remote signals or barrier semaphores. Data moves between devices by JAX's collectives and lax.ppermute only.
A program may use at most 192 MiB of HBM per device.

v0:
```python
from functools import partial

import jax
import jax.numpy as jnp
from jax import lax
from jax.sharding import PartitionSpec as P

TILE_SIDE = 32
PIXELS = 1024
TILE_ROWS = 8
LIST = 1024
BLOCK = 128


focal_length = 400.0
precise = lax.Precision.HIGHEST
decay_one = 0.9
decay_two = 0.999
adam_epsilon = 1e-08


def sh_basis(direction):
    dir_x, dir_y, dir_z = (direction[0], direction[1], direction[2])
    sq_x, sq_y, sq_z = (dir_x * dir_x, dir_y * dir_y, dir_z * dir_z)
    terms = [
        0.28209479177387814 * jnp.ones_like(dir_x),
        -0.4886025119029199 * dir_y,
        0.4886025119029199 * dir_z,
        -0.4886025119029199 * dir_x,
        1.0925484305920792 * dir_x * dir_y,
        -1.0925484305920792 * dir_y * dir_z,
        0.31539156525252005 * (2.0 * sq_z - sq_x - sq_y),
        -1.0925484305920792 * dir_x * dir_z,
        0.5462742152960396 * (sq_x - sq_y),
        -0.5900435899266435 * dir_y * (3.0 * sq_x - sq_y),
        2.890611442640554 * dir_x * dir_y * dir_z,
        -0.4570457994644658 * dir_y * (4.0 * sq_z - sq_x - sq_y),
        0.3731763325901154 * dir_z * (2.0 * sq_z - 3.0 * sq_x - 3.0 * sq_y),
        -0.4570457994644658 * dir_x * (4.0 * sq_z - sq_x - sq_y),
        1.445305721320277 * dir_z * (sq_x - sq_y),
        -0.5900435899266435 * dir_x * (sq_x - 3.0 * sq_y),
    ]
    return jnp.stack(terms)


def quat_rotation(quat):
    length = jnp.sqrt(jnp.sum(quat * quat, axis=0))
    quat_w, quat_x, quat_y, quat_z = (
        quat[0] / length,
        quat[1] / length,
        quat[2] / length,
        quat[3] / length,
    )
    rows = [
        [
            1.0 - 2.0 * (quat_y * quat_y + quat_z * quat_z),
            2.0 * (quat_x * quat_y - quat_w * quat_z),
            2.0 * (quat_x * quat_z + quat_w * quat_y),
        ],
        [
            2.0 * (quat_x * quat_y + quat_w * quat_z),
            1.0 - 2.0 * (quat_x * quat_x + quat_z * quat_z),
            2.0 * (quat_y * quat_z - quat_w * quat_x),
        ],
        [
            2.0 * (quat_x * quat_z - quat_w * quat_y),
            2.0 * (quat_y * quat_z + quat_w * quat_x),
            1.0 - 2.0 * (quat_x * quat_x + quat_y * quat_y),
        ],
    ]
    return jnp.stack([jnp.stack(entries) for entries in rows])


def project(params, camera, center_x, center_y):
    means = params[0:3]
    rotate = camera[0:9].reshape(3, 3)
    shift = camera[9:12]
    view_pos = jnp.dot(rotate, means, precision=precise) + shift[:, None]
    inv_depth = 1.0 / view_pos[2]
    image_x = focal_length * view_pos[0] * inv_depth + center_x
    image_y = focal_length * view_pos[1] * inv_depth + center_y
    scales = jnp.exp(params[3:6])
    local_axes = quat_rotation(params[6:10]) * scales[None, :, :]
    world_axes = jnp.einsum("ik,kjg->ijg", rotate, local_axes, precision=precise)
    proj_x = (
        focal_length * inv_depth * world_axes[0]
        - focal_length * view_pos[0] * inv_depth * inv_depth * world_axes[2]
    )
    proj_y = (
        focal_length * inv_depth * world_axes[1]
        - focal_length * view_pos[1] * inv_depth * inv_depth * world_axes[2]
    )
    cov_xx = jnp.sum(proj_x * proj_x, axis=0) + 0.3
    cov_xy = jnp.sum(proj_x * proj_y, axis=0)
    cov_yy = jnp.sum(proj_y * proj_y, axis=0) + 0.3
    determ = cov_xx * cov_yy - cov_xy * cov_xy
    opacity = 0.99 * jax.nn.sigmoid(params[10])
    center = -jnp.dot(rotate.T, shift, precision=precise)
    offset = means - center[:, None]
    direction = offset / jnp.sqrt(jnp.sum(offset * offset, axis=0))
    basis = sh_basis(direction)
    coeffs = params[11:59].reshape(16, 3, -1)
    colors = 0.5 + jnp.sum(basis[:, None, :] * coeffs, axis=0)
    head = jnp.stack(
        [image_x, image_y, cov_yy / determ, -cov_xy / determ, cov_xx / determ, opacity]
    )
    return jnp.concatenate([head, colors], axis=0)


def pixel_grid(tile, tile_cols):
    offsets = jnp.arange(PIXELS)
    pixel_x = (tile % tile_cols * TILE_SIDE + offsets % TILE_SIDE).astype(jnp.float32) + 0.5
    pixel_y = (tile // tile_cols * TILE_SIDE + offsets // TILE_SIDE).astype(jnp.float32) + 0.5
    return (pixel_x, pixel_y)


def block_terms(entry, count, pixel_x, pixel_y, index):
    start = index * BLOCK
    piece = lax.dynamic_slice_in_dim(entry, start, BLOCK, 1)
    live = (start + jnp.arange(BLOCK) < count)[None, :]
    delta_x = pixel_x[:, None] - piece[0][None, :]
    delta_y = pixel_y[:, None] - piece[1][None, :]
    power = -0.5 * (
        piece[2] * delta_x * delta_x
        + 2.0 * piece[3] * delta_x * delta_y
        + piece[4] * delta_y * delta_y
    )
    falloff = jnp.exp(power)
    alpha = jnp.where(live, piece[5][None, :] * falloff, 0.0)
    log_keep = jnp.log1p(-alpha)
    return (start, piece, live, delta_x, delta_y, falloff, alpha, log_keep)


def tile_pass(entry, count, pixel_x, pixel_y, target, background):
    blocks = (count + BLOCK - 1) // BLOCK

    def forward(index, carry):
        color, log_total = carry
        start, piece, live, delta_x, delta_y, falloff, alpha, log_keep = block_terms(
            entry, count, pixel_x, pixel_y, index
        )
        weight = jnp.exp(log_total[:, None] + jnp.cumsum(log_keep, axis=1) - log_keep) * alpha
        color = color + lax.dot_general(
            piece[6:9], weight, (((1,), (1,)), ((), ())), precision=precise
        )
        return (color, log_total + jnp.sum(log_keep, axis=1))

    zeros_pix = jnp.zeros((PIXELS,), jnp.float32)
    color, log_total = lax.fori_loop(
        0, blocks, forward, (jnp.zeros((3, PIXELS), jnp.float32), zeros_pix)
    )
    image = color + jnp.exp(log_total)[None, :] * background[:, None]
    resid = image - target
    dot_total = jnp.sum(image * resid, axis=0)

    def backward(index, carry):
        grads, log_before, prefix = carry
        start, piece, live, delta_x, delta_y, falloff, alpha, log_keep = block_terms(
            entry, count, pixel_x, pixel_y, index
        )
        trans = jnp.exp(log_before[:, None] + jnp.cumsum(log_keep, axis=1) - log_keep)
        weight = trans * alpha
        along = lax.dot_general(resid, piece[6:9], (((0,), (0,)), ((), ())), precision=precise)
        running = prefix[:, None] + jnp.cumsum(weight * along, axis=1)
        d_alpha = jnp.where(
            live, trans * along - (dot_total[:, None] - running) / (1.0 - alpha), 0.0
        )
        d_power = d_alpha * alpha
        sum_x = jnp.sum(d_power * delta_x, axis=0)
        sum_y = jnp.sum(d_power * delta_y, axis=0)
        head = jnp.stack(
            [
                piece[2] * sum_x + piece[3] * sum_y,
                piece[3] * sum_x + piece[4] * sum_y,
                -0.5 * jnp.sum(d_power * delta_x * delta_x, axis=0),
                -jnp.sum(d_power * delta_x * delta_y, axis=0),
                -0.5 * jnp.sum(d_power * delta_y * delta_y, axis=0),
                jnp.sum(d_alpha * falloff, axis=0),
            ]
        )
        color_grad = jnp.dot(resid, weight, precision=precise)
        block_grad = jnp.concatenate([head, color_grad], axis=0)
        grads = lax.dynamic_update_slice_in_dim(grads, block_grad, start, 1)
        return (grads, log_before + jnp.sum(log_keep, axis=1), running[:, -1])

    start_grads = jnp.zeros((9, LIST), jnp.float32)
    grads, ignored, unused = lax.fori_loop(0, blocks, backward, (start_grads, zeros_pix, zeros_pix))
    return (image, grads)


def adam_step(values, first, second, grad, rates):
    first_new = decay_one * first + (1.0 - decay_one) * grad
    second_new = decay_two * second + (1.0 - decay_two) * grad * grad
    return (
        values - rates[:, None] * first_new / (jnp.sqrt(second_new) + adam_epsilon),
        first_new,
        second_new,
    )


def body(
    gaussians,
    moment_one,
    moment_two,
    learn_rates,
    cameras,
    camera_ids,
    list_owner,
    list_index,
    list_length,
    targets,
    background,
):
    peers = lax.axis_size("tiles")
    tiles_here = list_index.shape[1]
    entries = tiles_here * LIST
    owned = gaussians.shape[1]
    capacity = 2 * entries // peers
    tile_cols = tiles_here * peers // TILE_ROWS
    center_x = 0.5 * TILE_SIDE * tile_cols
    center_y = 0.5 * TILE_SIDE * TILE_ROWS
    camera = cameras[camera_ids[0]]
    attrs, pullback = jax.vjp(
        partial(project, camera=camera, center_x=center_x, center_y=center_y), gaussians
    )
    owner_flat = list_owner.reshape(-1)
    index_flat = list_index.reshape(-1)
    order = jnp.argsort(owner_flat, stable=True)
    sorted_owner = owner_flat[order]
    one_hot = (sorted_owner[:, None] == jnp.arange(peers)[None, :]).astype(jnp.int32)
    counts = jnp.sum(one_hot, axis=0)
    starts = jnp.cumsum(counts) - counts
    rank = jnp.arange(entries) - jnp.sum(one_hot * starts[None, :], axis=1)
    slot = sorted_owner * capacity + rank
    position = jnp.zeros((entries,), jnp.int32).at[order].set(slot)
    asked_for = (
        jnp.zeros((peers * capacity,), jnp.int32)
        .at[slot]
        .set(index_flat[order])
        .reshape(peers, capacity)
    )
    asked = lax.all_to_all(asked_for, "tiles", split_axis=0, concat_axis=0, tiled=True)
    served = jnp.take(attrs, asked, axis=1)
    returned = lax.all_to_all(served, "tiles", split_axis=1, concat_axis=1, tiled=True)
    entry_attrs = returned.reshape(9, peers * capacity)[:, position].reshape(9, tiles_here, LIST)
    first_tile = lax.axis_index("tiles") * tiles_here

    def render(item):
        local_tile, entry, count, target = item
        pixel_x, pixel_y = pixel_grid(first_tile + local_tile, tile_cols)
        return tile_pass(entry, count, pixel_x, pixel_y, target.astype(jnp.float32), background)

    images, tile_grads = lax.map(
        render,
        (jnp.arange(tiles_here), jnp.moveaxis(entry_attrs, 1, 0), list_length[0], targets[0]),
    )
    flat_grads = jnp.moveaxis(tile_grads, 0, 1).reshape(9, entries)
    global_ids = owner_flat * owned + index_flat
    dense = jnp.zeros((9, peers * owned), jnp.float32).at[:, global_ids].add(flat_grads)
    attr_grad = lax.psum_scatter(dense, "tiles", scatter_dimension=1, tiled=True)
    param_grad = pullback(attr_grad)[0]
    total = lax.psum(param_grad, "views")
    new_values, first_new, second_new = adam_step(
        gaussians, moment_one, moment_two, total, learn_rates
    )
    return (images[None].astype(jnp.bfloat16), new_values, first_new, second_new)


def solution(mesh):
    return jax.shard_map(
        body,
        mesh=mesh,
        in_specs=(
            P(None, "tiles"),
            P(None, "tiles"),
            P(None, "tiles"),
            P(),
            P(),
            P("views"),
            P("views", "tiles", None, None),
            P("views", "tiles", None),
            P("views", "tiles"),
            P("views", "tiles", None, None),
            P(),
        ),
        out_specs=(
            P("views", "tiles", None, None),
            P(None, "tiles"),
            P(None, "tiles"),
            P(None, "tiles"),
        ),
        check_vma=False,
    )
```

profile of v0, /device:TPU:2, one launch (start us, length us, event | category | flops | bytes accessed | tf_op | source)
XLA Modules:
  0.0 474.9 jit_solution(15722905798426778904)
XLA Ops:
  7.2 5.1 %sort.17 = (s32[1024]{0:T(1024)}, s32[1024]{0:T(1024)S(1)}) sort(s32[1024]{0:T(1024)} %bitcast.355, s32[1024]{0:T(1024)S(1)} %iota.30), dimensions={0}, to_apply=%region_0.0 | sort | flops 10240 | bytes 16384 | tf_op jit(solution)/shard_map/jit(argsort)/sort | solution.py:228
  12.3 5.7 %gather_fusion = s32[1024]{0:T(1024)S(1)} fusion(s32[1024]{0:T(1024)} %bitcast.356, s32[1024]{0:T(1024)S(1)} %get-tuple-element.458), kind=kCustom, calls=%fused_computation | custom fusion | bytes 12288 | tf_op jit(solution)/shard_map/gather | solution.py:229
  18.0 5.7 %gather_fusion.1 = s32[1024]{0:T(1024)S(1)} fusion(s32[1024]{0:T(1024)} %bitcast.357, s32[1024]{0:T(1024)S(1)} %get-tuple-element.458), kind=kCustom, calls=%fused_computation.1 | custom fusion | bytes 12288 | tf_op jit(solution)/shard_map/gather | solution.py:239
  24.3 4.3 scatter_custom_fusion
  28.6 0.7 all_to_all.13
  29.3 12.0 %all-to-all-start = ((s32[64,1,32]{2,1,0:T(1,128)}), s32[64,1,32]{2,1,0:T(1,128)S(1)}, u32[]{:S(2)}, u32[]{:S(2)}) async-start(s32[64,1,32]{2,1,0:T(1,128)} %bitcast.7), calls=%async_computation | async-start | bytes 65536 | tf_op jit(solution)/shard_map/all_to_all | solution.py:242
  42.1 0.7 compare_select_fusion.2
  42.8 0.9 multiply_reduce_fusion.9
  43.8 1.1 slice.164
  45.0 0.2 fusion.67
  45.2 0.9 multiply_reduce_fusion.5
  46.2 1.0 convolution_add_fusion.2
  47.3 1.0 broadcast_divide_fusion
  48.3 1.7 broadcast_multiply_fusion.10
  50.1 1.0 subtract_multiply_fusion.21
  51.2 0.3 fusion.72
  51.7 0.2 reshape.735
  51.9 0.2 stack.28
  52.3 4.4 sort.18
  56.7 0.6 broadcast_clamp_fusion.1
  58.0 0.2 concatenate.6
  58.2 0.4 copy.61
  58.6 4.3 scatter_custom_fusion.1
  63.0 5.5 %gather_fusion.2 = f32[2048,9]{1,0:T(8,128)S(1)} fusion(f32[9,2048]{0,1:T(8,128)S(1)} %copy.61, s32[2048]{0:T(1024)S(1)} %broadcast_clamp_fusion), kind=kCustom, calls=%fused_computation.2 | custom fusion | bytes 155648 | tf_op jit(solution)/shard_map/jit(_take)/gather | solution.py:243
  68.5 0.5 copy.62
  69.0 0.9 reshape.822
  69.9 10.3 %all-to-all-start.1 = ((f32[64,1,288]{2,1,0:T(1,128)}), f32[64,1,288]{2,1,0:T(1,128)S(1)}, u32[]{:S(2)}, u32[]{:S(2)}) async-start(f32[64,1,288]{2,1,0:T(1,128)} %reshape.822), calls=%async_computation.1 | async-start | bytes 196608 | tf_op jit(solution)/shard_map/all_to_all | solution.py:244
  80.3 9.3 %all-to-all-done.1 = f32[64,1,288]{2,1,0:T(1,128)S(1)} async-done(((f32[64,1,288]{2,1,0:T(1,128)}), f32[64,1,288]{2,1,0:T(1,128)S(1)}, u32[]{:S(2)}, u32[]{:S(2)}) %all-to-all-start.1) | async-done | bytes 73760 | tf_op jit(solution)/shard_map/all_to_all | solution.py:244
  89.6 0.5 broadcast.1146
  90.1 0.9 reduce.7
  91.1 0.5 copy.63
  91.6 2.8 gather_fusion.3
  94.4 0.2 copy.64
  94.6 3.2 while.40
  95.1 0.7 add_compare_fusion.4
  95.8 0.5 fusion.207
  96.4 0.5 reduce_window_sum.36
  96.9 1.0 convolution_add_fusion.4
  97.9 1.4 multiply_reduce_fusion.10
  99.3 8.3 %while.41 = (s32[]{:T(128)}, f32[9,1024]{1,0:T(8,128)S(1)}, f32[1024]{0:T(1024)S(1)}, f32[1024]{0:T(1024)S(1)}, s32[]{:T(128)}, /*index=5*/f32[9,1024]{1,0:T(8,1...) while((s32[]{:T(128)}, f32[9,1024]{1,0:T(8,128)S(1)}, ...), condition=%wide.region_27.28_spmd.clone, body=%wide.region_17.27_spmd.clone.sunk | while | flops 55855884 | bytes 9094147 | solution.py:187
  99.3 0.7 add_compare_fusion.5
  100.1 0.5 negate_log-plus-one_fusion.4
  100.6 0.5 reduce_window_sum.37
  101.1 1.8 convolution_bitcast_fusion.4
  102.9 2.0 fusion.212
  104.8 0.5 reduce_window_sum.38
  105.3 0.9 fusion.213
  106.2 0.9 fusion.214
  107.6 0.2 copy.66
  107.9 42.6 %scatter_custom_fusion.2 = f32[9,131072]{0,1:T(8,128)} fusion(s32[1024]{0:T(1024)} %get-tuple-element.261, f32[]{:T(128)} %constant.125.clone.1, f32[1024,9]{1,0:T(8,128)S(1)} %copy.66, s32[1024]{0:T(1024)} %broadcast_clamp_fusion.1), kind=kCustom, calls=%fused_computation.125 | custom fusion | flops 9216 | bytes 4719104 | tf_op jit(solution)/shard_map/scatter-add | solution.py:259
  150.5 36.9 %copy.67 = f32[9,131072]{1,0:T(8,128)} copy(f32[9,131072]{0,1:T(8,128)} %scatter_custom_fusion.2) | data formatting | bytes 9437184 | tf_op jit(solution)/shard_map/scatter-add | solution.py:259
  187.5 223.7 %reduce-scatter.2.cloned.1.call-done = f32[9,2048]{1,0:T(8,128)} async-done(((f32[9,131072]{1,0:T(8,128)}), f32[9,2048]{1,0:T(8,128)}) %reduce-scatter.2.cloned.1.call-update) | async-done | bytes 73744 | tf_op jit(solution)/shard_map/reduce_scatter | solution.py:260
  411.2 0.9 split.5
  412.2 0.4 broadcast_multiply_fusion
  412.6 0.2 add_add_fusion.5
  412.8 0.2 add_add_fusion.4
  413.1 1.0 fusion.183
  414.3 0.4 fusion.74
  415.4 0.2 mul.1735
  415.8 1.1 multiply_multiply_fusion.2
  416.9 0.3 convolution_add_fusion.1
  417.2 0.9 pad_add_fusion
  418.1 47.4 %all-reduce.23.cloned.1.call-done = f32[59,2048]{1,0:T(8,128)} async-done(((f32[59,2048]{1,0:T(8,128)}), f32[59,2048]{1,0:T(8,128)}) %all-reduce.23.cloned.1.call-update) | async-done | bytes 483344 | tf_op jit(solution)/shard_map/psum | solution.py:262
  465.5 2.4 divide_subtract_fusion
  (101 shorter events, 3.6 us)
Async XLA Ops:
  7.2 34.8 %copy-start = (f32[16,12]{1,0:T(8,128)S(1)}, f32[16,12]{1,0:T(8,128)}, u32[]{:S(2)}) copy-start(f32[16,12]{1,0:T(8,128)} %param.19) | copy-start | bytes 2308
  29.3 33.6 %all-to-all-start = ((s32[64,1,32]{2,1,0:T(1,128)}), s32[64,1,32]{2,1,0:T(1,128)S(1)}, u32[]{:S(2)}, u32[]{:S(2)}) async-start(s32[64,1,32]{2,1,0:T(1,128)} %bitcast.7), calls=%async_computation | async-start | bytes 65536 | tf_op jit(solution)/shard_map/all_to_all | solution.py:242
  45.2 3.1 copy-start.6
  69.9 19.7 %all-to-all-start.1 = ((f32[64,1,288]{2,1,0:T(1,128)}), f32[64,1,288]{2,1,0:T(1,128)S(1)}, u32[]{:S(2)}, u32[]{:S(2)}) async-start(f32[64,1,288]{2,1,0:T(1,128)} %reshape.822), calls=%async_computation.1 | async-start | bytes 196608 | tf_op jit(solution)/shard_map/all_to_all | solution.py:244
  80.2 331.0 %reduce-scatter.2.cloned.1.call-start = ((), (), s32[]{:S(2)}) async-start(), calls=%async_computation.3 | async-start | bytes 8519680 | tf_op jit(solution)/shard_map/reduce_scatter | solution.py:260
  107.8 307.8 %copy-start.1 = (f32[59,2048]{1,0:T(8,128)S(1)}, f32[59,2048]{1,0:T(8,128)}, u32[]{:S(2)}) copy-start(f32[59,2048]{1,0:T(8,128)} %param.15) | copy-start | bytes 1449988
  107.8 307.8 %copy-start.7 = (f32[3]{0:T(128)S(1)}, f32[3]{0:T(128)}, u32[]{:S(2)}) copy-start(f32[3]{0:T(128)} %copy-done.6) | copy-start | bytes 40
  107.8 307.9 %copy-start.4 = (f32[1,2048]{1,0:T(1,128)S(1)}, f32[1,2048]{1,0:T(1,128)}, u32[]{:S(2)}) copy-start(f32[1,2048]{1,0:T(1,128)} %get-tuple-element.381) | copy-start | bytes 24580
  107.8 307.9 %copy-start.5 = (f32[1,2048]{1,0:T(1,128)S(1)}, f32[1,2048]{1,0:T(1,128)}, u32[]{:S(2)}) copy-start(f32[1,2048]{1,0:T(1,128)} %get-tuple-element.382) | copy-start | bytes 24580
  107.8 357.6 %copy-start.2 = (f32[59,2048]{1,0:T(8,128)S(1)}, f32[59,2048]{1,0:T(8,128)}, u32[]{:S(2)}) copy-start(f32[59,2048]{1,0:T(8,128)} %param.16) | copy-start | bytes 1449988
  107.9 357.6 %copy-start.3 = (f32[59,2048]{1,0:T(8,128)S(1)}, f32[59,2048]{1,0:T(8,128)}, u32[]{:S(2)}) copy-start(f32[59,2048]{1,0:T(8,128)} %param.17) | copy-start | bytes 1449988
  107.9 357.6 %copy-start.8 = (f32[59]{0:T(128)S(1)}, f32[59]{0:T(128)}, u32[]{:S(2)}) copy-start(f32[59]{0:T(128)} %param.18) | copy-start | bytes 712
  187.5 278.0 %all-reduce.23.cloned.1.call-start = ((), (), s32[]{:S(2)}) async-start(), calls=%async_computation.4 | async-start | bytes 1048576 | tf_op jit(solution)/shard_map/psum | solution.py:262
Sparse Core Ops, SparseCore 0:
  187.6 223.5 reduce-scatter.1
  418.2 47.2 all-reduce.22
where the time goes:
time: 485 us; the launch traced here: 475 us
  waiting for transfers between devices  280 us (58%)
  other arithmetic  74.5 us (15%)
  local copies, waits for them, and re-layouts  73.6 us (15%)
  starting transfers between devices  22.4 us (5%)
  between operations  16.3 us (3%)
  matrix products  6.91 us (1%)
    reduce_scatter x1, waiting for transfers between devices, body(): lax.psum_scatter(dense, 'tiles', scatter_dimension=1, tiled=True)  224 us
    scatter-add x3, other arithmetic, body(): jnp.zeros((9, peers * owned), jnp.float32).at[:, global_ids].add(flat_grads)  47.6 us
    psum x1, waiting for transfers between devices, body(): total = lax.psum(param_grad, 'views')  47.4 us
    scatter-add x2, local copies, waits for them, and re-layouts, body(): jnp.zeros((9, peers * owned), jnp.float32).at[:, global_ids].add(flat_grads)  36.9 us
    all_to_all x1, starting transfers between devices, body(): lax.all_to_all(asked_for, 'tiles', split_axis=0, concat_axis=0, tiled=True)  12 us
    all_to_all x1, starting transfers between devices, body(): lax.all_to_all(served, 'tiles', split_axis=1, concat_axis=1, tiled=True)  10.3 us
  transfers between devices with their start and end apart: 4, of which 3 were waited for; matrix products, arithmetic and copies ran while one was open for 4% of the time, Pallas kernels for 0%

commit v1 on v0

--- a/solution.py
+++ b/solution.py
@@ -219,30 +219,24 @@
     tile_cols = tiles_here * peers // TILE_ROWS
     center_x = 0.5 * TILE_SIDE * tile_cols
     center_y = 0.5 * TILE_SIDE * TILE_ROWS
-    camera = cameras[camera_ids[0]]
-    attrs, pullback = jax.vjp(
-        partial(project, camera=camera, center_x=center_x, center_y=center_y), gaussians
-    )
+    view_cameras = cameras[camera_ids]
+    camera = view_cameras[lax.axis_index("views")]
+    attrs = project(gaussians, camera, center_x, center_y)
     owner_flat = list_owner.reshape(-1)
     index_flat = list_index.reshape(-1)
-    order = jnp.argsort(owner_flat, stable=True)
-    sorted_owner = owner_flat[order]
-    one_hot = (sorted_owner[:, None] == jnp.arange(peers)[None, :]).astype(jnp.int32)
-    counts = jnp.sum(one_hot, axis=0)
-    starts = jnp.cumsum(counts) - counts
-    rank = jnp.arange(entries) - jnp.sum(one_hot * starts[None, :], axis=1)
-    slot = sorted_owner * capacity + rank
-    position = jnp.zeros((entries,), jnp.int32).at[order].set(slot)
+    one_hot = (owner_flat[:, None] == jnp.arange(peers)[None, :]).astype(jnp.int32)
+    rank = jnp.sum((jnp.cumsum(one_hot, axis=0) - 1) * one_hot, axis=1)
+    slot = owner_flat * capacity + rank
     asked_for = (
         jnp.zeros((peers * capacity,), jnp.int32)
         .at[slot]
-        .set(index_flat[order])
+        .set(index_flat, unique_indices=True)
         .reshape(peers, capacity)
     )
     asked = lax.all_to_all(asked_for, "tiles", split_axis=0, concat_axis=0, tiled=True)
     served = jnp.take(attrs, asked, axis=1)
     returned = lax.all_to_all(served, "tiles", split_axis=1, concat_axis=1, tiled=True)
-    entry_attrs = returned.reshape(9, peers * capacity)[:, position].reshape(9, tiles_here, LIST)
+    entry_attrs = returned.reshape(9, peers * capacity)[:, slot].reshape(9, tiles_here, LIST)
     first_tile = lax.axis_index("tiles") * tiles_here
 
     def render(item):
@@ -255,11 +249,28 @@
         (jnp.arange(tiles_here), jnp.moveaxis(entry_attrs, 1, 0), list_length[0], targets[0]),
     )
     flat_grads = jnp.moveaxis(tile_grads, 0, 1).reshape(9, entries)
-    global_ids = owner_flat * owned + index_flat
-    dense = jnp.zeros((9, peers * owned), jnp.float32).at[:, global_ids].add(flat_grads)
-    attr_grad = lax.psum_scatter(dense, "tiles", scatter_dimension=1, tiled=True)
-    param_grad = pullback(attr_grad)[0]
-    total = lax.psum(param_grad, "views")
+    grad_send = (
+        jnp.zeros((9, peers * capacity), jnp.float32)
+        .at[:, slot]
+        .set(flat_grads, unique_indices=True)
+        .reshape(9, peers, capacity)
+    )
+    grad_back = lax.all_to_all(grad_send, "tiles", split_axis=1, concat_axis=1, tiled=True)
+    attr_grad = (
+        jnp.zeros((9, owned), jnp.float32)
+        .at[:, asked.reshape(-1)]
+        .add(grad_back.reshape(9, peers * capacity))
+    )
+    view_grads = lax.all_gather(attr_grad, "views", axis=0, tiled=False)
+
+    def pull(view_camera, grad):
+        ignored, pullback = jax.vjp(
+            partial(project, camera=view_camera, center_x=center_x, center_y=center_y),
+            gaussians,
+        )
+        return pullback(grad)[0]
+
+    total = jnp.sum(jax.vmap(pull)(view_cameras, view_grads), axis=0)
     new_values, first_new, second_new = adam_step(
         gaussians, moment_one, moment_two, total, learn_rates
     )
@@ -276,7 +287,7 @@
             P(None, "tiles"),
             P(),
             P(),
-            P("views"),
+            P(),
             P("views", "tiles", None, None),
             P("views", "tiles", None),
             P("views", "tiles"),

time: 485 us -> 259 us (0.53); the launches traced: 475 us -> 256 us
  waiting for transfers between devices: 280 us -> 16.8 us
  starting transfers between devices: 22.4 us -> 67.8 us
  local copies, waits for them, and re-layouts: 73.6 us -> 33.8 us
  blocking collectives: 0 us -> 22.7 us
  matrix products: 6.91 us -> 27.1 us
  between operations: 16.3 us -> 3.32 us
  other arithmetic: 74.5 us -> 83.8 us
    reduce_scatter x1 -> x0, waiting for transfers between devices: 224 us -> none  [body(): lax.psum_scatter(dense, 'tiles', scatter_dimension=1, tiled=True)]
    psum x1 -> x0, waiting for transfers between devices: 47.4 us -> none  [body(): total = lax.psum(param_grad, 'views')]
    all_to_all x0 -> x1, starting transfers between devices: none -> 45.5 us  [body(): lax.all_to_all(grad_send, 'tiles', split_axis=1, concat_axis=1, tiled=True)]
    scatter-add x2 -> x0, local copies, waits for them, and re-layouts: 36.9 us -> none  [body(): jnp.zeros((9, peers * owned), jnp.float32).at[:, global_ids].add(flat_grads)]
    scatter-add x3 -> x1, other arithmetic: 47.6 us -> 11.7 us  [body(): attr_grad = jnp.zeros((9, owned), jnp.float32).at[:, asked.reshape(-1)].a...]
    another operation x2 -> x3, other arithmetic: 0.2 us -> 18.1 us
    all_gather x0 -> x1, blocking collectives: none -> 13.6 us  [body(): view_grads = lax.all_gather(attr_grad, 'views', axis=0, tiled=False)]
    gather x3 -> x2, local copies, waits for them, and re-layouts: 14.2 us -> 3.38 us  [the longest x1 2.82 us: body(): returned.reshape(9, peers * capacity)[:, slot].reshape(9, tiles_here, LIST)]
  transfers between devices with their start and end apart: 4 -> 3, of which waited for: 3 -> 2; matrix products, arithmetic and copies ran while one was open for 4% -> 5% of each run, Pallas kernels for 0% -> 0%
where the time goes in v1:
time: 259 us; the launch traced here: 256 us
  other arithmetic  83.8 us (32%)
  starting transfers between devices  67.8 us (26%)
  local copies, waits for them, and re-layouts  33.8 us (13%)
  matrix products  27.1 us (10%)
  blocking collectives  22.7 us (9%)
  waiting for transfers between devices  16.8 us (6%)
  between operations  3.32 us (1%)
    all_to_all x1, starting transfers between devices, body(): lax.all_to_all(grad_send, 'tiles', split_axis=1, concat_axis=1, tiled=True)  45.5 us
    another operation x2, other arithmetic  18 us
    all_gather x1, blocking collectives, body(): view_grads = lax.all_gather(attr_grad, 'views', axis=0, tiled=False)  13.6 us
    all_to_all x1, starting transfers between devices, body(): lax.all_to_all(asked_for, 'tiles', split_axis=0, concat_axis=0, tiled=True)  12 us
    scatter-add x1, other arithmetic, body(): attr_grad = jnp.zeros((9, owned), jnp.float32).at[:, asked.reshape(-1)].a...  11.7 us
    all_to_all x1, starting transfers between devices, body(): lax.all_to_all(served, 'tiles', split_axis=1, concat_axis=1, tiled=True)  10.3 us
    dot_general x5, matrix products, backward(): lax.dot_general(resid, piece[6:9], (((0,), (0,)), ((), ())), precision=pr...  9.81 us
    all_to_all x1, waiting for transfers between devices, body(): lax.all_to_all(grad_send, 'tiles', split_axis=1, concat_axis=1, tiled=True)  9.37 us
  transfers between devices with their start and end apart: 3, of which 2 were waited for; matrix products, arithmetic and copies ran while one was open for 5% of the time, Pallas kernels for 0%

profile of v1, /device:TPU:2, one launch (start us, length us, event | category | flops | bytes accessed | tf_op | source)
XLA Modules:
  0.0 256.2 jit_solution(4353798787864917889)
XLA Ops:
  1.4 0.7 fusion.74
  2.1 18.0 %reduce-window.6 = s32[64,8,128]{2,1,0:T(8,128)S(1)} reduce-window(s32[64,8,128]{2,1,0:T(8,128)S(1)} %fusion.74, s32[]{:T(128)} %constant.104.clone.1), window={size=1x1x128 pad=0_0x0_0x127_0}, to_apply=%region_0.0 | reduce-window | flops 8323072 | bytes 524292 | tf_op jit(solution)/shard_map/reduce-window
  20.8 4.5 %scatter_custom_fusion = s32[2048]{0:T(1024)S(1)} fusion(s32[1024]{0:T(1024)S(1)} %bitcast.562, s32[1024]{0:T(1024)} %bitcast.567, s32[]{:T(128)} %constant.104.clone.1), kind=kCustom, calls=%fused_computation.467 | custom fusion | bytes 8704 | tf_op jit(solution)/shard_map/scatter | solution.py:233
  25.3 0.7 all_to_all.16
  26.5 0.8 dynamic-update-slice
  27.3 12.0 %all-to-all-start = ((s32[64,1,32]{2,1,0:T(1,128)}), s32[64,1,32]{2,1,0:T(1,128)S(1)}, u32[]{:S(2)}, u32[]{:S(2)}) async-start(s32[64,1,32]{2,1,0:T(1,128)} %bitcast.9), calls=%async_computation | async-start | bytes 65536 | tf_op jit(solution)/shard_map/all_to_all | solution.py:236
  39.3 9.1 %all-reduce.21 = s32[4]{0:T(128)S(1)} all-reduce(s32[4]{0:T(128)S(1)} %dynamic-update-slice), channel_id=23, replica_groups=mesh['tiles'=64,'views'=4] {'views'}, use_global_device_ids=true, to_apply=%add.21 | all-reduce | flops 4 | bytes 32
  51.8 0.7 slice_multiply_fusion.15
  56.6 1.4 multiply_reduce_fusion.6
  59.5 5.5 %gather_fusion.1 = f32[2048,9]{1,0:T(8,128)S(1)} fusion(f32[9,2048]{0,1:T(8,128)S(1)} %copy.311, s32[2048]{0:T(1024)S(1)} %broadcast_clamp_fusion), kind=kCustom, calls=%fused_computation.1 | custom fusion | bytes 155648 | tf_op jit(solution)/shard_map/jit(_take)/gather | solution.py:237
  65.6 0.9 reshape.654
  66.5 10.3 %all-to-all-start.1 = ((f32[64,1,288]{2,1,0:T(1,128)}), f32[64,1,288]{2,1,0:T(1,128)S(1)}, u32[]{:S(2)}, u32[]{:S(2)}) async-start(f32[64,1,288]{2,1,0:T(1,128)} %reshape.654), calls=%async_computation.1 | async-start | bytes 196608 | tf_op jit(solution)/shard_map/all_to_all | solution.py:238
  77.3 0.7 reduce.9
  78.0 0.7 reshape.555
  78.7 7.5 %all-to-all-done.1 = f32[64,1,288]{2,1,0:T(1,128)S(1)} async-done(((f32[64,1,288]{2,1,0:T(1,128)}), f32[64,1,288]{2,1,0:T(1,128)S(1)}, u32[]{:S(2)}, u32[]{:S(2)}) %all-to-all-start.1) | async-done | bytes 73760 | tf_op jit(solution)/shard_map/all_to_all | solution.py:238
  86.7 0.9 reduce.10
  88.2 2.8 %gather_fusion.2 = f32[1024,9]{1,0:T(8,128)S(1)} fusion(f32[9,2048]{0,1:T(8,128)S(1)} %bitcast.515, s32[1024]{0:T(1024)S(1)} %copy-done.40), kind=kCustom, calls=%fused_computation.2 | custom fusion | bytes 77824 | tf_op jit(solution)/shard_map/gather | solution.py:239
  91.3 13.9 %while.40 = (s32[]{:T(128)}, f32[3,1024]{1,0:T(4,128)S(1)}, f32[1024]{0:T(1024)S(1)}, s32[]{:T(128)}, f32[9,1024]{1,0:T(8,128)S(1)}, /*index=5*/s32[]{:T(128)}, ...) while((s32[]{:T(128)}, f32[3,1024]{1,0:T(4,128)S(1)}, ...), condition=%wide.region_13.14_spmd.clone, body=%wide.region_10.13_spmd.clone.sunk | while | flops 25580940 | bytes 2186335 | solution.py:149
  91.4 0.7 add_compare_fusion.4
  93.1 1.0 convolution_add_fusion.4
  94.2 0.7 add_compare_fusion.4
  95.8 1.0 convolution_add_fusion.4
  98.6 1.0 convolution_add_fusion.4
  101.4 1.0 convolution_add_fusion.4
  104.1 1.0 convolution_add_fusion.4
  105.2 0.7 multiply_reduce_fusion.12
  106.5 53.5 %while.41 = (s32[]{:T(128)}, f32[9,1024]{1,0:T(8,128)}, f32[1024]{0:T(1024)S(1)}, f32[1024]{0:T(1024)S(1)}, s32[]{:T(128)}, /*index=5*/f32[9,1024]{1,0:T(8,128)S...) while((s32[]{:T(128)}, f32[9,1024]{1,0:T(8,128)}, ...), condition=%wide.region_26.27_spmd.clone, body=%wide.region_16.26_spmd.clone.sunk | while | flops 55855884 | bytes 9388155 | solution.py:187
  108.7 2.0 fusion.229
  111.2 0.9 fusion.230
  112.1 1.5 fusion.231
  113.7 0.9 fusion.232
  114.6 1.8 convolution_bitcast_fusion.4
  119.4 2.0 fusion.229
  121.9 0.9 fusion.230
  122.8 1.5 fusion.231
  124.4 0.9 fusion.232
  125.3 1.8 convolution_bitcast_fusion.4
  130.2 2.0 fusion.229
  132.6 0.9 fusion.230
  133.6 1.5 fusion.231
  135.1 0.8 fusion.232
  136.0 1.8 convolution_bitcast_fusion.4
  140.9 2.0 fusion.229
  143.3 0.9 fusion.230
  144.3 1.5 fusion.231
  145.8 0.8 fusion.232
  146.7 1.8 convolution_bitcast_fusion.4
  151.6 2.0 fusion.229
  154.0 0.9 fusion.230
  155.0 1.5 fusion.231
  156.5 0.8 fusion.232
  157.4 1.8 convolution_bitcast_fusion.4
  160.0 1.1 copy.316
  161.0 3.5 %scatter_custom_fusion.1 = f32[9,2048]{0,1:T(8,128)S(1)} fusion(s32[1024]{0:T(1024)} %bitcast.564, f32[1024,9]{1,0:T(8,128)S(1)} %copy.316, f32[]{:T(128)} %constant.105.clone.1), kind=kCustom, calls=%fused_computation.137 | custom fusion | bytes 74240 | tf_op jit(solution)/shard_map/scatter | solution.py:255
  165.0 0.9 reshape.656
  165.9 45.5 %all-to-all-start.2 = ((f32[64,1,288]{2,1,0:T(1,128)}), f32[64,1,288]{2,1,0:T(1,128)S(1)}, u32[]{:S(2)}, u32[]{:S(2)}) async-start(f32[64,1,288]{2,1,0:T(1,128)} %reshape.656), calls=%async_computation.2 | async-start | bytes 196608 | tf_op jit(solution)/shard_map/all_to_all | solution.py:258
  211.4 9.4 %all-to-all-done.2 = f32[64,1,288]{2,1,0:T(1,128)S(1)} async-done(((f32[64,1,288]{2,1,0:T(1,128)}), f32[64,1,288]{2,1,0:T(1,128)S(1)}, u32[]{:S(2)}, u32[]{:S(2)}) %all-to-all-start.2) | async-done | bytes 73760 | tf_op jit(solution)/shard_map/all_to_all | solution.py:258
  220.7 0.9 reduce.11
  222.4 11.7 %scatter_custom_fusion.2 = f32[9,2048]{0,1:T(8,128)S(1)} fusion(s32[2048]{0:T(1024)S(1)} %bitcast.565, f32[2048,9]{1,0:T(8,128)S(1)} %copy.319, f32[]{:T(128)} %constant.105.clone.1), kind=kCustom, calls=%fused_computation.135 | custom fusion | flops 18432 | bytes 73732 | tf_op jit(solution)/shard_map/scatter-add | solution.py:262
  234.5 13.6 %all-gather.2 = f32[4,9,2048]{2,1,0:T(8,128)S(1)} all-gather(f32[1,9,2048]{2,1,0:T(8,128)S(1)} %copy.320), channel_id=24, replica_groups=mesh['tiles'=64,'views'=4] {'views'}, dimensions={0}, use_global_device_ids=true | all-gather | bytes 368640 | tf_op jit(solution)/shard_map/all_gather | solution.py:264
  248.3 0.7 broadcast_multiply_fusion
  250.1 1.4 broadcast_multiply_fusion.1
  253.8 0.9 add_reduce_fusion
  254.8 1.4 divide_subtract_fusion
  (353 shorter events, 42.1 us)
Async XLA Ops:
  0.6 48.4 %copy-start = (f32[16,12]{1,0:T(8,128)S(1)}, f32[16,12]{1,0:T(8,128)}, u32[]{:S(2)}) copy-start(f32[16,12]{1,0:T(8,128)} %param.19) | copy-start | bytes 2308
  0.6 25.3 %copy-start.45 = (u32[256]{0:T(256)S(1)}, u32[256]{0:T(256)}, u32[]{:S(2)}) copy-start(u32[256]{0:T(256)} %constant.298) | copy-start | bytes 3076
  0.7 20.0 %copy-start.31 = (s32[1,1,1024,1]{2,3,1,0:T(1,128)S(1)}, s32[1,1,1024,1]{2,3,1,0:T(1,128)}, u32[]{:S(2)}) copy-start(s32[1,1,1024,1]{2,3,1,0:T(1,128)} %param.21) | copy-start | bytes 12292
  0.7 49.0 %copy-start.1 = (f32[59,2048]{1,0:T(8,128)S(1)}, f32[59,2048]{1,0:T(8,128)}, u32[]{:S(2)}) copy-start(f32[59,2048]{1,0:T(8,128)} %param.15) | copy-start | bytes 1449988
  20.8 32.5 %copy-start.41 = (s32[1024,1]{0,1:T(1,128)}, s32[1024,1]{0,1:T(1,128)S(1)}, u32[]{:S(2)}) copy-start(s32[1024,1]{0,1:T(1,128)S(1)} %compare_select_fusion.3) | copy-start | bytes 12292
  27.3 32.2 %all-to-all-start = ((s32[64,1,32]{2,1,0:T(1,128)}), s32[64,1,32]{2,1,0:T(1,128)S(1)}, u32[]{:S(2)}, u32[]{:S(2)}) async-start(s32[64,1,32]{2,1,0:T(1,128)} %bitcast.9), calls=%async_computation | async-start | bytes 65536 | tf_op jit(solution)/shard_map/all_to_all | solution.py:236
  52.5 5.5 %copy-start.19 = (f32[1,2048]{1,0:T(1,128)}, f32[1,2048]{1,0:T(1,128)S(1)}, u32[]{:S(2)}) copy-start(f32[1,2048]{1,0:T(1,128)S(1)} %get-tuple-element.448) | copy-start | bytes 24580
  52.5 5.5 %copy-start.21 = (f32[1,2048]{1,0:T(1,128)}, f32[1,2048]{1,0:T(1,128)S(1)}, u32[]{:S(2)}) copy-start(f32[1,2048]{1,0:T(1,128)S(1)} %get-tuple-element.449) | copy-start | bytes 24580
  52.5 24.2 %copy-start.23 = (f32[1,2048]{1,0:T(1,128)}, f32[1,2048]{1,0:T(1,128)S(1)}, u32[]{:S(2)}) copy-start(f32[1,2048]{1,0:T(1,128)S(1)} %get-tuple-element.450) | copy-start | bytes 24580
  55.0 3.7 %copy-start.12 = (f32[4,2048]{1,0:T(4,128)}, f32[4,2048]{1,0:T(4,128)S(1)}, u32[]{:S(2)}) copy-start(f32[4,2048]{1,0:T(4,128)S(1)} %get-tuple-element.496) | copy-start | bytes 98308
  55.3 2.7 %copy-start.28 = (f32[4,3]{0,1:T(4,128)}, f32[4,3]{0,1:T(4,128)S(1)}, u32[]{:S(2)}) copy-start(f32[4,3]{0,1:T(4,128)S(1)} %bitcast_negate_fusion) | copy-start | bytes 148
  56.0 2.7 %copy-start.10 = (f32[4,2048]{1,0:T(4,128)}, f32[4,2048]{1,0:T(4,128)S(1)}, u32[]{:S(2)}) copy-start(f32[4,2048]{1,0:T(4,128)S(1)} %get-tuple-element.503) | copy-start | bytes 98308
  56.6 2.2 copy-start.3
  65.6 22.6 %copy-start.40 = (s32[1024]{0:T(1024)S(1)}, s32[1024]{0:T(1024)}, u32[]{:S(2)}) copy-start(s32[1024]{0:T(1024)} %get-tuple-element.544) | copy-start | bytes 12292
  66.5 19.7 %all-to-all-start.1 = ((f32[64,1,288]{2,1,0:T(1,128)}), f32[64,1,288]{2,1,0:T(1,128)S(1)}, u32[]{:S(2)}, u32[]{:S(2)}) async-start(f32[64,1,288]{2,1,0:T(1,128)} %reshape.654), calls=%async_computation.1 | async-start | bytes 196608 | tf_op jit(solution)/shard_map/all_to_all | solution.py:238
  91.2 13.9 %copy-start.42 = (bf16[1,1,3,1024]{3,2,1,0:T(4,128)(2,1)S(1)}, bf16[1,1,3,1024]{3,2,1,0:T(4,128)(2,1)}, u32[]{:S(2)}) copy-start(bf16[1,1,3,1024]{3,2,1,0:T(4,128)(2,1)} %param.24) | copy-start | bytes 18436
  91.2 13.9 %copy-start.43 = (f32[3]{0:T(128)S(1)}, f32[3]{0:T(128)}, u32[]{:S(2)}) copy-start(f32[3]{0:T(128)} %param.25) | copy-start | bytes 40
  106.5 4.2 %copy-start.17 = (f32[9,1024]{1,0:T(8,128)}, f32[9,1024]{1,0:T(8,128)S(1)}, u32[]{:S(2)}) copy-start(f32[9,1024]{1,0:T(8,128)S(1)} %get-tuple-element.840) | copy-start | bytes 110596 | tf_op jit(solution)/shard_map/while/body/eval_jaxpr/while
  107.7 4.4 %copy-start.27 = (pred[128]{0:T(512)(128)(4,1)}, pred[128]{0:T(512)(128)(4,1)S(1)}, u32[]{:S(2)}) copy-start(pred[128]{0:T(512)(128)(4,1)S(1)} %add_compare_fusion.5) | copy-start | bytes 388 | tf_op jit(solution)/shard_map/while/body/eval_jaxpr/while
  111.2 2.5 copy-start.30
  113.7 3.5 %copy-start.18 = (f32[9,1024]{1,0:T(8,128)S(1)}, f32[9,1024]{1,0:T(8,128)}, u32[]{:S(2)}) copy-start(f32[9,1024]{1,0:T(8,128)} %copy-done.17) | copy-start | bytes 110596 | tf_op jit(solution)/shard_map/while/body/eval_jaxpr/while
  117.2 4.3 %copy-start.17 = (f32[9,1024]{1,0:T(8,128)}, f32[9,1024]{1,0:T(8,128)S(1)}, u32[]{:S(2)}) copy-start(f32[9,1024]{1,0:T(8,128)S(1)} %get-tuple-element.840) | copy-start | bytes 110596 | tf_op jit(solution)/shard_map/while/body/eval_jaxpr/while
  118.4 4.4 %copy-start.27 = (pred[128]{0:T(512)(128)(4,1)}, pred[128]{0:T(512)(128)(4,1)S(1)}, u32[]{:S(2)}) copy-start(pred[128]{0:T(512)(128)(4,1)S(1)} %add_compare_fusion.5) | copy-start | bytes 388 | tf_op jit(solution)/shard_map/while/body/eval_jaxpr/while
  121.9 2.5 copy-start.30
  124.4 3.5 %copy-start.18 = (f32[9,1024]{1,0:T(8,128)S(1)}, f32[9,1024]{1,0:T(8,128)}, u32[]{:S(2)}) copy-start(f32[9,1024]{1,0:T(8,128)} %copy-done.17) | copy-start | bytes 110596 | tf_op jit(solution)/shard_map/while/body/eval_jaxpr/while
  127.9 4.3 %copy-start.17 = (f32[9,1024]{1,0:T(8,128)}, f32[9,1024]{1,0:T(8,128)S(1)}, u32[]{:S(2)}) copy-start(f32[9,1024]{1,0:T(8,128)S(1)} %get-tuple-element.840) | copy-start | bytes 110596 | tf_op jit(solution)/shard_map/while/body/eval_jaxpr/while
  129.1 4.4 %copy-start.27 = (pred[128]{0:T(512)(128)(4,1)}, pred[128]{0:T(512)(128)(4,1)S(1)}, u32[]{:S(2)}) copy-start(pred[128]{0:T(512)(128)(4,1)S(1)} %add_compare_fusion.5) | copy-start | bytes 388 | tf_op jit(solution)/shard_map/while/body/eval_jaxpr/while
  132.6 2.5 copy-start.30
  135.1 3.5 %copy-start.18 = (f32[9,1024]{1,0:T(8,128)S(1)}, f32[9,1024]{1,0:T(8,128)}, u32[]{:S(2)}) copy-start(f32[9,1024]{1,0:T(8,128)} %copy-done.17) | copy-start | bytes 110596 | tf_op jit(solution)/shard_map/while/body/eval_jaxpr/while
  138.6 4.3 %copy-start.17 = (f32[9,1024]{1,0:T(8,128)}, f32[9,1024]{1,0:T(8,128)S(1)}, u32[]{:S(2)}) copy-start(f32[9,1024]{1,0:T(8,128)S(1)} %get-tuple-element.840) | copy-start | bytes 110596 | tf_op jit(solution)/shard_map/while/body/eval_jaxpr/while
  139.8 4.4 %copy-start.27 = (pred[128]{0:T(512)(128)(4,1)}, pred[128]{0:T(512)(128)(4,1)S(1)}, u32[]{:S(2)}) copy-start(pred[128]{0:T(512)(128)(4,1)S(1)} %add_compare_fusion.5) | copy-start | bytes 388 | tf_op jit(solution)/shard_map/while/body/eval_jaxpr/while
  143.3 2.5 copy-start.30
  145.8 3.5 %copy-start.18 = (f32[9,1024]{1,0:T(8,128)S(1)}, f32[9,1024]{1,0:T(8,128)}, u32[]{:S(2)}) copy-start(f32[9,1024]{1,0:T(8,128)} %copy-done.17) | copy-start | bytes 110596 | tf_op jit(solution)/shard_map/while/body/eval_jaxpr/while
  149.3 4.3 %copy-start.17 = (f32[9,1024]{1,0:T(8,128)}, f32[9,1024]{1,0:T(8,128)S(1)}, u32[]{:S(2)}) copy-start(f32[9,1024]{1,0:T(8,128)S(1)} %get-tuple-element.840) | copy-start | bytes 110596 | tf_op jit(solution)/shard_map/while/body/eval_jaxpr/while
  150.6 4.4 %copy-start.27 = (pred[128]{0:T(512)(128)(4,1)}, pred[128]{0:T(512)(128)(4,1)S(1)}, u32[]{:S(2)}) copy-start(pred[128]{0:T(512)(128)(4,1)S(1)} %add_compare_fusion.5) | copy-start | bytes 388 | tf_op jit(solution)/shard_map/while/body/eval_jaxpr/while
  154.0 2.5 copy-start.30
  156.5 3.4 %copy-start.18 = (f32[9,1024]{1,0:T(8,128)S(1)}, f32[9,1024]{1,0:T(8,128)}, u32[]{:S(2)}) copy-start(f32[9,1024]{1,0:T(8,128)} %copy-done.17) | copy-start | bytes 110596 | tf_op jit(solution)/shard_map/while/body/eval_jaxpr/while
  161.0 50.3 %copy-start.39 = (s32[2048,1]{0,1:T(1,128)S(1)}, s32[2048,1]{0,1:T(1,128)}, u32[]{:S(2)}) copy-start(s32[2048,1]{0,1:T(1,128)} %reshape.555) | copy-start | bytes 24580
  165.9 54.9 %all-to-all-start.2 = ((f32[64,1,288]{2,1,0:T(1,128)}), f32[64,1,288]{2,1,0:T(1,128)S(1)}, u32[]{:S(2)}, u32[]{:S(2)}) async-start(f32[64,1,288]{2,1,0:T(1,128)} %reshape.656), calls=%async_computation.2 | async-start | bytes 196608 | tf_op jit(solution)/shard_map/all_to_all | solution.py:258
  234.1 14.2 %copy-start.4 = (f32[4,16,2048]{2,0,1:T(4,128)S(1)}, f32[4,16,2048]{2,0,1:T(4,128)}, u32[]{:S(2)}) copy-start(f32[4,16,2048]{2,0,1:T(4,128)} %copy-done.3) | copy-start | bytes 1572868
  248.3 1.1 copy-start.14
  248.3 1.1 copy-start.15
  248.3 1.1 copy-start.16
  249.0 0.8 copy-start.13
  250.0 1.9 copy-start.20
  250.0 1.9 copy-start.22
  250.0 1.9 copy-start.24
  250.1 2.2 copy-start.7
  251.8 1.2 copy-start.25
  251.8 1.2 copy-start.29
  251.9 1.3 copy-start.9
  252.0 1.2 copy-start.11
  252.1 1.3 copy-start.38
  252.1 1.3 copy-start.32
  252.1 1.3 copy-start.33
  252.1 1.3 copy-start.34
  252.1 1.3 copy-start.35
  252.1 1.3 copy-start.36
  252.1 1.3 copy-start.37
  252.2 1.5 copy-start.26
  253.5 1.2 copy-start.2
  253.5 1.2 copy-start.5
  253.5 1.3 copy-start.6
  253.5 1.3 copy-start.44
  (1 other events, 0.7 us)

commit v2 on v1

--- a/solution.py
+++ b/solution.py
@@ -219,13 +219,13 @@
     tile_cols = tiles_here * peers // TILE_ROWS
     center_x = 0.5 * TILE_SIDE * tile_cols
     center_y = 0.5 * TILE_SIDE * TILE_ROWS
-    view_cameras = cameras[camera_ids]
-    camera = view_cameras[lax.axis_index("views")]
+    camera = cameras[camera_ids[0]]
     attrs = project(gaussians, camera, center_x, center_y)
     owner_flat = list_owner.reshape(-1)
     index_flat = list_index.reshape(-1)
-    one_hot = (owner_flat[:, None] == jnp.arange(peers)[None, :]).astype(jnp.int32)
-    rank = jnp.sum((jnp.cumsum(one_hot, axis=0) - 1) * one_hot, axis=1)
+    earlier = jnp.arange(entries)[None, :] < jnp.arange(entries)[:, None]
+    same = owner_flat[:, None] == owner_flat[None, :]
+    rank = jnp.sum((same & earlier).astype(jnp.int32), axis=1)
     slot = owner_flat * capacity + rank
     asked_for = (
         jnp.zeros((peers * capacity,), jnp.int32)
@@ -261,7 +261,11 @@
         .at[:, asked.reshape(-1)]
         .add(grad_back.reshape(9, peers * capacity))
     )
-    view_grads = lax.all_gather(attr_grad, "views", axis=0, tiled=False)
+    payload = jnp.concatenate([attr_grad.reshape(-1), jnp.pad(camera, (0, 128 - 12))])
+    gathered = lax.all_gather(payload.reshape(-1, 128), "views", axis=0, tiled=False)
+    gathered = gathered.reshape(gathered.shape[0], -1)
+    view_grads = gathered[:, : 9 * owned].reshape(-1, 9, owned)
+    view_cameras = gathered[:, 9 * owned : 9 * owned + 12]
 
     def pull(view_camera, grad):
         ignored, pullback = jax.vjp(
@@ -287,7 +291,7 @@
             P(None, "tiles"),
             P(),
             P(),
-            P(),
+            P("views"),
             P("views", "tiles", None, None),
             P("views", "tiles", None),
             P("views", "tiles"),

time: 259 us -> 240 us (0.927)
  the two profiles are of different devices: /device:TPU:2 before, /device:TPU:8 now
where the time goes in v2:
time: 240 us; the launch traced here: 236 us
  other arithmetic  98 us (41%)
  matrix products  47.8 us (20%)
  local copies, waits for them, and re-layouts  28.9 us (12%)
  starting transfers between devices  26.8 us (11%)
  waiting for transfers between devices  18.2 us (8%)
  blocking collectives  11.8 us (5%)
  between operations  3.12 us (1%)
    dot_general x8, matrix products, backward(): lax.dot_general(resid, piece[6:9], (((0,), (0,)), ((), ())), precision=pr...  16 us
    mul x16, other arithmetic, block_terms(): alpha = jnp.where(live, piece[5][None, :] * falloff, 0.0)  16 us
    dot_general x8, matrix products, backward(): color_grad = jnp.dot(resid, weight, precision=precise)  14.4 us
    dot_general x8, matrix products, forward(): lax.dot_general(piece[6:9], weight, (((1,), (1,)), ((), ())), precision=p...  13.3 us
    scatter-add x1, other arithmetic, body(): attr_grad = jnp.zeros((9, owned), jnp.float32).at[:, asked.reshape(-1)].a...  12.6 us
    all_to_all x1, starting transfers between devices, body(): lax.all_to_all(asked_for, 'tiles', split_axis=0, concat_axis=0, tiled=True)  11.9 us
    all_gather x1, blocking collectives, body(): lax.all_gather(payload.reshape(-1, 128), 'views', axis=0, tiled=False)  11.8 us
    all_to_all x1, waiting for transfers between devices, body(): lax.all_to_all(grad_send, 'tiles', split_axis=1, concat_axis=1, tiled=True)  10.5 us
  transfers between devices with their start and end apart: 3, of which 2 were waited for; matrix products, arithmetic and copies ran while one was open for 6% of the time, Pallas kernels for 0%

profile of v2, /device:TPU:8, one launch (start us, length us, event | category | flops | bytes accessed | tf_op | source)
XLA Modules:
  0.0 236.0 jit_solution(14769879873712483938)
XLA Ops:
  0.7 1.3 convert_reduce_fusion
  2.7 4.5 %scatter_custom_fusion = s32[2048]{0:T(1024)S(1)} fusion(s32[1024]{0:T(1024)S(1)} %bitcast.536, s32[1024]{0:T(1024)} %bitcast.543, s32[]{:T(128)} %constant.99.clone.1), kind=kCustom, calls=%fused_computation.461 | custom fusion | bytes 8704 | tf_op jit(solution)/shard_map/scatter | solution.py:233
  7.8 11.9 %all-to-all-start = ((s32[64,1,32]{2,1,0:T(1,128)}), s32[64,1,32]{2,1,0:T(1,128)S(1)}, u32[]{:S(2)}, u32[]{:S(2)}) async-start(s32[64,1,32]{2,1,0:T(1,128)} %bitcast.6), calls=%async_computation | async-start | bytes 65536 | tf_op jit(solution)/shard_map/all_to_all | solution.py:236
  20.5 1.5 fusion.187
  22.1 1.0 slice.194
  24.1 0.9 multiply_reduce_fusion.7
  25.1 1.0 convolution_add_fusion.2
  26.8 1.0 fusion.188
  32.0 5.5 %gather_fusion = f32[2048,9]{1,0:T(8,128)S(1)} fusion(f32[9,2048]{0,1:T(8,128)S(1)} %copy.116, s32[2048]{0:T(1024)S(1)} %broadcast_clamp_fusion), kind=kCustom, calls=%fused_computation | custom fusion | bytes 155648 | tf_op jit(solution)/shard_map/jit(_take)/gather | solution.py:237
  38.9 10.3 %all-to-all-start.1 = ((f32[64,1,288]{2,1,0:T(1,128)}), f32[64,1,288]{2,1,0:T(1,128)S(1)}, u32[]{:S(2)}, u32[]{:S(2)}) async-start(f32[64,1,288]{2,1,0:T(1,128)} %reshape.630), calls=%async_computation.1 | async-start | bytes 196608 | tf_op jit(solution)/shard_map/all_to_all | solution.py:238
  52.0 7.7 %all-to-all-done.1 = f32[64,1,288]{2,1,0:T(1,128)S(1)} async-done(((f32[64,1,288]{2,1,0:T(1,128)}), f32[64,1,288]{2,1,0:T(1,128)S(1)}, u32[]{:S(2)}, u32[]{:S(2)}) %all-to-all-start.1) | async-done | bytes 73760 | tf_op jit(solution)/shard_map/all_to_all | solution.py:238
  61.5 2.8 %gather_fusion.1 = f32[1024,9]{1,0:T(8,128)S(1)} fusion(f32[9,2048]{0,1:T(8,128)S(1)} %bitcast.486, s32[1024]{0:T(1024)S(1)} %broadcast_clamp_fusion.1), kind=kCustom, calls=%fused_computation.1 | custom fusion | bytes 77824 | tf_op jit(solution)/shard_map/gather | solution.py:239
  65.2 35.0 %while.40 = (s32[]{:T(128)}, f32[3,1024]{1,0:T(4,128)S(1)}, f32[1024]{0:T(1024)S(1)}, s32[]{:T(128)}, f32[9,1024]{1,0:T(8,128)}, /*index=5*/s32[]{:T(128)}, s32[...) while((s32[]{:T(128)}, f32[3,1024]{1,0:T(4,128)S(1)}, ...), condition=%wide.region_11.12_spmd.clone, body=%wide.region_8.11_spmd.clone.sunk | while | flops 25580940 | bytes 2181847 | solution.py:149
  65.9 1.0 dynamic-slice_bitcast_fusion.12
  67.9 1.7 convolution_add_fusion.4
  70.2 1.0 dynamic-slice_bitcast_fusion.12
  72.3 1.7 convolution_add_fusion.4
  74.6 1.0 dynamic-slice_bitcast_fusion.12
  76.6 1.7 convolution_add_fusion.4
  79.0 1.0 dynamic-slice_bitcast_fusion.12
  81.0 1.7 convolution_add_fusion.4
  83.4 1.0 dynamic-slice_bitcast_fusion.12
  85.4 1.7 convolution_add_fusion.4
  87.7 1.0 dynamic-slice_bitcast_fusion.12
  89.8 1.7 convolution_add_fusion.4
  92.1 1.0 dynamic-slice_bitcast_fusion.12
  94.1 1.7 convolution_add_fusion.4
  96.5 1.0 dynamic-slice_bitcast_fusion.12
  98.5 1.7 convolution_add_fusion.4
  100.9 78.8 %while.41 = (s32[]{:T(128)}, f32[9,1024]{1,0:T(8,128)S(1)}, f32[1024]{0:T(1024)S(1)}, f32[1024]{0:T(1024)S(1)}, s32[]{:T(128)}, /*index=5*/f32[9,1024]{1,0:T(8,1...) while((s32[]{:T(128)}, f32[9,1024]{1,0:T(8,128)S(1)}, ...), condition=%wide.region_23.24_spmd.clone, body=%wide.region_13.23_spmd.clone.sunk | while | flops 55855884 | bytes 9097859 | solution.py:187
  101.8 1.0 dynamic-slice_bitcast_fusion.13
  103.8 1.8 convolution_bitcast_fusion.4
  105.6 2.0 fusion.222
  111.6 1.0 dynamic-slice_bitcast_fusion.13
  113.6 1.8 convolution_bitcast_fusion.4
  115.4 2.0 fusion.222
  118.8 0.9 fusion.224
  121.5 1.0 dynamic-slice_bitcast_fusion.13
  123.5 1.8 convolution_bitcast_fusion.4
  125.3 2.0 fusion.222
  128.7 0.9 fusion.224
  131.3 1.0 dynamic-slice_bitcast_fusion.13
  133.3 1.8 convolution_bitcast_fusion.4
  135.1 2.0 fusion.222
  141.1 1.0 dynamic-slice_bitcast_fusion.13
  143.1 1.8 convolution_bitcast_fusion.4
  144.9 2.0 fusion.222
  151.0 1.0 dynamic-slice_bitcast_fusion.13
  153.0 1.8 convolution_bitcast_fusion.4
  154.8 2.0 fusion.222
  160.8 1.0 dynamic-slice_bitcast_fusion.13
  162.8 1.8 convolution_bitcast_fusion.4
  164.6 2.0 fusion.222
  168.0 0.9 fusion.224
  170.6 1.0 dynamic-slice_bitcast_fusion.13
  172.6 1.8 convolution_bitcast_fusion.4
  174.4 2.0 fusion.222
  180.0 3.5 %scatter_custom_fusion.1 = f32[9,2048]{0,1:T(8,128)S(1)} fusion(s32[1024]{0:T(1024)} %bitcast.537, f32[1024,9]{1,0:T(8,128)S(1)} %copy.121, f32[]{:T(128)} %constant.102.clone.1), kind=kCustom, calls=%fused_computation.139 | custom fusion | bytes 74240 | tf_op jit(solution)/shard_map/scatter | solution.py:255
  184.8 4.6 %all-to-all-start.2 = ((f32[64,1,288]{2,1,0:T(1,128)}), f32[64,1,288]{2,1,0:T(1,128)S(1)}, u32[]{:S(2)}, u32[]{:S(2)}) async-start(f32[64,1,288]{2,1,0:T(1,128)} %reshape.632), calls=%async_computation.2 | async-start | bytes 196608 | tf_op jit(solution)/shard_map/all_to_all | solution.py:258
  189.5 10.5 %all-to-all-done.2 = f32[64,1,288]{2,1,0:T(1,128)S(1)} async-done(((f32[64,1,288]{2,1,0:T(1,128)}), f32[64,1,288]{2,1,0:T(1,128)S(1)}, u32[]{:S(2)}, u32[]{:S(2)}) %all-to-all-start.2) | async-done | bytes 73760 | tf_op jit(solution)/shard_map/all_to_all | solution.py:258
  201.5 12.6 %scatter_custom_fusion.2 = f32[9,2048]{0,1:T(8,128)S(1)} fusion(s32[2048]{0:T(1024)S(1)} %bitcast.539, f32[2048,9]{1,0:T(8,128)S(1)} %copy.124, f32[]{:T(128)} %constant.102.clone.1), kind=kCustom, calls=%fused_computation.137 | custom fusion | flops 18432 | bytes 73732 | tf_op jit(solution)/shard_map/scatter-add | solution.py:262
  214.5 11.8 %all_gather.3 = f32[4,145,128]{2,1,0:T(8,128)S(1)} all-gather(f32[1,145,128]{2,1,0:T(8,128)S(1)} %fusion.89), channel_id=1, replica_groups=mesh['tiles'=64,'views'=4] {'views'}, dimensions={0}, use_global_device_ids=true | all-gather | bytes 371200 | tf_op jit(solution)/shard_map/all_gather | solution.py:265
  228.1 1.3 multiply_reduce_fusion.3
  234.6 1.3 divide_subtract_fusion
  (357 shorter events, 74.0 us)
Async XLA Ops:
  0.6 19.8 %copy-start = (f32[16,12]{1,0:T(8,128)S(1)}, f32[16,12]{1,0:T(8,128)}, u32[]{:S(2)}) copy-start(f32[16,12]{1,0:T(8,128)} %param.19) | copy-start | bytes 2308
  0.6 27.3 %copy-start.1 = (f32[59,2048]{1,0:T(8,128)S(1)}, f32[59,2048]{1,0:T(8,128)}, u32[]{:S(2)}) copy-start(f32[59,2048]{1,0:T(8,128)} %param.15) | copy-start | bytes 1449988
  2.6 22.4 %copy-start.28 = (s32[1024,1]{0,1:T(1,128)}, s32[1024,1]{0,1:T(1,128)S(1)}, u32[]{:S(2)}) copy-start(s32[1024,1]{0,1:T(1,128)S(1)} %compare_select_fusion.3) | copy-start | bytes 12292
  7.8 24.0 %all-to-all-start = ((s32[64,1,32]{2,1,0:T(1,128)}), s32[64,1,32]{2,1,0:T(1,128)S(1)}, u32[]{:S(2)}, u32[]{:S(2)}) async-start(s32[64,1,32]{2,1,0:T(1,128)} %bitcast.6), calls=%async_computation | async-start | bytes 65536 | tf_op jit(solution)/shard_map/all_to_all | solution.py:236
  28.6 1.4 copy-start.13
  28.6 1.4 copy-start.15
  28.6 2.0 copy-start.5
  28.6 2.0 copy-start.17
  37.4 11.7 %copy-start.29 = (s32[1024,1]{0,1:T(1,128)S(1)}, s32[1024,1]{0,1:T(1,128)}, u32[]{:S(2)}) copy-start(s32[1024,1]{0,1:T(1,128)} %copy-done.28) | copy-start | bytes 12292
  38.9 20.8 %all-to-all-start.1 = ((f32[64,1,288]{2,1,0:T(1,128)}), f32[64,1,288]{2,1,0:T(1,128)S(1)}, u32[]{:S(2)}, u32[]{:S(2)}) async-start(f32[64,1,288]{2,1,0:T(1,128)} %reshape.630), calls=%async_computation.1 | async-start | bytes 196608 | tf_op jit(solution)/shard_map/all_to_all | solution.py:238
  65.2 35.0 %copy-start.30 = (bf16[1,1,3,1024]{3,2,1,0:T(4,128)(2,1)S(1)}, bf16[1,1,3,1024]{3,2,1,0:T(4,128)(2,1)}, u32[]{:S(2)}) copy-start(bf16[1,1,3,1024]{3,2,1,0:T(4,128)(2,1)} %param.24) | copy-start | bytes 18436
  65.2 35.1 %copy-start.31 = (f32[3]{0:T(128)S(1)}, f32[3]{0:T(128)}, u32[]{:S(2)}) copy-start(f32[3]{0:T(128)} %param.25) | copy-start | bytes 40
  180.0 9.4 %copy-start.27 = (s32[2048,1]{0,1:T(1,128)S(1)}, s32[2048,1]{0,1:T(1,128)}, u32[]{:S(2)}) copy-start(s32[2048,1]{0,1:T(1,128)} %reshape.545) | copy-start | bytes 24580
  184.8 15.2 %all-to-all-start.2 = ((f32[64,1,288]{2,1,0:T(1,128)}), f32[64,1,288]{2,1,0:T(1,128)S(1)}, u32[]{:S(2)}, u32[]{:S(2)}) async-start(f32[64,1,288]{2,1,0:T(1,128)} %reshape.632), calls=%async_computation.2 | async-start | bytes 196608 | tf_op jit(solution)/shard_map/all_to_all | solution.py:258
  226.7 1.4 copy-start.11
  227.9 1.7 copy-start.7
  227.9 1.7 copy-start.8
  227.9 1.7 copy-start.9
  227.9 1.7 copy-start.14
  228.0 1.7 copy-start.16
  228.0 1.7 copy-start.18
  228.0 1.8 copy-start.6
  228.0 1.8 copy-start.10
  229.4 0.7 copy-start.12
  229.4 1.2 copy-start.2
  231.7 0.7 copy-start.26
  232.0 1.4 copy-start.20
  232.0 1.4 copy-start.21
  232.0 1.4 copy-start.22
  232.0 1.4 copy-start.23
  232.0 1.4 copy-start.24
  232.0 1.4 copy-start.25
  232.2 1.5 copy-start.19
  233.4 1.2 copy-start.3
  233.4 1.2 copy-start.4
  233.4 1.2 copy-start.32

commit v3 on v2

--- a/solution.py
+++ b/solution.py
@@ -3,6 +3,8 @@
 import jax
 import jax.numpy as jnp
 from jax import lax
+from jax.experimental import pallas as pl
+from jax.experimental.pallas import tpu as pltpu
 from jax.sharding import PartitionSpec as P
 
 TILE_SIDE = 32
@@ -10,6 +12,8 @@
 TILE_ROWS = 8
 LIST = 1024
 BLOCK = 128
+KB = 128
+PC = 128
 
 
 focal_length = 400.0
@@ -186,6 +190,100 @@
     start_grads = jnp.zeros((9, LIST), jnp.float32)
     grads, ignored, unused = lax.fori_loop(0, blocks, backward, (start_grads, zeros_pix, zeros_pix))
     return (image, grads)
+
+
+def render_kernel(counts_ref, tiles_ref, entry_ref, target_ref, bg_ref, image_ref, sums_ref, *, tile_cols):
+    t = pl.program_id(0)
+    count = counts_ref[t]
+    tile = tiles_ref[t]
+    blocks = (count + KB - 1) // KB
+    sums_ref[...] = jnp.zeros(sums_ref.shape, jnp.float32)
+    row = lax.broadcasted_iota(jnp.int32, (KB, KB), 0)
+    col = lax.broadcasted_iota(jnp.int32, (KB, KB), 1)
+    upper = (row <= col).astype(jnp.float32)
+    lane = lax.broadcasted_iota(jnp.int32, (1, KB), 1)
+    base_x = (tile % tile_cols) * TILE_SIDE
+    base_y = (tile // tile_cols) * TILE_SIDE
+    bg = bg_ref[...]
+
+    def terms(index, pix_x, pix_y):
+        start = pl.multiple_of(index * KB, KB)
+        blk = entry_ref[:, pl.ds(start, KB)]
+        live = (start + lane) < count
+        delta_x = pix_x - blk[0:1]
+        delta_y = pix_y - blk[1:2]
+        power = -0.5 * (blk[2:3] * delta_x * delta_x + 2.0 * blk[3:4] * delta_x * delta_y + blk[4:5] * delta_y * delta_y)
+        falloff = jnp.exp(power)
+        alpha = jnp.where(live, blk[5:6] * falloff, 0.0)
+        log_keep = jnp.log1p(-alpha)
+        cum = jnp.dot(log_keep, upper, precision=precise, preferred_element_type=jnp.float32)
+        return start, blk, live, delta_x, delta_y, falloff, alpha, log_keep, cum
+
+    def chunk(c, carry):
+        first = pl.multiple_of(c * PC, PC)
+        q = first + lax.broadcasted_iota(jnp.int32, (PC, KB), 0)
+        pix_x = (base_x + q % TILE_SIDE).astype(jnp.float32) + 0.5
+        pix_y = (base_y + q // TILE_SIDE).astype(jnp.float32) + 0.5
+
+        def forward(i, fc):
+            log_total, color = fc
+            start, blk, live, dx, dy, fall, alpha, lk, cum = terms(i, pix_x, pix_y)
+            weight = jnp.exp(log_total + cum - lk) * alpha
+            color = color + lax.dot_general(weight, blk[8:16], (((1,), (1,)), ((), ())), precision=precise, preferred_element_type=jnp.float32)
+            return (log_total + cum[:, KB - 1:KB], color)
+
+        log_total, color = lax.fori_loop(0, blocks, forward, (jnp.zeros((PC, 1), jnp.float32), jnp.zeros((PC, 8), jnp.float32)))
+        image = color + jnp.exp(log_total) * bg
+        image_ref[pl.ds(first, PC), :] = image
+        resid = image - target_ref[pl.ds(first, PC), :]
+        dot_total = jnp.sum(image * resid, axis=1, keepdims=True)
+
+        def backward(i, bc):
+            log_before, prefix = bc
+            start, blk, live, dx, dy, fall, alpha, lk, cum = terms(i, pix_x, pix_y)
+            trans = jnp.exp(log_before + cum - lk)
+            weight = trans * alpha
+            along = jnp.dot(resid, blk[8:16], precision=precise, preferred_element_type=jnp.float32)
+            running = prefix + jnp.dot(weight * along, upper, precision=precise, preferred_element_type=jnp.float32)
+            d_alpha = jnp.where(live, trans * along - (dot_total - running) / (1.0 - alpha), 0.0)
+            d_power = d_alpha * alpha
+            px_term = d_power * dx
+            py_term = d_power * dy
+            parts = [
+                px_term, py_term, px_term * dx, px_term * dy, py_term * dy, d_alpha * fall,
+                weight * resid[:, 0:1], weight * resid[:, 1:2], weight * resid[:, 2:3],
+            ]
+            for r, part in enumerate(parts):
+                sums_ref[r:r + 1, pl.ds(start, KB)] += jnp.sum(part, axis=0, keepdims=True)
+            return (log_before + cum[:, KB - 1:KB], running[:, KB - 1:KB])
+
+        lax.fori_loop(0, blocks, backward, (jnp.zeros((PC, 1), jnp.float32), jnp.zeros((PC, 1), jnp.float32)))
+        return carry
+
+    lax.fori_loop(0, PIXELS // PC, chunk, 0)
+
+
+def render_tiles(entry16, counts, tiles, target8, bg8, tile_cols):
+    n = entry16.shape[0]
+    return pl.pallas_call(
+        partial(render_kernel, tile_cols=tile_cols),
+        grid=(n,),
+        in_specs=[
+            pl.BlockSpec(memory_space=pltpu.SMEM),
+            pl.BlockSpec(memory_space=pltpu.SMEM),
+            pl.BlockSpec((None, 16, LIST), lambda t: (t, 0, 0)),
+            pl.BlockSpec((None, PIXELS, 8), lambda t: (t, 0, 0)),
+            pl.BlockSpec((1, 8), lambda t: (0, 0)),
+        ],
+        out_specs=[
+            pl.BlockSpec((None, PIXELS, 8), lambda t: (t, 0, 0)),
+            pl.BlockSpec((None, 16, LIST), lambda t: (t, 0, 0)),
+        ],
+        out_shape=[
+            jax.ShapeDtypeStruct((n, PIXELS, 8), jnp.float32),
+            jax.ShapeDtypeStruct((n, 16, LIST), jnp.float32),
+        ],
+    )(counts, tiles, entry16, target8, bg8)
 
 
 def adam_step(values, first, second, grad, rates):
@@ -239,16 +337,32 @@
     entry_attrs = returned.reshape(9, peers * capacity)[:, slot].reshape(9, tiles_here, LIST)
     first_tile = lax.axis_index("tiles") * tiles_here
 
-    def render(item):
-        local_tile, entry, count, target = item
-        pixel_x, pixel_y = pixel_grid(first_tile + local_tile, tile_cols)
-        return tile_pass(entry, count, pixel_x, pixel_y, target.astype(jnp.float32), background)
-
-    images, tile_grads = lax.map(
-        render,
-        (jnp.arange(tiles_here), jnp.moveaxis(entry_attrs, 1, 0), list_length[0], targets[0]),
-    )
-    flat_grads = jnp.moveaxis(tile_grads, 0, 1).reshape(9, entries)
+    colors_pad = jnp.zeros((5, tiles_here, LIST), jnp.float32)
+    entry16 = jnp.moveaxis(
+        jnp.concatenate([entry_attrs[0:6], colors_pad[0:2], entry_attrs[6:9], colors_pad], axis=0), 1, 0
+    )
+    target8 = jnp.pad(
+        jnp.swapaxes(targets[0].astype(jnp.float32), 1, 2), ((0, 0), (0, 0), (0, 5))
+    )
+    background8 = jnp.pad(background, (0, 5))[None]
+    tile_ids = first_tile + jnp.arange(tiles_here, dtype=jnp.int32)
+    image8, sums = render_tiles(entry16, list_length[0], tile_ids, target8, background8, tile_cols)
+    images = jnp.swapaxes(image8[:, :, 0:3], 1, 2)
+    sums = jnp.moveaxis(sums, 1, 0).reshape(16, entries)
+    flat = entry_attrs.reshape(9, entries)
+    flat_grads = jnp.stack(
+        [
+            flat[2] * sums[0] + flat[3] * sums[1],
+            flat[3] * sums[0] + flat[4] * sums[1],
+            -0.5 * sums[2],
+            -sums[3],
+            -0.5 * sums[4],
+            sums[5],
+            sums[6],
+            sums[7],
+            sums[8],
+        ]
+    )
     grad_send = (
         jnp.zeros((9, peers * capacity), jnp.float32)
         .at[:, slot]

time: 240 us -> 208 us (0.87)
  the two profiles are of different devices: /device:TPU:8 before, /device:TPU:2 now
where the time goes in v3:
time: 208 us; the launch traced here: 206 us
  starting transfers between devices  53.8 us (26%)
  Pallas kernels  48.3 us (23%)
  other arithmetic  35.8 us (17%)
  local copies, waits for them, and re-layouts  30 us (14%)
  waiting for transfers between devices  18 us (9%)
  blocking collectives  13 us (6%)
  matrix products  4.22 us (2%)
  between operations  3.17 us (2%)
    pallas_call x1, Pallas kernels, render_tiles(): pl.pallas_call(partial(render_kernel, tile_cols=tile_cols), grid=(n,), in...  48.3 us
    all_to_all x1, starting transfers between devices, body(): lax.all_to_all(grad_send, 'tiles', split_axis=1, concat_axis=1, tiled=True)  31.5 us
    scatter-add x1, other arithmetic, body(): attr_grad = jnp.zeros((9, owned), jnp.float32).at[:, asked.reshape(-1)].a...  13.1 us
    all_gather x1, blocking collectives, body(): lax.all_gather(payload.reshape(-1, 128), 'views', axis=0, tiled=False)  13 us
    all_to_all x1, starting transfers between devices, body(): lax.all_to_all(asked_for, 'tiles', split_axis=0, concat_axis=0, tiled=True)  12 us
    all_to_all x1, starting transfers between devices, body(): lax.all_to_all(served, 'tiles', split_axis=1, concat_axis=1, tiled=True)  10.3 us
    all_to_all x1, waiting for transfers between devices, body(): lax.all_to_all(served, 'tiles', split_axis=1, concat_axis=1, tiled=True)  9.38 us
    all_to_all x1, waiting for transfers between devices, body(): lax.all_to_all(grad_send, 'tiles', split_axis=1, concat_axis=1, tiled=True)  8.61 us
  transfers between devices with their start and end apart: 3, of which 2 were waited for; matrix products, arithmetic and copies ran while one was open for 7% of the time, Pallas kernels for 0%

profile of v3, /device:TPU:2, one launch (start us, length us, event | category | flops | bytes accessed | tf_op | source)
XLA Modules:
  0.0 206.3 jit_solution(474400813438251114)
XLA Ops:
  0.7 1.3 convert_reduce_fusion
  2.0 0.7 compare_select_fusion.3
  2.7 4.5 %scatter_custom_fusion = s32[2048]{0:T(1024)S(1)} fusion(s32[1024]{0:T(1024)S(1)} %bitcast.494, s32[1024]{0:T(1024)} %bitcast.501, s32[]{:T(128)} %constant.40.clone.1), kind=kCustom, calls=%fused_computation.358 | custom fusion | bytes 8704 | tf_op jit(solution)/shard_map/scatter | solution.py:331
  7.2 0.7 all_to_all.16
  7.8 12.0 %all-to-all-start = ((s32[64,1,32]{2,1,0:T(1,128)}), s32[64,1,32]{2,1,0:T(1,128)S(1)}, u32[]{:S(2)}, u32[]{:S(2)}) async-start(s32[64,1,32]{2,1,0:T(1,128)} %bitcast.7), calls=%async_computation | async-start | bytes 65536 | tf_op jit(solution)/shard_map/all_to_all | solution.py:334
  20.5 0.5 fusion.136
  21.2 0.6 broadcast_clamp_fusion.1
  21.7 1.5 fusion.124
  23.3 1.0 slice.220
  24.3 0.6 constant_dynamic-update-slice_fusion.15
  25.3 0.9 multiply_reduce_fusion.6
  26.3 1.0 convolution_add_fusion.1
  27.4 0.6 multiply_divide_fusion.1
  28.0 1.0 fusion.125
  29.1 0.7 slice_multiply_fusion.18
  30.1 0.3 fusion.24
  30.6 0.2 copy.124
  30.8 0.8 pad_convert_fusion.target_ref
  31.9 0.2 stack.30
  32.3 0.6 broadcast_multiply_fusion.5
  32.9 0.5 pad_bitcast_fusion.bg_ref
  34.2 0.7 copy.137
  34.9 0.2 concatenate.9
  35.2 0.4 copy.120
  35.6 0.5 broadcast.899
  36.1 0.7 reduce.9
  37.0 5.5 %gather_fusion = f32[2048,9]{1,0:T(8,128)S(1)} fusion(f32[9,2048]{0,1:T(8,128)S(1)} %copy.120, s32[2048]{0:T(1024)S(1)} %broadcast_clamp_fusion), kind=kCustom, calls=%fused_computation | custom fusion | bytes 155648 | tf_op jit(solution)/shard_map/jit(_take)/gather | solution.py:335
  42.5 0.5 copy.121
  43.0 0.9 reshape.653
  43.9 10.3 %all-to-all-start.1 = ((f32[64,1,288]{2,1,0:T(1,128)}), f32[64,1,288]{2,1,0:T(1,128)S(1)}, u32[]{:S(2)}, u32[]{:S(2)}) async-start(f32[64,1,288]{2,1,0:T(1,128)} %reshape.653), calls=%async_computation.1 | async-start | bytes 196608 | tf_op jit(solution)/shard_map/all_to_all | solution.py:336
  54.2 9.4 %all-to-all-done.1 = f32[64,1,288]{2,1,0:T(1,128)S(1)} async-done(((f32[64,1,288]{2,1,0:T(1,128)}), f32[64,1,288]{2,1,0:T(1,128)S(1)}, u32[]{:S(2)}, u32[]{:S(2)}) %all-to-all-start.1) | async-done | bytes 73760 | tf_op jit(solution)/shard_map/all_to_all | solution.py:336
  63.6 0.6 broadcast.909
  64.2 0.9 reduce.10
  65.2 0.5 copy.122
  65.7 2.8 %gather_fusion.1 = f32[1024,9]{1,0:T(8,128)S(1)} fusion(f32[9,2048]{0,1:T(8,128)S(1)} %bitcast.443, s32[1024]{0:T(1024)S(1)} %copy-done.35), kind=kCustom, calls=%fused_computation.1 | custom fusion | bytes 77824 | tf_op jit(solution)/shard_map/gather | solution.py:337
  68.7 0.7 maximum_bitcast_fusion.entry_ref
  69.4 48.3 %shard_map.138 = (f32[1,1024,8]{2,1,0:T(8,128)}, f32[1,16,1024]{2,1,0:T(8,128)}) custom-call(s32[1]{0:T(128)} %bitcast.438.counts_ref, s32[1]{0:T(128)} %bitcast.1.tiles_ref, f32[1,16,1024]{2,1,0:T(8,128)} %maximum_bitcast_fusion.entry_ref, f32[1,1024,8]{2,1,0:T(8,128)} %pad_convert_fusion.target_ref, f32[1,8]{1,0:T(1,128)} %pad_bitcast_fusion.bg_ref), custom_call_target="tpu_custom_call" | custom-call | tf_op jit(solution)/shard_map/pallas_call | solution.py:268
  117.7 0.9 fusion.107
  118.5 1.0 slice_bitcast_fusion.8
  119.6 0.2 copy.125
  119.8 3.6 %scatter_custom_fusion.1 = f32[9,2048]{0,1:T(8,128)S(1)} fusion(s32[1024]{0:T(1024)} %bitcast.496, f32[1024,9]{1,0:T(8,128)S(1)} %copy.125, f32[]{:T(128)} %constant.48.clone.1), kind=kCustom, calls=%fused_computation.23 | custom fusion | bytes 74240 | tf_op jit(solution)/shard_map/scatter | solution.py:369
  123.4 0.5 copy.126
  123.9 0.9 reshape.655
  124.8 31.5 %all-to-all-start.2 = ((f32[64,1,288]{2,1,0:T(1,128)}), f32[64,1,288]{2,1,0:T(1,128)S(1)}, u32[]{:S(2)}, u32[]{:S(2)}) async-start(f32[64,1,288]{2,1,0:T(1,128)} %reshape.655), calls=%async_computation.2 | async-start | bytes 196608 | tf_op jit(solution)/shard_map/all_to_all | solution.py:372
  156.4 0.7 copy.142
  157.1 8.6 %all-to-all-done.2 = f32[64,1,288]{2,1,0:T(1,128)S(1)} async-done(((f32[64,1,288]{2,1,0:T(1,128)}), f32[64,1,288]{2,1,0:T(1,128)S(1)}, u32[]{:S(2)}, u32[]{:S(2)}) %all-to-all-start.2) | async-done | bytes 73760 | tf_op jit(solution)/shard_map/all_to_all | solution.py:372
  165.7 0.9 reduce.11
  167.0 0.4 copy.128
  167.4 13.1 %scatter_custom_fusion.2 = f32[9,2048]{0,1:T(8,128)S(1)} fusion(s32[2048]{0:T(1024)S(1)} %bitcast.497, f32[2048,9]{1,0:T(8,128)S(1)} %copy.128, f32[]{:T(128)} %constant.48.clone.1), kind=kCustom, calls=%fused_computation.21 | custom fusion | flops 18432 | bytes 73732 | tf_op jit(solution)/shard_map/scatter-add | solution.py:376
  180.5 0.3 copy.129
  180.9 13.0 %all_gather.3 = f32[4,145,128]{2,1,0:T(8,128)S(1)} all-gather(f32[1,145,128]{2,1,0:T(8,128)S(1)} %fusion.26), channel_id=1, replica_groups=mesh['tiles'=64,'views'=4] {'views'}, dimensions={0}, use_global_device_ids=true | all-gather | bytes 371200 | tf_op jit(solution)/shard_map/all_gather | solution.py:379
  194.2 0.3 convolution_add_fusion
  194.6 0.5 fusion.21
  195.5 0.3 copy-done.6
  195.9 1.4 multiply_reduce_fusion.2
  197.3 0.2 copy_multiply_fusion
  197.6 0.7 add_divide_fusion
  198.3 0.7 fusion.35
  198.9 0.7 fusion.30
  199.6 0.7 fusion.31
  201.2 0.7 broadcast_multiply_fusion
  202.8 0.4 fusion.10
  204.0 0.9 add_reduce_fusion
  204.9 1.3 divide_subtract_fusion
  (184 shorter events, 5.8 us)
Async XLA Ops:
  0.6 19.9 %copy-start = (f32[16,12]{1,0:T(8,128)S(1)}, f32[16,12]{1,0:T(8,128)}, u32[]{:S(2)}) copy-start(f32[16,12]{1,0:T(8,128)} %param.15) | copy-start | bytes 2308
  0.6 28.5 %copy-start.1 = (f32[59,2048]{1,0:T(8,128)S(1)}, f32[59,2048]{1,0:T(8,128)}, u32[]{:S(2)}) copy-start(f32[59,2048]{1,0:T(8,128)} %param.11) | copy-start | bytes 1449988
  1.9 28.7 %copy-start.37 = (bf16[1,1,3,1024]{3,2,1,0:T(4,128)(2,1)S(1)}, bf16[1,1,3,1024]{3,2,1,0:T(4,128)(2,1)}, u32[]{:S(2)}) copy-start(bf16[1,1,3,1024]{3,2,1,0:T(4,128)(2,1)} %param.20) | copy-start | bytes 18436
  2.7 22.4 %copy-start.36 = (s32[1024,1]{0,1:T(1,128)}, s32[1024,1]{0,1:T(1,128)S(1)}, u32[]{:S(2)}) copy-start(s32[1024,1]{0,1:T(1,128)S(1)} %compare_select_fusion.3) | copy-start | bytes 12292
  7.8 27.7 %all-to-all-start = ((s32[64,1,32]{2,1,0:T(1,128)}), s32[64,1,32]{2,1,0:T(1,128)S(1)}, u32[]{:S(2)}, u32[]{:S(2)}) async-start(s32[64,1,32]{2,1,0:T(1,128)} %bitcast.7), calls=%async_computation | async-start | bytes 65536 | tf_op jit(solution)/shard_map/all_to_all | solution.py:334
  29.8 2.4 %copy-start.13 = (f32[1,2048]{1,0:T(1,128)}, f32[1,2048]{1,0:T(1,128)S(1)}, u32[]{:S(2)}) copy-start(f32[1,2048]{1,0:T(1,128)S(1)} %get-tuple-element.63) | copy-start | bytes 24580
  29.8 2.4 %copy-start.16 = (f32[1,2048]{1,0:T(1,128)}, f32[1,2048]{1,0:T(1,128)S(1)}, u32[]{:S(2)}) copy-start(f32[1,2048]{1,0:T(1,128)S(1)} %get-tuple-element.64) | copy-start | bytes 24580
  29.8 2.4 %copy-start.19 = (f32[1,2048]{1,0:T(1,128)}, f32[1,2048]{1,0:T(1,128)S(1)}, u32[]{:S(2)}) copy-start(f32[1,2048]{1,0:T(1,128)S(1)} %get-tuple-element.65) | copy-start | bytes 24580
  30.6 2.3 %copy-start.42 = (f32[3]{0:T(128)S(1)}, f32[3]{0:T(128)}, u32[]{:S(2)}) copy-start(f32[3]{0:T(128)} %param.21) | copy-start | bytes 40
  43.0 22.6 %copy-start.35 = (s32[1024]{0:T(1024)S(1)}, s32[1024]{0:T(1024)}, u32[]{:S(2)}) copy-start(s32[1024]{0:T(1024)} %broadcast_clamp_fusion.1) | copy-start | bytes 12292
  43.9 19.7 %all-to-all-start.1 = ((f32[64,1,288]{2,1,0:T(1,128)}), f32[64,1,288]{2,1,0:T(1,128)S(1)}, u32[]{:S(2)}, u32[]{:S(2)}) async-start(f32[64,1,288]{2,1,0:T(1,128)} %reshape.653), calls=%async_computation.1 | async-start | bytes 196608 | tf_op jit(solution)/shard_map/all_to_all | solution.py:336
  119.8 36.5 %copy-start.24 = (f32[1,1024,8]{2,1,0:T(8,128)S(1)}, f32[1,1024,8]{2,1,0:T(8,128)}, u32[]{:S(2)}) copy-start(f32[1,1024,8]{2,1,0:T(8,128)} %get-tuple-element.6) | copy-start | bytes 98308
  124.8 40.9 %all-to-all-start.2 = ((f32[64,1,288]{2,1,0:T(1,128)}), f32[64,1,288]{2,1,0:T(1,128)S(1)}, u32[]{:S(2)}, u32[]{:S(2)}) async-start(f32[64,1,288]{2,1,0:T(1,128)} %reshape.655), calls=%async_computation.2 | async-start | bytes 196608 | tf_op jit(solution)/shard_map/all_to_all | solution.py:372
  167.0 13.8 %copy-start.40 = (f32[12]{0:T(128)S(1)}, f32[12]{0:T(128)}, u32[]{:S(2)}) copy-start(f32[12]{0:T(128)} %fusion.136) | copy-start | bytes 148
  194.0 1.0 copy-start.38
  194.2 1.7 copy-start.10
  195.0 0.9 copy-start.5
  195.2 0.6 copy-start.6
  195.5 2.1 %copy-start.14 = (f32[1,2048]{1,0:T(1,128)S(1)}, f32[1,2048]{1,0:T(1,128)}, u32[]{:S(2)}) copy-start(f32[1,2048]{1,0:T(1,128)} %copy-done.13) | copy-start | bytes 24580
  195.5 2.1 %copy-start.17 = (f32[1,2048]{1,0:T(1,128)S(1)}, f32[1,2048]{1,0:T(1,128)}, u32[]{:S(2)}) copy-start(f32[1,2048]{1,0:T(1,128)} %copy-done.16) | copy-start | bytes 24580
  195.5 2.1 %copy-start.20 = (f32[1,2048]{1,0:T(1,128)S(1)}, f32[1,2048]{1,0:T(1,128)}, u32[]{:S(2)}) copy-start(f32[1,2048]{1,0:T(1,128)} %copy-done.19) | copy-start | bytes 24580
  195.9 2.4 %copy-start.8 = (f32[2048]{0:T(1024)S(1)}, f32[2048]{0:T(1024)}, u32[]{:S(2)}) copy-start(f32[2048]{0:T(1024)} %get-tuple-element.162) | copy-start | bytes 24580
  197.3 3.0 %copy-start.11 = (f32[4,3,3]{2,1,0:T(4,128)S(1)}, f32[4,3,3]{2,1,0:T(4,128)}, u32[]{:S(2)}) copy-start(f32[4,3,3]{2,1,0:T(4,128)} %copy-done.10) | copy-start | bytes 436
  197.3 3.0 %copy-start.39 = (f32[4,3]{1,0:T(4,128)S(1)}, f32[4,3]{1,0:T(4,128)}, u32[]{:S(2)}) copy-start(f32[4,3]{1,0:T(4,128)} %copy-done.38) | copy-start | bytes 148
  197.3 3.5 %copy-start.2 = (f32[4,16,2048]{2,0,1:T(4,128)S(1)}, f32[4,16,2048]{2,0,1:T(4,128)}, u32[]{:S(2)}) copy-start(f32[4,16,2048]{2,0,1:T(4,128)} %constant_dynamic-update-slice_fusion.15) | copy-start | bytes 1572868
  201.2 1.2 copy-start.7
  201.9 0.7 copy-start.34
  201.9 0.8 copy-start.12
  202.2 1.4 copy-start.9
  202.2 1.4 copy-start.15
  202.2 1.4 copy-start.18
  202.2 1.4 copy-start.21
  202.2 1.4 copy-start.28
  202.2 1.4 copy-start.29
  202.2 1.4 copy-start.30
  202.2 1.4 copy-start.31
  202.3 1.4 copy-start.32
  202.3 1.4 copy-start.33
  202.4 1.5 copy-start.22
  202.4 1.5 copy-start.23
  202.4 1.5 copy-start.25
  202.4 1.5 copy-start.26
  202.5 1.5 copy-start.27
  203.7 1.2 copy-start.3
  203.7 1.2 copy-start.4
  203.7 1.2 copy-start.41

commit v4 on v3

--- a/solution.py
+++ b/solution.py
@@ -13,7 +13,6 @@
 LIST = 1024
 BLOCK = 128
 KB = 128
-PC = 128
 
 
 focal_length = 400.0
@@ -192,7 +191,19 @@
     return (image, grads)
 
 
-def render_kernel(counts_ref, tiles_ref, entry_ref, target_ref, bg_ref, image_ref, sums_ref, *, tile_cols):
+def split_cumsum(x, upper):
+    high = x.astype(jnp.bfloat16)
+    rest = x - high.astype(jnp.float32)
+    middle = rest.astype(jnp.bfloat16)
+    low = (rest - middle.astype(jnp.float32)).astype(jnp.bfloat16)
+    total = jnp.dot(high, upper, preferred_element_type=jnp.float32)
+    total = total + jnp.dot(middle, upper, preferred_element_type=jnp.float32)
+    return total + jnp.dot(low, upper, preferred_element_type=jnp.float32)
+
+
+def render_kernel(
+    counts_ref, tiles_ref, entry_ref, target_ref, bg_ref, image_ref, sums_ref, trans_ref, fall_ref, *, tile_cols
+):
     t = pl.program_id(0)
     count = counts_ref[t]
     tile = tiles_ref[t]
@@ -200,67 +211,81 @@
     sums_ref[...] = jnp.zeros(sums_ref.shape, jnp.float32)
     row = lax.broadcasted_iota(jnp.int32, (KB, KB), 0)
     col = lax.broadcasted_iota(jnp.int32, (KB, KB), 1)
-    upper = (row <= col).astype(jnp.float32)
+    upper = (row <= col).astype(jnp.bfloat16)
     lane = lax.broadcasted_iota(jnp.int32, (1, KB), 1)
-    base_x = (tile % tile_cols) * TILE_SIDE
-    base_y = (tile // tile_cols) * TILE_SIDE
-    bg = bg_ref[...]
-
-    def terms(index, pix_x, pix_y):
+    pixel = lax.broadcasted_iota(jnp.int32, (PIXELS, KB), 0)
+    pix_x = ((tile % tile_cols) * TILE_SIDE + pixel % TILE_SIDE).astype(jnp.float32) + 0.5
+    pix_y = ((tile // tile_cols) * TILE_SIDE + pixel // TILE_SIDE).astype(jnp.float32) + 0.5
+
+    def geometry(index):
         start = pl.multiple_of(index * KB, KB)
         blk = entry_ref[:, pl.ds(start, KB)]
         live = (start + lane) < count
-        delta_x = pix_x - blk[0:1]
-        delta_y = pix_y - blk[1:2]
-        power = -0.5 * (blk[2:3] * delta_x * delta_x + 2.0 * blk[3:4] * delta_x * delta_y + blk[4:5] * delta_y * delta_y)
+        return start, blk, live, pix_x - blk[0:1], pix_y - blk[1:2]
+
+    def forward(i, carry):
+        log_total, red, green, blue = carry
+        start, blk, live, dx, dy = geometry(i)
+        power = -0.5 * (blk[2:3] * dx * dx + 2.0 * blk[3:4] * dx * dy + blk[4:5] * dy * dy)
         falloff = jnp.exp(power)
         alpha = jnp.where(live, blk[5:6] * falloff, 0.0)
         log_keep = jnp.log1p(-alpha)
-        cum = jnp.dot(log_keep, upper, precision=precise, preferred_element_type=jnp.float32)
-        return start, blk, live, delta_x, delta_y, falloff, alpha, log_keep, cum
-
-    def chunk(c, carry):
-        first = pl.multiple_of(c * PC, PC)
-        q = first + lax.broadcasted_iota(jnp.int32, (PC, KB), 0)
-        pix_x = (base_x + q % TILE_SIDE).astype(jnp.float32) + 0.5
-        pix_y = (base_y + q // TILE_SIDE).astype(jnp.float32) + 0.5
-
-        def forward(i, fc):
-            log_total, color = fc
-            start, blk, live, dx, dy, fall, alpha, lk, cum = terms(i, pix_x, pix_y)
-            weight = jnp.exp(log_total + cum - lk) * alpha
-            color = color + lax.dot_general(weight, blk[8:16], (((1,), (1,)), ((), ())), precision=precise, preferred_element_type=jnp.float32)
-            return (log_total + cum[:, KB - 1:KB], color)
-
-        log_total, color = lax.fori_loop(0, blocks, forward, (jnp.zeros((PC, 1), jnp.float32), jnp.zeros((PC, 8), jnp.float32)))
-        image = color + jnp.exp(log_total) * bg
-        image_ref[pl.ds(first, PC), :] = image
-        resid = image - target_ref[pl.ds(first, PC), :]
-        dot_total = jnp.sum(image * resid, axis=1, keepdims=True)
-
-        def backward(i, bc):
-            log_before, prefix = bc
-            start, blk, live, dx, dy, fall, alpha, lk, cum = terms(i, pix_x, pix_y)
-            trans = jnp.exp(log_before + cum - lk)
-            weight = trans * alpha
-            along = jnp.dot(resid, blk[8:16], precision=precise, preferred_element_type=jnp.float32)
-            running = prefix + jnp.dot(weight * along, upper, precision=precise, preferred_element_type=jnp.float32)
-            d_alpha = jnp.where(live, trans * along - (dot_total - running) / (1.0 - alpha), 0.0)
-            d_power = d_alpha * alpha
-            px_term = d_power * dx
-            py_term = d_power * dy
-            parts = [
-                px_term, py_term, px_term * dx, px_term * dy, py_term * dy, d_alpha * fall,
-                weight * resid[:, 0:1], weight * resid[:, 1:2], weight * resid[:, 2:3],
-            ]
-            for r, part in enumerate(parts):
-                sums_ref[r:r + 1, pl.ds(start, KB)] += jnp.sum(part, axis=0, keepdims=True)
-            return (log_before + cum[:, KB - 1:KB], running[:, KB - 1:KB])
-
-        lax.fori_loop(0, blocks, backward, (jnp.zeros((PC, 1), jnp.float32), jnp.zeros((PC, 1), jnp.float32)))
-        return carry
-
-    lax.fori_loop(0, PIXELS // PC, chunk, 0)
+        cum = split_cumsum(log_keep, upper)
+        trans = jnp.exp(log_total + cum - log_keep)
+        weight = trans * alpha
+        trans_ref[:, pl.ds(start, KB)] = trans
+        fall_ref[:, pl.ds(start, KB)] = falloff
+        return (
+            log_total + cum[:, KB - 1 : KB],
+            red + weight * blk[8:9],
+            green + weight * blk[9:10],
+            blue + weight * blk[10:11],
+        )
+
+    zeros = jnp.zeros((PIXELS, KB), jnp.float32)
+    log_total, red, green, blue = lax.fori_loop(
+        0, blocks, forward, (jnp.zeros((PIXELS, 1), jnp.float32), zeros, zeros, zeros)
+    )
+    lane8 = lax.broadcasted_iota(jnp.int32, (1, 8), 1)
+    color = (
+        jnp.where(lane8 == 0, jnp.sum(red, axis=1, keepdims=True), 0.0)
+        + jnp.where(lane8 == 1, jnp.sum(green, axis=1, keepdims=True), 0.0)
+        + jnp.where(lane8 == 2, jnp.sum(blue, axis=1, keepdims=True), 0.0)
+    )
+    image = color + jnp.exp(log_total) * bg_ref[...]
+    image_ref[...] = image
+    resid = image - target_ref[...]
+    dot_total = jnp.sum(image * resid, axis=1, keepdims=True)
+    resid_r, resid_g, resid_b = resid[:, 0:1], resid[:, 1:2], resid[:, 2:3]
+
+    def backward(i, prefix):
+        start, blk, live, dx, dy = geometry(i)
+        trans = trans_ref[:, pl.ds(start, KB)]
+        falloff = fall_ref[:, pl.ds(start, KB)]
+        alpha = jnp.where(live, blk[5:6] * falloff, 0.0)
+        weight = trans * alpha
+        along = resid_r * blk[8:9] + resid_g * blk[9:10] + resid_b * blk[10:11]
+        running = prefix + split_cumsum(weight * along, upper)
+        d_alpha = jnp.where(live, trans * along - (dot_total - running) / (1.0 - alpha), 0.0)
+        d_power = d_alpha * alpha
+        x_term = d_power * dx
+        y_term = d_power * dy
+        parts = [
+            x_term,
+            y_term,
+            x_term * dx,
+            x_term * dy,
+            y_term * dy,
+            d_alpha * falloff,
+            weight * resid_r,
+            weight * resid_g,
+            weight * resid_b,
+        ]
+        for r, part in enumerate(parts):
+            sums_ref[r : r + 1, pl.ds(start, KB)] += jnp.sum(part, axis=0, keepdims=True)
+        return running[:, KB - 1 : KB]
+
+    lax.fori_loop(0, blocks, backward, jnp.zeros((PIXELS, 1), jnp.float32))
 
 
 def render_tiles(entry16, counts, tiles, target8, bg8, tile_cols):
@@ -282,6 +307,10 @@
         out_shape=[
             jax.ShapeDtypeStruct((n, PIXELS, 8), jnp.float32),
             jax.ShapeDtypeStruct((n, 16, LIST), jnp.float32),
+        ],
+        scratch_shapes=[
+            pltpu.VMEM((PIXELS, LIST), jnp.float32),
+            pltpu.VMEM((PIXELS, LIST), jnp.float32),
         ],
     )(counts, tiles, entry16, target8, bg8)
 

time: 208 us -> 154 us (0.74)
  Pallas kernels: 48.3 us -> 21.8 us
  starting transfers between devices: 53.8 us -> 27.3 us
    all_to_all x1, starting transfers between devices: 31.5 us -> 4.99 us  [body(): lax.all_to_all(grad_send, 'tiles', split_axis=1, concat_axis=1, tiled=True)]
    pallas_call x1, Pallas kernels: 48.3 us -> 21.8 us  [render_tiles(): pl.pallas_call(partial(render_kernel, tile_cols=tile_cols), grid=(n,), in...]
  transfers between devices with their start and end apart: 3 -> 3, of which waited for: 2 -> 2; matrix products, arithmetic and copies ran while one was open for 7% -> 10% of each run, Pallas kernels for 0% -> 0%
where the time goes in v4:
time: 154 us; the launch traced here: 152 us
  other arithmetic  34.5 us (22%)
  local copies, waits for them, and re-layouts  30 us (19%)
  starting transfers between devices  27.3 us (18%)
  Pallas kernels  21.8 us (14%)
  waiting for transfers between devices  18 us (12%)
  blocking collectives  12.8 us (8%)
  matrix products  4.22 us (3%)
  between operations  3.17 us (2%)
    pallas_call x1, Pallas kernels, render_tiles(): pl.pallas_call(partial(render_kernel, tile_cols=tile_cols), grid=(n,), in...  21.8 us
    all_gather x1, blocking collectives, body(): lax.all_gather(payload.reshape(-1, 128), 'views', axis=0, tiled=False)  12.8 us
    all_to_all x1, starting transfers between devices, body(): lax.all_to_all(asked_for, 'tiles', split_axis=0, concat_axis=0, tiled=True)  12 us
    scatter-add x1, other arithmetic, body(): attr_grad = jnp.zeros((9, owned), jnp.float32).at[:, asked.reshape(-1)].a...  11.7 us
    all_to_all x1, starting transfers between devices, body(): lax.all_to_all(served, 'tiles', split_axis=1, concat_axis=1, tiled=True)  10.3 us
    all_to_all x1, waiting for transfers between devices, body(): lax.all_to_all(served, 'tiles', split_axis=1, concat_axis=1, tiled=True)  9.38 us
    all_to_all x1, waiting for transfers between devices, body(): lax.all_to_all(grad_send, 'tiles', split_axis=1, concat_axis=1, tiled=True)  8.61 us
    gather x2, local copies, waits for them, and re-layouts, body(): served = jnp.take(attrs, asked, axis=1)  5.93 us
  transfers between devices with their start and end apart: 3, of which 2 were waited for; matrix products, arithmetic and copies ran while one was open for 10% of the time, Pallas kernels for 0%

profile of v4, /device:TPU:2, one launch (start us, length us, event | category | flops | bytes accessed | tf_op | source)
XLA Modules:
  0.0 151.7 jit_solution(8197119844843774217)
XLA Ops:
  0.7 1.3 convert_reduce_fusion
  2.0 0.7 compare_select_fusion.3
  2.7 4.5 %scatter_custom_fusion = s32[2048]{0:T(1024)S(1)} fusion(s32[1024]{0:T(1024)S(1)} %bitcast.494, s32[1024]{0:T(1024)} %bitcast.501, s32[]{:T(128)} %constant.40.clone.1), kind=kCustom, calls=%fused_computation.358 | custom fusion | bytes 8704 | tf_op jit(solution)/shard_map/scatter | solution.py:360
  7.2 0.7 all_to_all.16
  7.8 12.0 %all-to-all-start = ((s32[64,1,32]{2,1,0:T(1,128)}), s32[64,1,32]{2,1,0:T(1,128)S(1)}, u32[]{:S(2)}, u32[]{:S(2)}) async-start(s32[64,1,32]{2,1,0:T(1,128)} %bitcast.7), calls=%async_computation | async-start | bytes 65536 | tf_op jit(solution)/shard_map/all_to_all | solution.py:363
  20.5 0.5 fusion.136
  21.2 0.6 broadcast_clamp_fusion.1
  21.7 1.5 %fusion.124 = (f32[4,2048]{1,0:T(4,128)}, f32[2048]{0:T(1024)S(1)}) fusion(f32[59,2048]{1,0:T(8,128)} %param.11), kind=kLoop, calls=%fused_computation.385 | loop fusion | flops 14336 | bytes 73728 | tf_op jit(solution)/shard_map/slice | solution.py:86
  23.3 1.0 slice.220
  24.3 0.6 constant_dynamic-update-slice_fusion.15
  25.3 0.9 multiply_reduce_fusion.6
  26.3 1.0 convolution_add_fusion.1
  27.4 0.6 multiply_divide_fusion.1
  28.0 1.0 fusion.125
  29.1 0.7 slice_multiply_fusion.18
  30.1 0.3 fusion.24
  30.6 0.2 copy.124
  30.8 0.8 pad_convert_fusion.target_ref
  31.9 0.2 stack.30
  32.3 0.6 broadcast_multiply_fusion.5
  32.9 0.5 pad_bitcast_fusion.bg_ref
  34.2 0.7 copy.137
  34.9 0.2 concatenate.9
  35.2 0.4 copy.120
  35.6 0.5 broadcast.899
  36.1 0.7 reduce.9
  37.0 5.5 %gather_fusion = f32[2048,9]{1,0:T(8,128)S(1)} fusion(f32[9,2048]{0,1:T(8,128)S(1)} %copy.120, s32[2048]{0:T(1024)S(1)} %broadcast_clamp_fusion), kind=kCustom, calls=%fused_computation | custom fusion | bytes 155648 | tf_op jit(solution)/shard_map/jit(_take)/gather | solution.py:364
  42.5 0.5 copy.121
  43.0 0.9 reshape.653
  43.9 10.3 %all-to-all-start.1 = ((f32[64,1,288]{2,1,0:T(1,128)}), f32[64,1,288]{2,1,0:T(1,128)S(1)}, u32[]{:S(2)}, u32[]{:S(2)}) async-start(f32[64,1,288]{2,1,0:T(1,128)} %reshape.653), calls=%async_computation.1 | async-start | bytes 196608 | tf_op jit(solution)/shard_map/all_to_all | solution.py:365
  54.2 9.4 %all-to-all-done.1 = f32[64,1,288]{2,1,0:T(1,128)S(1)} async-done(((f32[64,1,288]{2,1,0:T(1,128)}), f32[64,1,288]{2,1,0:T(1,128)S(1)}, u32[]{:S(2)}, u32[]{:S(2)}) %all-to-all-start.1) | async-done | bytes 73760 | tf_op jit(solution)/shard_map/all_to_all | solution.py:365
  63.6 0.6 broadcast.909
  64.2 0.9 reduce.10
  65.2 0.5 copy.122
  65.7 2.8 %gather_fusion.1 = f32[1024,9]{1,0:T(8,128)S(1)} fusion(f32[9,2048]{0,1:T(8,128)S(1)} %bitcast.443, s32[1024]{0:T(1024)S(1)} %copy-done.35), kind=kCustom, calls=%fused_computation.1 | custom fusion | bytes 77824 | tf_op jit(solution)/shard_map/gather | solution.py:366
  68.7 0.7 maximum_bitcast_fusion.entry_ref
  69.4 21.8 %shard_map.138 = (f32[1,1024,8]{2,1,0:T(8,128)}, f32[1,16,1024]{2,1,0:T(8,128)}) custom-call(s32[1]{0:T(128)} %bitcast.438.counts_ref, s32[1]{0:T(128)} %bitcast.1.tiles_ref, f32[1,16,1024]{2,1,0:T(8,128)} %maximum_bitcast_fusion.entry_ref, f32[1,1024,8]{2,1,0:T(8,128)} %pad_convert_fusion.target_ref, f32[1,8]{1,0:T(1,128)} %pad_bitcast_fusion.bg_ref), custom_call_target="tpu_custom_call" | custom-call | tf_op jit(solution)/shard_map/pallas_call | solution.py:293
  91.2 0.9 fusion.107
  92.0 1.0 slice_bitcast_fusion.8
  93.1 0.2 copy.125
  93.4 3.6 %scatter_custom_fusion.1 = f32[9,2048]{0,1:T(8,128)S(1)} fusion(s32[1024]{0:T(1024)} %bitcast.496, f32[1024,9]{1,0:T(8,128)S(1)} %copy.125, f32[]{:T(128)} %constant.48.clone.1), kind=kCustom, calls=%fused_computation.23 | custom fusion | bytes 74240 | tf_op jit(solution)/shard_map/scatter | solution.py:398
  97.0 0.5 copy.126
  97.4 0.9 reshape.655
  98.3 5.0 %all-to-all-start.2 = ((f32[64,1,288]{2,1,0:T(1,128)}), f32[64,1,288]{2,1,0:T(1,128)S(1)}, u32[]{:S(2)}, u32[]{:S(2)}) async-start(f32[64,1,288]{2,1,0:T(1,128)} %reshape.655), calls=%async_computation.2 | async-start | bytes 196608 | tf_op jit(solution)/shard_map/all_to_all | solution.py:401
  103.4 0.7 copy.142
  104.1 8.6 %all-to-all-done.2 = f32[64,1,288]{2,1,0:T(1,128)S(1)} async-done(((f32[64,1,288]{2,1,0:T(1,128)}), f32[64,1,288]{2,1,0:T(1,128)S(1)}, u32[]{:S(2)}, u32[]{:S(2)}) %all-to-all-start.2) | async-done | bytes 73760 | tf_op jit(solution)/shard_map/all_to_all | solution.py:401
  112.7 0.9 reduce.11
  114.0 0.4 copy.128
  114.4 11.7 %scatter_custom_fusion.2 = f32[9,2048]{0,1:T(8,128)S(1)} fusion(s32[2048]{0:T(1024)S(1)} %bitcast.497, f32[2048,9]{1,0:T(8,128)S(1)} %copy.128, f32[]{:T(128)} %constant.48.clone.1), kind=kCustom, calls=%fused_computation.21 | custom fusion | flops 18432 | bytes 73732 | tf_op jit(solution)/shard_map/scatter-add | solution.py:405
  126.1 0.3 copy.129
  126.5 12.8 %all_gather.3 = f32[4,145,128]{2,1,0:T(8,128)S(1)} all-gather(f32[1,145,128]{2,1,0:T(8,128)S(1)} %fusion.26), channel_id=1, replica_groups=mesh['tiles'=64,'views'=4] {'views'}, dimensions={0}, use_global_device_ids=true | all-gather | bytes 371200 | tf_op jit(solution)/shard_map/all_gather | solution.py:408
  139.6 0.3 convolution_add_fusion
  140.0 0.5 fusion.21
  140.9 0.3 copy-done.6
  141.4 1.4 multiply_reduce_fusion.2
  142.7 0.2 copy_multiply_fusion
  143.0 0.7 add_divide_fusion
  143.7 0.7 fusion.35
  144.3 0.7 fusion.30
  145.0 0.7 fusion.31
  146.6 0.7 broadcast_multiply_fusion
  148.2 0.4 fusion.10
  149.4 0.9 add_reduce_fusion
  150.3 1.3 divide_subtract_fusion
  (184 shorter events, 5.8 us)
Async XLA Ops:
  0.6 19.9 %copy-start = (f32[16,12]{1,0:T(8,128)S(1)}, f32[16,12]{1,0:T(8,128)}, u32[]{:S(2)}) copy-start(f32[16,12]{1,0:T(8,128)} %param.15) | copy-start | bytes 2308
  0.6 28.5 %copy-start.1 = (f32[59,2048]{1,0:T(8,128)S(1)}, f32[59,2048]{1,0:T(8,128)}, u32[]{:S(2)}) copy-start(f32[59,2048]{1,0:T(8,128)} %param.11) | copy-start | bytes 1449988
  1.9 28.7 %copy-start.37 = (bf16[1,1,3,1024]{3,2,1,0:T(4,128)(2,1)S(1)}, bf16[1,1,3,1024]{3,2,1,0:T(4,128)(2,1)}, u32[]{:S(2)}) copy-start(bf16[1,1,3,1024]{3,2,1,0:T(4,128)(2,1)} %param.20) | copy-start | bytes 18436
  2.7 22.4 %copy-start.36 = (s32[1024,1]{0,1:T(1,128)}, s32[1024,1]{0,1:T(1,128)S(1)}, u32[]{:S(2)}) copy-start(s32[1024,1]{0,1:T(1,128)S(1)} %compare_select_fusion.3) | copy-start | bytes 12292
  7.8 27.7 %all-to-all-start = ((s32[64,1,32]{2,1,0:T(1,128)}), s32[64,1,32]{2,1,0:T(1,128)S(1)}, u32[]{:S(2)}, u32[]{:S(2)}) async-start(s32[64,1,32]{2,1,0:T(1,128)} %bitcast.7), calls=%async_computation | async-start | bytes 65536 | tf_op jit(solution)/shard_map/all_to_all | solution.py:363
  29.8 2.4 %copy-start.13 = (f32[1,2048]{1,0:T(1,128)}, f32[1,2048]{1,0:T(1,128)S(1)}, u32[]{:S(2)}) copy-start(f32[1,2048]{1,0:T(1,128)S(1)} %get-tuple-element.63) | copy-start | bytes 24580
  29.8 2.4 %copy-start.16 = (f32[1,2048]{1,0:T(1,128)}, f32[1,2048]{1,0:T(1,128)S(1)}, u32[]{:S(2)}) copy-start(f32[1,2048]{1,0:T(1,128)S(1)} %get-tuple-element.64) | copy-start | bytes 24580
  29.8 2.4 %copy-start.19 = (f32[1,2048]{1,0:T(1,128)}, f32[1,2048]{1,0:T(1,128)S(1)}, u32[]{:S(2)}) copy-start(f32[1,2048]{1,0:T(1,128)S(1)} %get-tuple-element.65) | copy-start | bytes 24580
  30.6 2.3 %copy-start.42 = (f32[3]{0:T(128)S(1)}, f32[3]{0:T(128)}, u32[]{:S(2)}) copy-start(f32[3]{0:T(128)} %param.21) | copy-start | bytes 40
  43.0 22.6 %copy-start.35 = (s32[1024]{0:T(1024)S(1)}, s32[1024]{0:T(1024)}, u32[]{:S(2)}) copy-start(s32[1024]{0:T(1024)} %broadcast_clamp_fusion.1) | copy-start | bytes 12292
  43.9 19.7 %all-to-all-start.1 = ((f32[64,1,288]{2,1,0:T(1,128)}), f32[64,1,288]{2,1,0:T(1,128)S(1)}, u32[]{:S(2)}, u32[]{:S(2)}) async-start(f32[64,1,288]{2,1,0:T(1,128)} %reshape.653), calls=%async_computation.1 | async-start | bytes 196608 | tf_op jit(solution)/shard_map/all_to_all | solution.py:365
  93.3 10.0 %copy-start.24 = (f32[1,1024,8]{2,1,0:T(8,128)S(1)}, f32[1,1024,8]{2,1,0:T(8,128)}, u32[]{:S(2)}) copy-start(f32[1,1024,8]{2,1,0:T(8,128)} %get-tuple-element.6) | copy-start | bytes 98308
  98.3 14.4 %all-to-all-start.2 = ((f32[64,1,288]{2,1,0:T(1,128)}), f32[64,1,288]{2,1,0:T(1,128)S(1)}, u32[]{:S(2)}, u32[]{:S(2)}) async-start(f32[64,1,288]{2,1,0:T(1,128)} %reshape.655), calls=%async_computation.2 | async-start | bytes 196608 | tf_op jit(solution)/shard_map/all_to_all | solution.py:401
  114.0 12.5 %copy-start.40 = (f32[12]{0:T(128)S(1)}, f32[12]{0:T(128)}, u32[]{:S(2)}) copy-start(f32[12]{0:T(128)} %fusion.136) | copy-start | bytes 148
  139.4 1.0 copy-start.38
  139.6 1.7 %copy-start.10 = (f32[4,3,3]{2,1,0:T(4,128)}, f32[4,3,3]{2,1,0:T(4,128)S(1)}, u32[]{:S(2)}) copy-start(f32[4,3,3]{2,1,0:T(4,128)S(1)} %reshape.574) | copy-start | bytes 436
  140.5 0.9 copy-start.5
  140.6 0.6 copy-start.6
  140.9 2.1 %copy-start.14 = (f32[1,2048]{1,0:T(1,128)S(1)}, f32[1,2048]{1,0:T(1,128)}, u32[]{:S(2)}) copy-start(f32[1,2048]{1,0:T(1,128)} %copy-done.13) | copy-start | bytes 24580
  140.9 2.1 %copy-start.17 = (f32[1,2048]{1,0:T(1,128)S(1)}, f32[1,2048]{1,0:T(1,128)}, u32[]{:S(2)}) copy-start(f32[1,2048]{1,0:T(1,128)} %copy-done.16) | copy-start | bytes 24580
  140.9 2.1 %copy-start.20 = (f32[1,2048]{1,0:T(1,128)S(1)}, f32[1,2048]{1,0:T(1,128)}, u32[]{:S(2)}) copy-start(f32[1,2048]{1,0:T(1,128)} %copy-done.19) | copy-start | bytes 24580
  141.3 2.4 %copy-start.8 = (f32[2048]{0:T(1024)S(1)}, f32[2048]{0:T(1024)}, u32[]{:S(2)}) copy-start(f32[2048]{0:T(1024)} %get-tuple-element.162) | copy-start | bytes 24580
  142.7 3.0 %copy-start.11 = (f32[4,3,3]{2,1,0:T(4,128)S(1)}, f32[4,3,3]{2,1,0:T(4,128)}, u32[]{:S(2)}) copy-start(f32[4,3,3]{2,1,0:T(4,128)} %copy-done.10) | copy-start | bytes 436
  142.7 3.0 %copy-start.39 = (f32[4,3]{1,0:T(4,128)S(1)}, f32[4,3]{1,0:T(4,128)}, u32[]{:S(2)}) copy-start(f32[4,3]{1,0:T(4,128)} %copy-done.38) | copy-start | bytes 148
  142.7 3.5 %copy-start.2 = (f32[4,16,2048]{2,0,1:T(4,128)S(1)}, f32[4,16,2048]{2,0,1:T(4,128)}, u32[]{:S(2)}) copy-start(f32[4,16,2048]{2,0,1:T(4,128)} %constant_dynamic-update-slice_fusion.15) | copy-start | bytes 1572868
  146.6 1.2 copy-start.7
  147.3 0.7 copy-start.34
  147.3 0.8 copy-start.12
  147.6 1.4 copy-start.9
  147.6 1.4 copy-start.15
  147.6 1.4 copy-start.18
  147.6 1.4 copy-start.21
  147.6 1.4 copy-start.28
  147.6 1.4 copy-start.29
  147.6 1.4 copy-start.30
  147.7 1.4 copy-start.31
  147.7 1.4 copy-start.32
  147.7 1.4 copy-start.33
  147.8 1.5 copy-start.22
  147.8 1.5 copy-start.23
  147.8 1.5 copy-start.25
  147.9 1.5 copy-start.26
  147.9 1.5 copy-start.27
  149.1 1.2 copy-start.3
  149.1 1.2 copy-start.4
  149.1 1.2 copy-start.41

commit v5 on v4

--- a/solution.py
+++ b/solution.py
@@ -361,7 +361,10 @@
         .reshape(peers, capacity)
     )
     asked = lax.all_to_all(asked_for, "tiles", split_axis=0, concat_axis=0, tiled=True)
-    served = jnp.take(attrs, asked, axis=1)
+    chosen = (asked.reshape(-1)[:, None] == jnp.arange(owned)[None, :]).astype(jnp.float32)
+    served = lax.dot_general(
+        attrs, chosen, (((1,), (1,)), ((), ())), precision=precise
+    ).reshape(9, peers, capacity)
     returned = lax.all_to_all(served, "tiles", split_axis=1, concat_axis=1, tiled=True)
     entry_attrs = returned.reshape(9, peers * capacity)[:, slot].reshape(9, tiles_here, LIST)
     first_tile = lax.axis_index("tiles") * tiles_here
@@ -399,11 +402,7 @@
         .reshape(9, peers, capacity)
     )
     grad_back = lax.all_to_all(grad_send, "tiles", split_axis=1, concat_axis=1, tiled=True)
-    attr_grad = (
-        jnp.zeros((9, owned), jnp.float32)
-        .at[:, asked.reshape(-1)]
-        .add(grad_back.reshape(9, peers * capacity))
-    )
+    attr_grad = jnp.dot(grad_back.reshape(9, peers * capacity), chosen, precision=precise)
     payload = jnp.concatenate([attr_grad.reshape(-1), jnp.pad(camera, (0, 128 - 12))])
     gathered = lax.all_gather(payload.reshape(-1, 128), "views", axis=0, tiled=False)
     gathered = gathered.reshape(gathered.shape[0], -1)

time: 154 us -> 141 us (0.916)
  Pallas kernels: 21.8 us -> 5.59 us
  starting transfers between devices: 27.3 us -> 43.3 us
  other arithmetic: 34.5 us -> 19.5 us
  matrix products: 4.22 us -> 17.1 us
  local copies, waits for them, and re-layouts: 30 us -> 22.8 us
  waiting for transfers between devices: 18 us -> 13.8 us
    pallas_call x1, Pallas kernels: 21.8 us -> 5.59 us  [render_tiles(): pl.pallas_call(partial(render_kernel, tile_cols=tile_cols), grid=(n,), in...]
    all_to_all x1, starting transfers between devices: 4.99 us -> 21 us  [body(): lax.all_to_all(grad_send, 'tiles', split_axis=1, concat_axis=1, tiled=True)]
    dot_general x0 -> x2, matrix products: none -> 12.9 us  [the longest x1 7.58 us: body(): lax.dot_general(attrs, chosen, (((1,), (1,)), ((), ())), precision=precise)]
    scatter-add x1 -> x0, other arithmetic: 11.7 us -> none  [body(): attr_grad = jnp.zeros((9, owned), jnp.float32).at[:, asked.reshape(-1)].a...]
    gather x2 -> x0, local copies, waits for them, and re-layouts: 5.93 us -> none  [body(): served = jnp.take(attrs, asked, axis=1)]
    all_to_all x1, waiting for transfers between devices: 9.38 us -> 6.26 us  [body(): lax.all_to_all(served, 'tiles', split_axis=1, concat_axis=1, tiled=True)]
    unnamed x94 -> x62, local copies, waits for them, and re-layouts: 4.19 us -> 3.54 us
  transfers between devices with their start and end apart: 3 -> 3, of which waited for: 2 -> 2; matrix products, arithmetic and copies ran while one was open for 10% -> 9% of each run, Pallas kernels for 0% -> 0%
where the time goes in v5:
time: 141 us; the launch traced here: 139 us
  starting transfers between devices  43.3 us (31%)
  local copies, waits for them, and re-layouts  22.8 us (16%)
  other arithmetic  19.5 us (14%)
  matrix products  17.1 us (12%)
  waiting for transfers between devices  13.8 us (10%)
  blocking collectives  13.8 us (10%)
  Pallas kernels  5.59 us (4%)
  between operations  2.96 us (2%)
    all_to_all x1, starting transfers between devices, body(): lax.all_to_all(grad_send, 'tiles', split_axis=1, concat_axis=1, tiled=True)  21 us
    all_gather x1, blocking collectives, body(): lax.all_gather(payload.reshape(-1, 128), 'views', axis=0, tiled=False)  13.8 us
    all_to_all x1, starting transfers between devices, body(): lax.all_to_all(asked_for, 'tiles', split_axis=0, concat_axis=0, tiled=True)  12 us
    all_to_all x1, starting transfers between devices, body(): lax.all_to_all(served, 'tiles', split_axis=1, concat_axis=1, tiled=True)  10.3 us
    dot_general x1, matrix products, body(): lax.dot_general(attrs, chosen, (((1,), (1,)), ((), ())), precision=precise)  7.58 us
    all_to_all x1, waiting for transfers between devices, body(): lax.all_to_all(grad_send, 'tiles', split_axis=1, concat_axis=1, tiled=True)  7.58 us
    all_to_all x1, waiting for transfers between devices, body(): lax.all_to_all(served, 'tiles', split_axis=1, concat_axis=1, tiled=True)  6.26 us
    pallas_call x1, Pallas kernels, render_tiles(): pl.pallas_call(partial(render_kernel, tile_cols=tile_cols), grid=(n,), in...  5.59 us
  transfers between devices with their start and end apart: 3, of which 2 were waited for; matrix products, arithmetic and copies ran while one was open for 9% of the time, Pallas kernels for 0%

profile of v5, /device:TPU:2, one launch (start us, length us, event | category | flops | bytes accessed | tf_op | source)
XLA Modules:
  0.0 139.0 jit_solution(15379478799557556185)
XLA Ops:
  0.7 1.3 convert_reduce_fusion
  1.9 0.7 compare_select_fusion
  2.6 4.5 %scatter_custom_fusion = s32[2048]{0:T(1024)S(1)} fusion(s32[1024]{0:T(1024)S(1)} %bitcast.483, s32[1024]{0:T(1024)} %bitcast.489, s32[]{:T(128)} %constant.38.clone.1), kind=kCustom, calls=%fused_computation.343 | custom fusion | bytes 8704 | tf_op jit(solution)/shard_map/scatter | solution.py:360
  7.1 0.7 all_to_all.12
  7.8 12.0 %all-to-all-start = ((s32[64,1,32]{2,1,0:T(1,128)}), s32[64,1,32]{2,1,0:T(1,128)S(1)}, u32[]{:S(2)}, u32[]{:S(2)}) async-start(s32[64,1,32]{2,1,0:T(1,128)} %bitcast.25), calls=%async_computation | async-start | bytes 65536 | tf_op jit(solution)/shard_map/all_to_all | solution.py:363
  20.6 1.5 %fusion.126 = (f32[4,2048]{1,0:T(4,128)}, f32[2048]{0:T(1024)S(1)}) fusion(f32[59,2048]{1,0:T(8,128)} %param.11), kind=kLoop, calls=%fused_computation.380 | loop fusion | flops 14336 | bytes 73728 | tf_op jit(solution)/shard_map/slice | solution.py:86
  22.1 1.0 slice.220
  23.4 0.2 fusion.5
  23.6 0.9 multiply_reduce_fusion.6
  24.5 1.0 convolution_add_fusion.1
  25.6 1.0 fusion.127
  27.2 0.3 fusion.26
  27.7 0.2 reshape.505
  27.9 0.2 stack.30
  28.1 0.2 multiply_reduce_fusion.1
  28.3 0.6 broadcast_multiply_fusion.5
  29.0 0.2 concatenate.9
  29.2 0.5 broadcast.834
  29.7 0.7 reduce.9
  30.5 7.6 %fusion.1 = f32[9,2048]{1,0:T(8,128)S(1)} fusion(f32[9,2048]{1,0:T(8,128)S(1)} %concatenate.9, s32[2048]{0:T(1024)S(1)} %eq.34), kind=kOutput, calls=%fused_computation.5 | convolution fusion | flops 457179136 | bytes 155648 | tf_op jit(solution)/shard_map/dot_general | solution.py:365
  38.2 0.2 copy.190
  38.4 0.9 reshape.573
  39.3 10.3 %all-to-all-start.1 = ((f32[64,1,288]{2,1,0:T(1,128)}), f32[64,1,288]{2,1,0:T(1,128)S(1)}, u32[]{:S(2)}, u32[]{:S(2)}) async-start(f32[64,1,288]{2,1,0:T(1,128)} %reshape.573), calls=%async_computation.1 | async-start | bytes 196608 | tf_op jit(solution)/shard_map/all_to_all | solution.py:368
  49.6 0.6 pad_bitcast_fusion.bg_ref
  51.0 0.7 copy.118
  51.7 0.2 copy.107
  51.9 0.8 pad_convert_fusion.target_ref
  52.7 6.3 %all-to-all-done.1 = f32[64,1,288]{2,1,0:T(1,128)S(1)} async-done(((f32[64,1,288]{2,1,0:T(1,128)}), f32[64,1,288]{2,1,0:T(1,128)S(1)}, u32[]{:S(2)}, u32[]{:S(2)}) %all-to-all-start.1) | async-done | bytes 73760 | tf_op jit(solution)/shard_map/all_to_all | solution.py:368
  59.0 0.5 broadcast.840
  59.5 0.8 reduce.10
  60.4 0.5 copy.105
  60.9 2.8 %gather_fusion = f32[1024,9]{1,0:T(8,128)S(1)} fusion(f32[9,2048]{0,1:T(8,128)S(1)} %bitcast.435, s32[1024]{0:T(1024)S(1)} %broadcast_clamp_fusion), kind=kCustom, calls=%fused_computation | custom fusion | bytes 77824 | tf_op jit(solution)/shard_map/gather | solution.py:369
  63.7 0.2 copy.106
  63.9 0.7 maximum_bitcast_fusion.entry_ref
  64.6 5.6 %shard_map.138 = (f32[1,1024,8]{2,1,0:T(8,128)}, f32[1,16,1024]{2,1,0:T(8,128)}) custom-call(s32[1]{0:T(128)} %bitcast.430.counts_ref, s32[1]{0:T(128)} %bitcast.1.tiles_ref, f32[1,16,1024]{2,1,0:T(8,128)} %maximum_bitcast_fusion.entry_ref, f32[1,1024,8]{2,1,0:T(8,128)} %pad_convert_fusion.target_ref, f32[1,8]{1,0:T(1,128)} %pad_bitcast_fusion.bg_ref), custom_call_target="tpu_custom_call" | custom-call | tf_op jit(solution)/shard_map/pallas_call | solution.py:293
  70.2 0.9 fusion.109
  71.1 1.1 slice_bitcast_fusion.8
  72.2 0.2 copy.108
  72.4 3.3 %scatter_custom_fusion.1 = f32[9,2048]{0,1:T(8,128)S(1)} fusion(s32[1024]{0:T(1024)S(1)} %bitcast.485, f32[1024,9]{1,0:T(8,128)S(1)} %copy.108, f32[]{:T(128)} %constant.43.clone.1), kind=kCustom, calls=%fused_computation.23 | custom fusion | bytes 73732 | tf_op jit(solution)/shard_map/scatter | solution.py:401
  75.8 0.5 copy.109
  76.2 0.9 reshape.575
  77.1 21.0 %all-to-all-start.2 = ((f32[64,1,288]{2,1,0:T(1,128)}), f32[64,1,288]{2,1,0:T(1,128)S(1)}, u32[]{:S(2)}, u32[]{:S(2)}) async-start(f32[64,1,288]{2,1,0:T(1,128)} %reshape.575), calls=%async_computation.2 | async-start | bytes 196608 | tf_op jit(solution)/shard_map/all_to_all | solution.py:404
  98.1 1.1 fusion.11
  99.2 0.7 copy.123
  99.9 7.6 %all-to-all-done.2 = f32[64,1,288]{2,1,0:T(1,128)S(1)} async-done(((f32[64,1,288]{2,1,0:T(1,128)}), f32[64,1,288]{2,1,0:T(1,128)S(1)}, u32[]{:S(2)}, u32[]{:S(2)}) %all-to-all-start.2) | async-done | bytes 73760 | tf_op jit(solution)/shard_map/all_to_all | solution.py:404
  107.5 0.8 reduce.11
  108.5 0.2 reshape.510
  108.7 5.4 %fusion = f32[9,2048]{1,0:T(8,128)S(1)} fusion(f32[9,2048]{1,0:T(8,128)S(1)} %reshape.510, s32[2048]{0:T(1024)S(1)} %eq.34), kind=kOutput, calls=%fused_computation.4 | convolution fusion | flops 457179136 | bytes 155648 | tf_op jit(solution)/shard_map/dot_general | solution.py:405
  114.1 13.8 %all_gather.3 = f32[4,145,128]{2,1,0:T(8,128)S(1)} all-gather(f32[1,145,128]{2,1,0:T(8,128)S(1)} %fusion.28), channel_id=1, replica_groups=mesh['tiles'=64,'views'=4] {'views'}, dimensions={0}, use_global_device_ids=true | all-gather | bytes 371200 | tf_op jit(solution)/shard_map/all_gather | solution.py:407
  128.2 0.3 convolution_add_fusion
  128.6 0.5 fusion.23
  129.1 0.8 multiply_reduce_fusion.5
  130.3 0.4 copy-done.11
  130.7 1.3 multiply_reduce_fusion.2
  132.0 0.2 copy_multiply_fusion
  132.3 0.7 add_divide_fusion
  133.2 0.2 fusion.131
  134.1 0.7 broadcast_multiply_fusion
  134.8 0.1 add_add_fusion.5
  135.3 0.2 fusion.20
  135.6 0.4 fusion.12
  136.4 0.2 fusion.49
  136.7 0.9 add_reduce_fusion
  137.6 1.3 divide_subtract_fusion
  (144 shorter events, 4.3 us)
Async XLA Ops:
  0.6 19.9 %copy-start = (f32[16,12]{1,0:T(8,128)S(1)}, f32[16,12]{1,0:T(8,128)}, u32[]{:S(2)}) copy-start(f32[16,12]{1,0:T(8,128)} %param.15) | copy-start | bytes 2308
  0.6 26.1 %copy-start.1 = (f32[59,2048]{1,0:T(8,128)S(1)}, f32[59,2048]{1,0:T(8,128)}, u32[]{:S(2)}) copy-start(f32[59,2048]{1,0:T(8,128)} %param.11) | copy-start | bytes 1449988
  7.8 21.4 %all-to-all-start = ((s32[64,1,32]{2,1,0:T(1,128)}), s32[64,1,32]{2,1,0:T(1,128)S(1)}, u32[]{:S(2)}, u32[]{:S(2)}) async-start(s32[64,1,32]{2,1,0:T(1,128)} %bitcast.25), calls=%async_computation | async-start | bytes 65536 | tf_op jit(solution)/shard_map/all_to_all | solution.py:363
  26.9 1.4 copy-start.13
  26.9 1.4 copy-start.16
  26.9 1.4 %copy-start.19 = (f32[1,2048]{1,0:T(1,128)}, f32[1,2048]{1,0:T(1,128)S(1)}, u32[]{:S(2)}) copy-start(f32[1,2048]{1,0:T(1,128)S(1)} %get-tuple-element.65) | copy-start | bytes 24580
  38.1 11.5 %copy-start.26 = (f32[3]{0:T(128)S(1)}, f32[3]{0:T(128)}, u32[]{:S(2)}) copy-start(f32[3]{0:T(128)} %param.21) | copy-start | bytes 40
  38.1 13.6 %copy-start.24 = (bf16[1,1,3,1024]{3,2,1,0:T(4,128)(2,1)S(1)}, bf16[1,1,3,1024]{3,2,1,0:T(4,128)(2,1)}, u32[]{:S(2)}) copy-start(bf16[1,1,3,1024]{3,2,1,0:T(4,128)(2,1)} %param.20) | copy-start | bytes 18436
  39.3 19.7 %all-to-all-start.1 = ((f32[64,1,288]{2,1,0:T(1,128)}), f32[64,1,288]{2,1,0:T(1,128)S(1)}, u32[]{:S(2)}, u32[]{:S(2)}) async-start(f32[64,1,288]{2,1,0:T(1,128)} %reshape.573), calls=%async_computation.1 | async-start | bytes 196608 | tf_op jit(solution)/shard_map/all_to_all | solution.py:368
  77.1 30.4 %all-to-all-start.2 = ((f32[64,1,288]{2,1,0:T(1,128)}), f32[64,1,288]{2,1,0:T(1,128)S(1)}, u32[]{:S(2)}, u32[]{:S(2)}) async-start(f32[64,1,288]{2,1,0:T(1,128)} %reshape.575), calls=%async_computation.2 | async-start | bytes 196608 | tf_op jit(solution)/shard_map/all_to_all | solution.py:404
  128.2 1.7 %copy-start.10 = (f32[4,3,3]{2,1,0:T(4,128)}, f32[4,3,3]{2,1,0:T(4,128)S(1)}, u32[]{:S(2)}) copy-start(f32[4,3,3]{2,1,0:T(4,128)S(1)} %reshape.513) | copy-start | bytes 436
  129.0 1.2 copy-start.5
  129.9 2.1 %copy-start.6 = (f32[4,2048]{1,0:T(4,128)}, f32[4,2048]{1,0:T(4,128)S(1)}, u32[]{:S(2)}) copy-start(f32[4,2048]{1,0:T(4,128)S(1)} %get-tuple-element.48) | copy-start | bytes 98308
  130.0 0.7 copy-start.11
  130.2 2.1 %copy-start.14 = (f32[1,2048]{1,0:T(1,128)S(1)}, f32[1,2048]{1,0:T(1,128)}, u32[]{:S(2)}) copy-start(f32[1,2048]{1,0:T(1,128)} %copy-done.13) | copy-start | bytes 24580
  130.2 2.1 %copy-start.17 = (f32[1,2048]{1,0:T(1,128)S(1)}, f32[1,2048]{1,0:T(1,128)}, u32[]{:S(2)}) copy-start(f32[1,2048]{1,0:T(1,128)} %copy-done.16) | copy-start | bytes 24580
  130.2 2.1 %copy-start.20 = (f32[1,2048]{1,0:T(1,128)S(1)}, f32[1,2048]{1,0:T(1,128)}, u32[]{:S(2)}) copy-start(f32[1,2048]{1,0:T(1,128)} %copy-done.19) | copy-start | bytes 24580
  130.2 2.8 %copy-start.8 = (f32[2048]{0:T(1024)S(1)}, f32[2048]{0:T(1024)}, u32[]{:S(2)}) copy-start(f32[2048]{0:T(1024)} %get-tuple-element.163) | copy-start | bytes 24580
  134.1 1.1 copy-start.4
  134.1 1.1 copy-start.7
  134.8 0.8 copy-start.12
  135.1 1.3 copy-start.9
  135.1 1.3 copy-start.15
  135.1 1.3 copy-start.18
  135.1 1.3 copy-start.21
  135.2 1.4 %copy-start.22 = (f32[4,1,2048]{2,0,1:T(4,128)S(1)}, f32[4,1,2048]{2,0,1:T(4,128)}, u32[]{:S(2)}) copy-start(f32[4,1,2048]{2,0,1:T(4,128)} %add_divide_fusion) | copy-start | bytes 98308
  135.3 1.4 copy-start.23
  136.4 1.2 copy-start.2
  136.4 1.2 copy-start.3
  136.4 1.2 copy-start.25

commit v6 on v5

--- a/solution.py
+++ b/solution.py
@@ -313,6 +313,19 @@
             pltpu.VMEM((PIXELS, LIST), jnp.float32),
         ],
     )(counts, tiles, entry16, target8, bg8)
+
+
+def select_rows(values, chosen, contract):
+    high = lax.reduce_precision(values, exponent_bits=8, mantissa_bits=7)
+    rest = values - high
+    middle = lax.reduce_precision(rest, exponent_bits=8, mantissa_bits=7)
+    low = rest - middle
+    pieces = jnp.concatenate([high, middle, low], axis=0).astype(jnp.bfloat16)
+    out = lax.dot_general(
+        pieces, chosen, (((1,), (contract,)), ((), ())), preferred_element_type=jnp.float32
+    )
+    rows = values.shape[0]
+    return (out[:rows] + out[rows : 2 * rows]) + out[2 * rows :]
 
 
 def adam_step(values, first, second, grad, rates):
@@ -354,19 +367,19 @@
     same = owner_flat[:, None] == owner_flat[None, :]
     rank = jnp.sum((same & earlier).astype(jnp.int32), axis=1)
     slot = owner_flat * capacity + rank
+    placed = (slot[:, None] == jnp.arange(peers * capacity)[None, :]).astype(jnp.bfloat16)
     asked_for = (
-        jnp.zeros((peers * capacity,), jnp.int32)
-        .at[slot]
-        .set(index_flat, unique_indices=True)
+        jnp.round(select_rows(index_flat.astype(jnp.float32)[None], placed, 0))
+        .astype(jnp.int32)
         .reshape(peers, capacity)
     )
     asked = lax.all_to_all(asked_for, "tiles", split_axis=0, concat_axis=0, tiled=True)
-    chosen = (asked.reshape(-1)[:, None] == jnp.arange(owned)[None, :]).astype(jnp.float32)
-    served = lax.dot_general(
-        attrs, chosen, (((1,), (1,)), ((), ())), precision=precise
-    ).reshape(9, peers, capacity)
+    chosen = (asked.reshape(-1)[:, None] == jnp.arange(owned)[None, :]).astype(jnp.bfloat16)
+    served = select_rows(attrs, chosen, 1).reshape(9, peers, capacity)
     returned = lax.all_to_all(served, "tiles", split_axis=1, concat_axis=1, tiled=True)
-    entry_attrs = returned.reshape(9, peers * capacity)[:, slot].reshape(9, tiles_here, LIST)
+    entry_attrs = select_rows(returned.reshape(9, peers * capacity), placed, 1).reshape(
+        9, tiles_here, LIST
+    )
     first_tile = lax.axis_index("tiles") * tiles_here
 
     colors_pad = jnp.zeros((5, tiles_here, LIST), jnp.float32)
@@ -395,14 +408,9 @@
             sums[8],
         ]
     )
-    grad_send = (
-        jnp.zeros((9, peers * capacity), jnp.float32)
-        .at[:, slot]
-        .set(flat_grads, unique_indices=True)
-        .reshape(9, peers, capacity)
-    )
+    grad_send = select_rows(flat_grads, placed, 0).reshape(9, peers, capacity)
     grad_back = lax.all_to_all(grad_send, "tiles", split_axis=1, concat_axis=1, tiled=True)
-    attr_grad = jnp.dot(grad_back.reshape(9, peers * capacity), chosen, precision=precise)
+    attr_grad = select_rows(grad_back.reshape(9, peers * capacity), chosen, 0)
     payload = jnp.concatenate([attr_grad.reshape(-1), jnp.pad(camera, (0, 128 - 12))])
     gathered = lax.all_gather(payload.reshape(-1, 128), "views", axis=0, tiled=False)
     gathered = gathered.reshape(gathered.shape[0], -1)

time: 141 us -> 121 us (0.86)
  local copies, waits for them, and re-layouts: 22.8 us -> 8.2 us
  starting transfers between devices: 43.3 us -> 33.6 us
  waiting for transfers between devices: 13.8 us -> 20.4 us
  Pallas kernels: 5.59 us -> 10.2 us
  other arithmetic: 19.5 us -> 15.4 us
  matrix products: 17.1 us -> 15.4 us
    scatter x2 -> x0, local copies, waits for them, and re-layouts: 7.82 us -> none  [the longest x1 4.48 us: body(): asked_for = jnp.zeros((peers * capacity,), jnp.int32).at[slot].set(index_...]
    all_to_all x1, starting transfers between devices: 21 us -> 16 us  [body(): lax.all_to_all(grad_send, 'tiles', split_axis=1, concat_axis=1, tiled=True)]
    all_to_all x1, waiting for transfers between devices: 0.01 us -> 4.91 us  [body(): lax.all_to_all(asked_for, 'tiles', split_axis=0, concat_axis=0, tiled=True)]
    all_to_all x1, starting transfers between devices: 10.3 us -> 5.52 us  [body(): lax.all_to_all(served, 'tiles', split_axis=1, concat_axis=1, tiled=True)]
    pallas_call x1, Pallas kernels: 5.59 us -> 10.2 us  [render_tiles(): pl.pallas_call(partial(render_kernel, tile_cols=tile_cols), grid=(n,), in...]
    gather x2 -> x0, local copies, waits for them, and re-layouts: 2.99 us -> none  [body(): returned.reshape(9, peers * capacity)[:, slot].reshape(9, tiles_here, LIST)]
    slice x1, other arithmetic: 1.51 us -> 0.03 us  [project(): local_axes = quat_rotation(params[6:10]) * scales[None, :, :]]
    dot_general x2 -> x5, matrix products: 12.9 us -> 12 us  [select_rows(): lax.dot_general(pieces, chosen, (((1,), (contract,)), ((), ())), preferre...]
  transfers between devices with their start and end apart: 3 -> 3, of which waited for: 2 -> 3; matrix products, arithmetic and copies ran while one was open for 9% -> 4% of each run, Pallas kernels for 0% -> 0%
where the time goes in v6:
time: 121 us; the launch traced here: 119 us
  starting transfers between devices  33.6 us (28%)
  waiting for transfers between devices  20.4 us (17%)
  other arithmetic  15.4 us (13%)
  matrix products  15.4 us (13%)
  blocking collectives  13 us (11%)
  Pallas kernels  10.2 us (8%)
  local copies, waits for them, and re-layouts  8.2 us (7%)
  between operations  2.76 us (2%)
    all_to_all x1, starting transfers between devices, body(): lax.all_to_all(grad_send, 'tiles', split_axis=1, concat_axis=1, tiled=True)  16 us
    all_gather x1, blocking collectives, body(): lax.all_gather(payload.reshape(-1, 128), 'views', axis=0, tiled=False)  13 us
    dot_general x5, matrix products, select_rows(): lax.dot_general(pieces, chosen, (((1,), (contract,)), ((), ())), preferre...  12 us
    all_to_all x1, starting transfers between devices, body(): lax.all_to_all(asked_for, 'tiles', split_axis=0, concat_axis=0, tiled=True)  12 us
    pallas_call x1, Pallas kernels, render_tiles(): pl.pallas_call(partial(render_kernel, tile_cols=tile_cols), grid=(n,), in...  10.2 us
    all_to_all x1, waiting for transfers between devices, body(): lax.all_to_all(grad_send, 'tiles', split_axis=1, concat_axis=1, tiled=True)  8.61 us
    all_to_all x1, waiting for transfers between devices, body(): lax.all_to_all(served, 'tiles', split_axis=1, concat_axis=1, tiled=True)  6.94 us
    all_to_all x1, starting transfers between devices, body(): lax.all_to_all(served, 'tiles', split_axis=1, concat_axis=1, tiled=True)  5.52 us
  transfers between devices with their start and end apart: 3, of which 3 were waited for; matrix products, arithmetic and copies ran while one was open for 4% of the time, Pallas kernels for 0%

profile of v6, /device:TPU:2, one launch (start us, length us, event | category | flops | bytes accessed | tf_op | source)
XLA Modules:
  0.0 119.1 jit_solution(17610327916446654590)
XLA Ops:
  0.7 1.3 %convert_reduce_fusion = s32[1024]{0:T(1024)S(1)} fusion(s32[1024]{0:T(1024)} %bitcast.472), kind=kLoop, calls=%fused_computation.12 | loop fusion | flops 5241856 | bytes 8192 | tf_op jit(solution)/shard_map/reduce_sum | solution.py:368
  1.9 0.7 multiply_add_fusion.7
  2.6 0.7 reduce-precision_convert_fusion.9
  3.3 1.6 %fusion.6 = f32[3,2048]{1,0:T(4,128)S(1)} fusion(s32[1024]{0:T(1024)S(1)} %multiply_add_fusion.7, bf16[1,1024]{1,0:T(2,128)(2,1)S(1)} %get-tuple-element.164, bf16[1,1024]{1,0:T(2,128)(2,1)S(1)} %get-tuple-element.165, bf16[1,1024]{1,0:T(2,128)(2,1)S(1)} %get-tuple-element.163), kind=kOutput, calls=%fused_computation.8 | convolution fusion | flops 14698496 | bytes 34816 | tf_op jit(solution)/shard_map/dot_general | solution.py:324
  5.0 0.7 all_to_all.12
  5.7 12.0 %all-to-all-start = ((s32[64,1,32]{2,1,0:T(1,128)}), s32[64,1,32]{2,1,0:T(1,128)S(1)}, u32[]{:S(2)}, u32[]{:S(2)}) async-start(s32[64,1,32]{2,1,0:T(1,128)} %bitcast.22), calls=%async_computation | async-start | bytes 65536 | tf_op jit(solution)/shard_map/all_to_all | solution.py:376
  18.7 0.2 fusion.11
  18.9 0.1 multiply_reduce_fusion.6
  19.0 0.2 convolution_add_fusion.1
  19.9 0.3 fusion.48
  20.4 0.2 reshape.520
  20.6 0.2 stack.30
  20.8 0.1 multiply_reduce_fusion.1
  21.0 0.2 concatenate.29
  21.3 4.9 %all-to-all-done = s32[64,1,32]{2,1,0:T(1,128)S(1)} async-done(((s32[64,1,32]{2,1,0:T(1,128)}), s32[64,1,32]{2,1,0:T(1,128)S(1)}, u32[]{:S(2)}, u32[]{:S(2)}) %all-to-all-start) | async-done | bytes 8224 | tf_op jit(solution)/shard_map/all_to_all | solution.py:376
  26.2 0.5 broadcast.804
  26.7 0.7 reduce.13
  27.5 3.6 %fusion.1 = f32[27,2048]{1,0:T(8,128)S(1)} fusion(s32[2048]{0:T(1024)S(1)} %eq.47, bf16[9,2048]{1,0:T(8,128)(2,1)S(1)} %get-tuple-element.103, bf16[9,2048]{1,0:T(8,128)(2,1)S(1)} %get-tuple-element.104, bf16[9,2048]{1,0:T(8,128)(2,1)S(1)} %get-tuple-element.102), kind=kOutput, calls=%fused_computation.2 | convolution fusion | flops 231018496 | bytes 339968 | tf_op jit(solution)/shard_map/dot_general | solution.py:324
  31.2 0.1 reshape.522
  31.3 0.2 copy.159
  31.5 0.9 reshape.565
  32.3 5.5 %all-to-all-start.1 = ((f32[64,1,288]{2,1,0:T(1,128)}), f32[64,1,288]{2,1,0:T(1,128)S(1)}, u32[]{:S(2)}, u32[]{:S(2)}) async-start(f32[64,1,288]{2,1,0:T(1,128)} %reshape.565), calls=%async_computation.1 | async-start | bytes 196608 | tf_op jit(solution)/shard_map/all_to_all | solution.py:379
  37.9 0.5 pad_bitcast_fusion.bg_ref
  39.3 0.2 copy.75
  39.5 0.8 pad_convert_fusion.target_ref
  40.3 6.9 %all-to-all-done.1 = f32[64,1,288]{2,1,0:T(1,128)S(1)} async-done(((f32[64,1,288]{2,1,0:T(1,128)}), f32[64,1,288]{2,1,0:T(1,128)S(1)}, u32[]{:S(2)}, u32[]{:S(2)}) %all-to-all-start.1) | async-done | bytes 73760 | tf_op jit(solution)/shard_map/all_to_all | solution.py:379
  47.2 0.5 broadcast.810
  47.8 0.8 reduce.14
  48.6 0.1 reshape.566
  48.9 0.2 reshape.523
  49.1 1.8 %fusion.5 = f32[27,1024]{1,0:T(8,128)S(1)} fusion(s32[1024]{0:T(1024)S(1)} %multiply_add_fusion.7, bf16[9,2048]{1,0:T(8,128)(2,1)S(1)} %get-tuple-element.100, bf16[9,2048]{1,0:T(8,128)(2,1)S(1)} %get-tuple-element.101, bf16[9,2048]{1,0:T(8,128)(2,1)S(1)} %get-tuple-element.99), kind=kOutput, calls=%fused_computation.7 | convolution fusion | flops 115675136 | bytes 225280 | tf_op jit(solution)/shard_map/dot_general | solution.py:324
  50.9 0.7 maximum_bitcast_fusion.entry_ref
  51.6 10.2 %shard_map.138 = (f32[1,1024,8]{2,1,0:T(8,128)}, f32[1,16,1024]{2,1,0:T(8,128)}) custom-call(s32[1]{0:T(128)} %bitcast.426.counts_ref, s32[1]{0:T(128)} %bitcast.1.tiles_ref, f32[1,16,1024]{2,1,0:T(8,128)} %maximum_bitcast_fusion.entry_ref, f32[1,1024,8]{2,1,0:T(8,128)} %pad_convert_fusion.target_ref, f32[1,8]{1,0:T(1,128)} %pad_bitcast_fusion.bg_ref), custom_call_target="tpu_custom_call" | custom-call | tf_op jit(solution)/shard_map/pallas_call | solution.py:293
  61.8 0.9 fusion.144
  62.7 1.0 slice_bitcast_fusion.8
  63.8 1.7 %fusion.4 = f32[27,2048]{1,0:T(8,128)S(1)} fusion(s32[1024]{0:T(1024)S(1)} %multiply_add_fusion.7, bf16[9,1024]{1,0:T(8,128)(2,1)S(1)} %get-tuple-element.116, bf16[9,1024]{1,0:T(8,128)(2,1)S(1)} %get-tuple-element.117, bf16[9,1024]{1,0:T(8,128)(2,1)S(1)} %get-tuple-element.115), kind=kOutput, calls=%fused_computation.6 | convolution fusion | flops 115509248 | bytes 280576 | tf_op jit(solution)/shard_map/dot_general | solution.py:324
  65.6 0.1 reshape.524
  65.7 0.2 copy.158
  65.9 0.9 reshape.567
  66.8 16.0 %all-to-all-start.2 = ((f32[64,1,288]{2,1,0:T(1,128)}), f32[64,1,288]{2,1,0:T(1,128)S(1)}, u32[]{:S(2)}, u32[]{:S(2)}) async-start(f32[64,1,288]{2,1,0:T(1,128)} %reshape.567), calls=%async_computation.2 | async-start | bytes 196608 | tf_op jit(solution)/shard_map/all_to_all | solution.py:412
  82.9 0.7 copy.90
  83.6 8.6 %all-to-all-done.2 = f32[64,1,288]{2,1,0:T(1,128)S(1)} async-done(((f32[64,1,288]{2,1,0:T(1,128)}), f32[64,1,288]{2,1,0:T(1,128)S(1)}, u32[]{:S(2)}, u32[]{:S(2)}) %all-to-all-start.2) | async-done | bytes 73760 | tf_op jit(solution)/shard_map/all_to_all | solution.py:412
  92.2 0.8 reduce.15
  93.1 0.1 reshape.568
  93.3 0.2 reshape.525
  93.5 3.3 %fusion = f32[27,2048]{1,0:T(8,128)S(1)} fusion(s32[2048]{0:T(1024)S(1)} %eq.47, bf16[9,2048]{1,0:T(8,128)(2,1)S(1)} %get-tuple-element.95, bf16[9,2048]{1,0:T(8,128)(2,1)S(1)} %get-tuple-element.96, bf16[9,2048]{1,0:T(8,128)(2,1)S(1)} %get-tuple-element.94), kind=kOutput, calls=%fused_computation.1 | convolution fusion | flops 231018496 | bytes 339968 | tf_op jit(solution)/shard_map/dot_general | solution.py:324
  96.9 13.0 %all_gather.3 = f32[4,145,128]{2,1,0:T(8,128)S(1)} all-gather(f32[1,145,128]{2,1,0:T(8,128)S(1)} %fusion.50), channel_id=1, replica_groups=mesh['tiles'=64,'views'=4] {'views'}, dimensions={0}, use_global_device_ids=true | all-gather | bytes 371200 | tf_op jit(solution)/shard_map/all_gather | solution.py:415
  110.3 0.3 convolution_add_fusion
  110.6 0.5 fusion.45
  111.1 0.1 multiply_reduce_fusion.5
  111.6 1.3 %multiply_reduce_fusion.2 = (f32[4,3,2048]{2,1,0:T(4,128)S(1)}, f32[4,3,3,2048]{3,1,2,0:T(4,128)S(1)}) fusion(f32[3,3,2048]{2,0,1:T(4,128)S(1)} %copy.85, f32[4,3,3,2048]{3,0,2,1:T(4,128)S(1)} %pad_add_fusion, f32[4,3,3]{2,1,0:T(4,128)S(1)} %reshape.528), kind=kOutput, calls=%fused_computation.30 | convolution fusion | flops 2777088 | bytes 762000 | tf_op jit(solution)/shard_map/vmap(transpose(jvp(ik,kjg->ijg)))/dot_general | solution.py:87
  112.9 0.2 copy_multiply_fusion
  113.4 0.2 fusion.169
  113.7 0.1 fusion.37
  114.4 0.7 broadcast_multiply_fusion
  115.0 0.1 add_add_fusion.5
  115.3 0.1 add_add_fusion.4
  115.4 0.2 fusion.42
  115.7 0.4 fusion.34
  116.2 0.1 fusion.38
  116.4 0.1 fusion.36
  116.5 0.2 fusion.77
  116.8 0.9 add_reduce_fusion
  117.7 1.3 %divide_subtract_fusion = (f32[59,2048]{1,0:T(8,128)}, f32[59,2048]{1,0:T(8,128)}, f32[59,2048]{1,0:T(8,128)}) fusion(f32[59,2048]{1,0:T(8,128)S(1)} %copy-done.1, f32[59]{0:T(128)S(1)} %copy-done.6, f32[59,2048]{1,0:T(8,128)S(1)} %add_reduce_fusion, f32[59,2048]{1,0:T(8,128)S(1)} %copy-done.2, f32[59,2048]{1,0:T(8,128)S(1)} %copy-done.3), kind=kLoop, calls=%fused_computation.25 | loop fusion | flops 1329152 | bytes 3383532 | tf_op jit(solution)/shard_map/sub | solution.py:335
  (115 shorter events, 4.0 us)
Async XLA Ops:
  0.6 17.7 %copy-start = (f32[16,12]{1,0:T(8,128)S(1)}, f32[16,12]{1,0:T(8,128)}, u32[]{:S(2)}) copy-start(f32[16,12]{1,0:T(8,128)} %param.15) | copy-start | bytes 2308
  0.6 17.8 %copy-start.1 = (f32[59,2048]{1,0:T(8,128)S(1)}, f32[59,2048]{1,0:T(8,128)}, u32[]{:S(2)}) copy-start(f32[59,2048]{1,0:T(8,128)} %param.11) | copy-start | bytes 1449988
  5.7 20.6 %all-to-all-start = ((s32[64,1,32]{2,1,0:T(1,128)}), s32[64,1,32]{2,1,0:T(1,128)S(1)}, u32[]{:S(2)}, u32[]{:S(2)}) async-start(s32[64,1,32]{2,1,0:T(1,128)} %bitcast.22), calls=%async_computation | async-start | bytes 65536 | tf_op jit(solution)/shard_map/all_to_all | solution.py:376
  31.1 6.8 %copy-start.7 = (f32[3]{0:T(128)S(1)}, f32[3]{0:T(128)}, u32[]{:S(2)}) copy-start(f32[3]{0:T(128)} %param.21) | copy-start | bytes 40
  31.1 8.2 %copy-start.5 = (bf16[1,1,3,1024]{3,2,1,0:T(4,128)(2,1)S(1)}, bf16[1,1,3,1024]{3,2,1,0:T(4,128)(2,1)}, u32[]{:S(2)}) copy-start(bf16[1,1,3,1024]{3,2,1,0:T(4,128)(2,1)} %param.20) | copy-start | bytes 18436
  32.3 14.9 %all-to-all-start.1 = ((f32[64,1,288]{2,1,0:T(1,128)}), f32[64,1,288]{2,1,0:T(1,128)S(1)}, u32[]{:S(2)}, u32[]{:S(2)}) async-start(f32[64,1,288]{2,1,0:T(1,128)} %reshape.565), calls=%async_computation.1 | async-start | bytes 196608 | tf_op jit(solution)/shard_map/all_to_all | solution.py:379
  65.6 17.3 %copy-start.4 = (f32[1,1024,8]{2,1,0:T(8,128)S(1)}, f32[1,1024,8]{2,1,0:T(8,128)}, u32[]{:S(2)}) copy-start(f32[1,1024,8]{2,1,0:T(8,128)} %get-tuple-element.6) | copy-start | bytes 98308
  66.8 25.4 %all-to-all-start.2 = ((f32[64,1,288]{2,1,0:T(1,128)}), f32[64,1,288]{2,1,0:T(1,128)S(1)}, u32[]{:S(2)}, u32[]{:S(2)}) async-start(f32[64,1,288]{2,1,0:T(1,128)} %reshape.567), calls=%async_computation.2 | async-start | bytes 196608 | tf_op jit(solution)/shard_map/all_to_all | solution.py:412
  116.5 1.2 copy-start.2
  116.5 1.2 %copy-start.3 = (f32[59,2048]{1,0:T(8,128)S(1)}, f32[59,2048]{1,0:T(8,128)}, u32[]{:S(2)}) copy-start(f32[59,2048]{1,0:T(8,128)} %param.13) | copy-start | bytes 1449988
  116.5 1.2 copy-start.6

commit v7 on v6

--- a/solution.py
+++ b/solution.py
@@ -412,8 +412,13 @@
     grad_back = lax.all_to_all(grad_send, "tiles", split_axis=1, concat_axis=1, tiled=True)
     attr_grad = select_rows(grad_back.reshape(9, peers * capacity), chosen, 0)
     payload = jnp.concatenate([attr_grad.reshape(-1), jnp.pad(camera, (0, 128 - 12))])
-    gathered = lax.all_gather(payload.reshape(-1, 128), "views", axis=0, tiled=False)
-    gathered = gathered.reshape(gathered.shape[0], -1)
+    views = lax.axis_size("views")
+    view = lax.axis_index("views")
+    shifted = [payload] + [
+        lax.ppermute(payload, "views", [(i, (i + s) % views) for i in range(views)])
+        for s in range(1, views)
+    ]
+    gathered = jnp.stack(shifted)[(view - jnp.arange(views)) % views]
     view_grads = gathered[:, : 9 * owned].reshape(-1, 9, owned)
     view_cameras = gathered[:, 9 * owned : 9 * owned + 12]
 

time: 121 us -> 122 us (level)
  blocking collectives: 13 us -> 0 us
  Pallas kernels: 10.2 us -> 19.3 us
  waiting for transfers between devices: 20.4 us -> 25.7 us
  starting transfers between devices: 33.6 us -> 30 us
  other arithmetic: 15.4 us -> 17.1 us
    all_gather x1 -> x0, blocking collectives: 13 us -> none  [body(): lax.all_gather(payload.reshape(-1, 128), 'views', axis=0, tiled=False)]
    pallas_call x1, Pallas kernels: 10.2 us -> 19.3 us  [render_tiles(): pl.pallas_call(partial(render_kernel, tile_cols=tile_cols), grid=(n,), in...]
    all_to_all x1, starting transfers between devices: 16 us -> 7.23 us  [body(): lax.all_to_all(grad_send, 'tiles', split_axis=1, concat_axis=1, tiled=True)]
    ppermute x0 -> x3, waiting for transfers between devices: none -> 5.07 us  [body(): lax.ppermute(payload, 'views', [(i, (i + s) % views) for i in range(views)])]
    ppermute x0 -> x3, starting transfers between devices: none -> 4.73 us  [body(): lax.ppermute(payload, 'views', [(i, (i + s) % views) for i in range(views)])]
    unnamed x24 -> x35, local copies, waits for them, and re-layouts: 3.04 us -> 3.09 us
  transfers between devices with their start and end apart: 3 -> 6, of which waited for: 3 -> 6; matrix products, arithmetic and copies ran while one was open for 4% -> 5% of each run, Pallas kernels for 0% -> 0%
where the time goes in v7:
time: 122 us; the launch traced here: 120 us
  starting transfers between devices  30 us (25%)
  waiting for transfers between devices  25.7 us (21%)
  Pallas kernels  19.3 us (16%)
  other arithmetic  17.1 us (14%)
  matrix products  15.4 us (13%)
  local copies, waits for them, and re-layouts  9.22 us (8%)
  between operations  2.85 us (2%)
    pallas_call x1, Pallas kernels, render_tiles(): pl.pallas_call(partial(render_kernel, tile_cols=tile_cols), grid=(n,), in...  19.3 us
    dot_general x5, matrix products, select_rows(): lax.dot_general(pieces, chosen, (((1,), (contract,)), ((), ())), preferre...  12 us
    all_to_all x1, starting transfers between devices, body(): lax.all_to_all(asked_for, 'tiles', split_axis=0, concat_axis=0, tiled=True)  12 us
    all_to_all x1, waiting for transfers between devices, body(): lax.all_to_all(grad_send, 'tiles', split_axis=1, concat_axis=1, tiled=True)  9.3 us
    all_to_all x1, starting transfers between devices, body(): lax.all_to_all(grad_send, 'tiles', split_axis=1, concat_axis=1, tiled=True)  7.23 us
    all_to_all x1, waiting for transfers between devices, body(): lax.all_to_all(served, 'tiles', split_axis=1, concat_axis=1, tiled=True)  6.98 us
    all_to_all x1, starting transfers between devices, body(): lax.all_to_all(served, 'tiles', split_axis=1, concat_axis=1, tiled=True)  6.01 us
    ppermute x3, waiting for transfers between devices, body(): lax.ppermute(payload, 'views', [(i, (i + s) % views) for i in range(views)])  5.07 us
  transfers between devices with their start and end apart: 6, of which 6 were waited for; matrix products, arithmetic and copies ran while one was open for 5% of the time, Pallas kernels for 0%

profile of v7, /device:TPU:2, one launch (start us, length us, event | category | flops | bytes accessed | tf_op | source)
XLA Modules:
  0.0 119.6 jit_solution(3119693247130672831)
XLA Ops:
  0.7 1.3 %convert_reduce_fusion = s32[1024]{0:T(1024)S(1)} fusion(s32[1024]{0:T(1024)} %bitcast.464), kind=kLoop, calls=%fused_computation.13 | loop fusion | flops 5241856 | bytes 8192 | tf_op jit(solution)/shard_map/reduce_sum | solution.py:368
  1.9 0.7 multiply_add_fusion.7
  2.6 0.7 reduce-precision_convert_fusion.9
  3.3 1.6 %fusion.6 = f32[3,2048]{1,0:T(4,128)S(1)} fusion(s32[1024]{0:T(1024)S(1)} %multiply_add_fusion.7, bf16[1,1024]{1,0:T(2,128)(2,1)S(1)} %get-tuple-element.164, bf16[1,1024]{1,0:T(2,128)(2,1)S(1)} %get-tuple-element.165, bf16[1,1024]{1,0:T(2,128)(2,1)S(1)} %get-tuple-element.163), kind=kOutput, calls=%fused_computation.9 | convolution fusion | flops 14698496 | bytes 34816 | tf_op jit(solution)/shard_map/dot_general | solution.py:324
  5.0 0.7 all_to_all.12
  5.7 12.0 %all-to-all-start = ((s32[64,1,32]{2,1,0:T(1,128)}), s32[64,1,32]{2,1,0:T(1,128)S(1)}, u32[]{:S(2)}, u32[]{:S(2)}) async-start(s32[64,1,32]{2,1,0:T(1,128)} %bitcast.22), calls=%async_computation | async-start | bytes 65536 | tf_op jit(solution)/shard_map/all_to_all | solution.py:376
  18.7 0.2 fusion.11
  19.0 0.2 convolution_add_fusion.1
  19.5 0.7 slice_multiply_fusion.18
  20.5 0.3 fusion.48
  21.0 0.2 reshape.566
  21.2 0.2 stack.40
  21.4 0.2 multiply_reduce_fusion.1
  21.6 0.2 concatenate.29
  21.9 4.3 %all-to-all-done = s32[64,1,32]{2,1,0:T(1,128)S(1)} async-done(((s32[64,1,32]{2,1,0:T(1,128)}), s32[64,1,32]{2,1,0:T(1,128)S(1)}, u32[]{:S(2)}, u32[]{:S(2)}) %all-to-all-start) | async-done | bytes 8224 | tf_op jit(solution)/shard_map/all_to_all | solution.py:376
  26.2 0.5 broadcast.873
  26.7 0.7 reduce.13
  27.5 3.6 %fusion.1 = f32[27,2048]{1,0:T(8,128)S(1)} fusion(s32[2048]{0:T(1024)S(1)} %eq.49, bf16[9,2048]{1,0:T(8,128)(2,1)S(1)} %get-tuple-element.103, bf16[9,2048]{1,0:T(8,128)(2,1)S(1)} %get-tuple-element.104, bf16[9,2048]{1,0:T(8,128)(2,1)S(1)} %get-tuple-element.102), kind=kOutput, calls=%fused_computation.3 | convolution fusion | flops 231018496 | bytes 339968 | tf_op jit(solution)/shard_map/dot_general | solution.py:324
  31.3 0.2 copy.156
  31.5 0.9 reshape.618
  32.3 6.0 %all-to-all-start.1 = ((f32[64,1,288]{2,1,0:T(1,128)}), f32[64,1,288]{2,1,0:T(1,128)S(1)}, u32[]{:S(2)}, u32[]{:S(2)}) async-start(f32[64,1,288]{2,1,0:T(1,128)} %reshape.618), calls=%async_computation.1 | async-start | bytes 196608 | tf_op jit(solution)/shard_map/all_to_all | solution.py:379
  38.4 0.5 pad_bitcast_fusion.bg_ref
  39.7 0.2 copy.75
  39.9 0.8 pad_convert_fusion.target_ref
  40.8 7.0 %all-to-all-done.1 = f32[64,1,288]{2,1,0:T(1,128)S(1)} async-done(((f32[64,1,288]{2,1,0:T(1,128)}), f32[64,1,288]{2,1,0:T(1,128)S(1)}, u32[]{:S(2)}, u32[]{:S(2)}) %all-to-all-start.1) | async-done | bytes 73760 | tf_op jit(solution)/shard_map/all_to_all | solution.py:379
  47.7 0.6 broadcast.879
  48.3 0.9 reduce.14
  49.5 0.2 reshape.569
  49.7 1.8 %fusion.5 = f32[27,1024]{1,0:T(8,128)S(1)} fusion(s32[1024]{0:T(1024)S(1)} %multiply_add_fusion.7, bf16[9,2048]{1,0:T(8,128)(2,1)S(1)} %get-tuple-element.100, bf16[9,2048]{1,0:T(8,128)(2,1)S(1)} %get-tuple-element.101, bf16[9,2048]{1,0:T(8,128)(2,1)S(1)} %get-tuple-element.99), kind=kOutput, calls=%fused_computation.8 | convolution fusion | flops 115675136 | bytes 225280 | tf_op jit(solution)/shard_map/dot_general | solution.py:324
  51.6 0.7 maximum_bitcast_fusion.entry_ref
  52.3 19.3 %shard_map.138 = (f32[1,1024,8]{2,1,0:T(8,128)}, f32[1,16,1024]{2,1,0:T(8,128)}) custom-call(s32[1]{0:T(128)} %bitcast.422.counts_ref, s32[1]{0:T(128)} %bitcast.1.tiles_ref, f32[1,16,1024]{2,1,0:T(8,128)} %maximum_bitcast_fusion.entry_ref, f32[1,1024,8]{2,1,0:T(8,128)} %pad_convert_fusion.target_ref, f32[1,8]{1,0:T(1,128)} %pad_bitcast_fusion.bg_ref), custom_call_target="tpu_custom_call" | custom-call | tf_op jit(solution)/shard_map/pallas_call | solution.py:293
  71.6 0.9 fusion.143
  72.4 1.0 slice_bitcast_fusion.8
  73.6 1.7 %fusion.4 = f32[27,2048]{1,0:T(8,128)S(1)} fusion(s32[1024]{0:T(1024)S(1)} %multiply_add_fusion.7, bf16[9,1024]{1,0:T(8,128)(2,1)S(1)} %get-tuple-element.116, bf16[9,1024]{1,0:T(8,128)(2,1)S(1)} %get-tuple-element.117, bf16[9,1024]{1,0:T(8,128)(2,1)S(1)} %get-tuple-element.115), kind=kOutput, calls=%fused_computation.7 | convolution fusion | flops 115509248 | bytes 280576 | tf_op jit(solution)/shard_map/dot_general | solution.py:324
  75.5 0.2 copy.155
  75.7 0.9 reshape.620
  76.5 7.2 %all-to-all-start.2 = ((f32[64,1,288]{2,1,0:T(1,128)}), f32[64,1,288]{2,1,0:T(1,128)S(1)}, u32[]{:S(2)}, u32[]{:S(2)}) async-start(f32[64,1,288]{2,1,0:T(1,128)} %reshape.620), calls=%async_computation.2 | async-start | bytes 196608 | tf_op jit(solution)/shard_map/all_to_all | solution.py:412
  83.8 9.3 %all-to-all-done.2 = f32[64,1,288]{2,1,0:T(1,128)S(1)} async-done(((f32[64,1,288]{2,1,0:T(1,128)}), f32[64,1,288]{2,1,0:T(1,128)S(1)}, u32[]{:S(2)}, u32[]{:S(2)}) %all-to-all-start.2) | async-done | bytes 73760 | tf_op jit(solution)/shard_map/all_to_all | solution.py:412
  93.2 0.9 reduce.15
  94.3 0.2 reshape.571
  94.5 3.3 %fusion = f32[27,2048]{1,0:T(8,128)S(1)} fusion(s32[2048]{0:T(1024)S(1)} %eq.49, bf16[9,2048]{1,0:T(8,128)(2,1)S(1)} %get-tuple-element.95, bf16[9,2048]{1,0:T(8,128)(2,1)S(1)} %get-tuple-element.96, bf16[9,2048]{1,0:T(8,128)(2,1)S(1)} %get-tuple-element.94), kind=kOutput, calls=%fused_computation.2 | convolution fusion | flops 231018496 | bytes 339968 | tf_op jit(solution)/shard_map/dot_general | solution.py:324
  97.9 3.8 %collective-permute-start.2 = (f32[18560]{0:T(1024)S(1)}, f32[18560]{0:T(1024)S(1)}, u32[]{:S(2)}, u32[]{:S(2)}) collective-permute-start(f32[18560]{0:T(1024)S(1)} %select_maximum_fusion), channel_id=1, source_target_pairs={{0,3},{1,0},{2,1},{3,2},{4,7},{5,4},{6,5},{7,6},{8,11},{9,8},{10,9... | collective-permute-start | bytes 222728 | tf_op jit(solution)/shard_map/ppermute | solution.py:418
  101.7 1.0 collective-permute-start
  102.7 0.7 copy.90
  103.5 1.8 %collective-permute-done.2 = f32[18560]{0:T(1024)S(1)} collective-permute-done((f32[18560]{0:T(1024)S(1)}, f32[18560]{0:T(1024)S(1)}, u32[]{:S(2)}, u32[]{:S(2)}) %collective-permute-start.2) | collective-permute-done | bytes 74272 | tf_op jit(solution)/shard_map/ppermute | solution.py:418
  105.3 2.8 %collective-permute-done.1 = f32[18560]{0:T(1024)S(1)} collective-permute-done((f32[18560]{0:T(1024)S(1)}, f32[18560]{0:T(1024)S(1)}, u32[]{:S(2)}, u32[]{:S(2)}) %collective-permute-start.1) | collective-permute-done | bytes 74272 | tf_op jit(solution)/shard_map/ppermute | solution.py:418
  108.2 0.5 collective-permute-done
  108.7 0.3 pad_maximum_fusion
  109.0 0.7 gather_fusion
  110.0 0.3 convolution_add_fusion
  110.3 0.5 fusion.45
  111.3 1.3 %multiply_reduce_fusion.2 = (f32[4,3,2048]{2,1,0:T(4,128)S(1)}, f32[4,3,3,2048]{3,1,2,0:T(4,128)S(1)}) fusion(f32[3,3,2048]{2,0,1:T(4,128)S(1)} %copy.85, f32[4,3,3,2048]{3,0,2,1:T(4,128)S(1)} %pad_add_fusion, f32[4,3,3]{2,1,0:T(4,128)S(1)} %reshape.573), kind=kOutput, calls=%fused_computation.31 | convolution fusion | flops 2777088 | bytes 762000 | tf_op jit(solution)/shard_map/vmap(transpose(jvp(ik,kjg->ijg)))/dot_general | solution.py:87
  112.6 0.2 copy_multiply_fusion
  113.1 0.7 fusion.60
  113.8 0.2 fusion.170
  114.7 0.7 broadcast_multiply_fusion
  115.4 0.1 add_add_fusion.5
  115.7 0.1 add_add_fusion.4
  115.8 0.2 fusion.42
  116.2 0.4 fusion.34
  116.9 0.1 fusion.36
  117.1 0.2 fusion.76
  117.3 0.9 add_reduce_fusion
  118.3 1.3 %divide_subtract_fusion = (f32[59,2048]{1,0:T(8,128)}, f32[59,2048]{1,0:T(8,128)}, f32[59,2048]{1,0:T(8,128)}) fusion(f32[59,2048]{1,0:T(8,128)S(1)} %copy-done.1, f32[59]{0:T(128)S(1)} %copy-done.12, f32[59,2048]{1,0:T(8,128)S(1)} %add_reduce_fusion, f32[59,2048]{1,0:T(8,128)S(1)} %copy-done.2, f32[59,2048]{1,0:T(8,128)S(1)} %copy-done.3), kind=kLoop, calls=%fused_computation.26 | loop fusion | flops 1329152 | bytes 3383532 | tf_op jit(solution)/shard_map/sub | solution.py:335
  (139 shorter events, 5.1 us)
Async XLA Ops:
  0.6 17.7 %copy-start = (f32[16,12]{1,0:T(8,128)S(1)}, f32[16,12]{1,0:T(8,128)}, u32[]{:S(2)}) copy-start(f32[16,12]{1,0:T(8,128)} %param.15) | copy-start | bytes 2308
  0.6 17.8 %copy-start.1 = (f32[59,2048]{1,0:T(8,128)S(1)}, f32[59,2048]{1,0:T(8,128)}, u32[]{:S(2)}) copy-start(f32[59,2048]{1,0:T(8,128)} %param.11) | copy-start | bytes 1449988
  5.7 20.6 %all-to-all-start = ((s32[64,1,32]{2,1,0:T(1,128)}), s32[64,1,32]{2,1,0:T(1,128)S(1)}, u32[]{:S(2)}, u32[]{:S(2)}) async-start(s32[64,1,32]{2,1,0:T(1,128)} %bitcast.22), calls=%async_computation | async-start | bytes 65536 | tf_op jit(solution)/shard_map/all_to_all | solution.py:376
  31.1 7.3 %copy-start.13 = (f32[3]{0:T(128)S(1)}, f32[3]{0:T(128)}, u32[]{:S(2)}) copy-start(f32[3]{0:T(128)} %param.21) | copy-start | bytes 40
  31.1 8.6 %copy-start.11 = (bf16[1,1,3,1024]{3,2,1,0:T(4,128)(2,1)S(1)}, bf16[1,1,3,1024]{3,2,1,0:T(4,128)(2,1)}, u32[]{:S(2)}) copy-start(bf16[1,1,3,1024]{3,2,1,0:T(4,128)(2,1)} %param.20) | copy-start | bytes 18436
  32.3 15.4 %all-to-all-start.1 = ((f32[64,1,288]{2,1,0:T(1,128)}), f32[64,1,288]{2,1,0:T(1,128)S(1)}, u32[]{:S(2)}, u32[]{:S(2)}) async-start(f32[64,1,288]{2,1,0:T(1,128)} %reshape.618), calls=%async_computation.1 | async-start | bytes 196608 | tf_op jit(solution)/shard_map/all_to_all | solution.py:379
  76.5 16.6 %all-to-all-start.2 = ((f32[64,1,288]{2,1,0:T(1,128)}), f32[64,1,288]{2,1,0:T(1,128)S(1)}, u32[]{:S(2)}, u32[]{:S(2)}) async-start(f32[64,1,288]{2,1,0:T(1,128)} %reshape.620), calls=%async_computation.2 | async-start | bytes 196608 | tf_op jit(solution)/shard_map/all_to_all | solution.py:412
  94.5 8.2 %copy-start.4 = (f32[1,1024,8]{2,1,0:T(8,128)S(1)}, f32[1,1024,8]{2,1,0:T(8,128)}, u32[]{:S(2)}) copy-start(f32[1,1024,8]{2,1,0:T(8,128)} %get-tuple-element.6) | copy-start | bytes 98308
  97.9 7.4 %collective-permute-start.2 = (f32[18560]{0:T(1024)S(1)}, f32[18560]{0:T(1024)S(1)}, u32[]{:S(2)}, u32[]{:S(2)}) collective-permute-start(f32[18560]{0:T(1024)S(1)} %select_maximum_fusion), channel_id=1, source_target_pairs={{0,3},{1,0},{2,1},{3,2},{4,7},{5,4},{6,5},{7,6},{8,11},{9,8},{10,9... | collective-permute-start | bytes 222728 | tf_op jit(solution)/shard_map/ppermute | solution.py:418
  101.7 6.4 %collective-permute-start.1 = (f32[18560]{0:T(1024)S(1)}, f32[18560]{0:T(1024)S(1)}, u32[]{:S(2)}, u32[]{:S(2)}) collective-permute-start(f32[18560]{0:T(1024)S(1)} %select_maximum_fusion), channel_id=1, source_target_pairs={{0,2},{1,3},{2,0},{3,1},{4,6},{5,7},{6,4},{7,5},{8,10},{9,11},{10,... | collective-permute-start | bytes 222728 | tf_op jit(solution)/shard_map/ppermute | solution.py:418
  101.7 7.0 %collective-permute-start = (f32[18560]{0:T(1024)S(1)}, f32[18560]{0:T(1024)S(1)}, u32[]{:S(2)}, u32[]{:S(2)}) collective-permute-start(f32[18560]{0:T(1024)S(1)} %select_maximum_fusion), channel_id=1, source_target_pairs={{0,1},{1,2},{2,3},{3,0},{4,5},{5,6},{6,7},{7,4},{8,9},{9,10},{10,1... | collective-permute-start | bytes 222728 | tf_op jit(solution)/shard_map/ppermute | solution.py:418
  115.4 0.7 copy-start.10
  115.6 1.4 %copy-start.6 = (f32[1,2048]{1,0:T(1,128)S(1)}, f32[1,2048]{1,0:T(1,128)}, u32[]{:S(2)}) copy-start(f32[1,2048]{1,0:T(1,128)} %get-tuple-element.68) | copy-start | bytes 24580
  115.6 1.4 %copy-start.7 = (f32[1,2048]{1,0:T(1,128)S(1)}, f32[1,2048]{1,0:T(1,128)}, u32[]{:S(2)}) copy-start(f32[1,2048]{1,0:T(1,128)} %get-tuple-element.69) | copy-start | bytes 24580
  115.6 1.4 %copy-start.8 = (f32[1,2048]{1,0:T(1,128)S(1)}, f32[1,2048]{1,0:T(1,128)}, u32[]{:S(2)}) copy-start(f32[1,2048]{1,0:T(1,128)} %get-tuple-element.70) | copy-start | bytes 24580
  115.7 1.4 %copy-start.9 = (f32[1,2048]{1,0:T(1,128)S(1)}, f32[1,2048]{1,0:T(1,128)}, u32[]{:S(2)}) copy-start(f32[1,2048]{1,0:T(1,128)} %get-tuple-element.71) | copy-start | bytes 24580
  115.8 1.5 %copy-start.5 = (f32[4,1,2048]{2,0,1:T(4,128)S(1)}, f32[4,1,2048]{2,0,1:T(4,128)}, u32[]{:S(2)}) copy-start(f32[4,1,2048]{2,0,1:T(4,128)} %fusion.60) | copy-start | bytes 98308
  117.0 1.2 %copy-start.2 = (f32[59,2048]{1,0:T(8,128)S(1)}, f32[59,2048]{1,0:T(8,128)}, u32[]{:S(2)}) copy-start(f32[59,2048]{1,0:T(8,128)} %param.12) | copy-start | bytes 1449988
  117.0 1.2 copy-start.3
  117.1 1.2 copy-start.12

commit v8 on v6

--- a/solution.py
+++ b/solution.py
@@ -12,7 +12,7 @@
 TILE_ROWS = 8
 LIST = 1024
 BLOCK = 128
-KB = 128
+KB = 256
 
 
 focal_length = 400.0

time: 121 us -> 120 us (level)
  starting transfers between devices: 33.6 us -> 30.6 us
  Pallas kernels: 10.2 us -> 11.9 us
    all_to_all x1, starting transfers between devices: 16 us -> 13.1 us  [body(): lax.all_to_all(grad_send, 'tiles', split_axis=1, concat_axis=1, tiled=True)]
    pallas_call x1, Pallas kernels: 10.2 us -> 11.9 us  [render_tiles(): pl.pallas_call(partial(render_kernel, tile_cols=tile_cols), grid=(n,), in...]
where the time goes in v8:
time: 120 us; the launch traced here: 118 us
  starting transfers between devices  30.6 us (26%)
  waiting for transfers between devices  20.4 us (17%)
  other arithmetic  15.4 us (13%)
  matrix products  15.4 us (13%)
  blocking collectives  13.6 us (11%)
  Pallas kernels  11.9 us (10%)
  local copies, waits for them, and re-layouts  8.2 us (7%)
  between operations  2.76 us (2%)
    all_gather x1, blocking collectives, body(): lax.all_gather(payload.reshape(-1, 128), 'views', axis=0, tiled=False)  13.6 us
    all_to_all x1, starting transfers between devices, body(): lax.all_to_all(grad_send, 'tiles', split_axis=1, concat_axis=1, tiled=True)  13.1 us
    dot_general x5, matrix products, select_rows(): lax.dot_general(pieces, chosen, (((1,), (contract,)), ((), ())), preferre...  12 us
    all_to_all x1, starting transfers between devices, body(): lax.all_to_all(asked_for, 'tiles', split_axis=0, concat_axis=0, tiled=True)  12 us
    pallas_call x1, Pallas kernels, render_tiles(): pl.pallas_call(partial(render_kernel, tile_cols=tile_cols), grid=(n,), in...  11.9 us
    all_to_all x1, waiting for transfers between devices, body(): lax.all_to_all(grad_send, 'tiles', split_axis=1, concat_axis=1, tiled=True)  8.61 us
    all_to_all x1, waiting for transfers between devices, body(): lax.all_to_all(served, 'tiles', split_axis=1, concat_axis=1, tiled=True)  6.94 us
    all_to_all x1, starting transfers between devices, body(): lax.all_to_all(served, 'tiles', split_axis=1, concat_axis=1, tiled=True)  5.52 us
  transfers between devices with their start and end apart: 3, of which 3 were waited for; matrix products, arithmetic and copies ran while one was open for 4% of the time, Pallas kernels for 0%

profile of v8, /device:TPU:2, one launch (start us, length us, event | category | flops | bytes accessed | tf_op | source)
XLA Modules:
  0.0 118.4 jit_solution(15054708739518076936)
XLA Ops:
  0.7 1.3 %convert_reduce_fusion = s32[1024]{0:T(1024)S(1)} fusion(s32[1024]{0:T(1024)} %bitcast.472), kind=kLoop, calls=%fused_computation.12 | loop fusion | flops 5241856 | bytes 8192 | tf_op jit(solution)/shard_map/reduce_sum | solution.py:368
  1.9 0.7 multiply_add_fusion.7
  2.6 0.7 reduce-precision_convert_fusion.9
  3.3 1.6 %fusion.6 = f32[3,2048]{1,0:T(4,128)S(1)} fusion(s32[1024]{0:T(1024)S(1)} %multiply_add_fusion.7, bf16[1,1024]{1,0:T(2,128)(2,1)S(1)} %get-tuple-element.164, bf16[1,1024]{1,0:T(2,128)(2,1)S(1)} %get-tuple-element.165, bf16[1,1024]{1,0:T(2,128)(2,1)S(1)} %get-tuple-element.163), kind=kOutput, calls=%fused_computation.8 | convolution fusion | flops 14698496 | bytes 34816 | tf_op jit(solution)/shard_map/dot_general | solution.py:324
  5.0 0.7 all_to_all.12
  5.7 12.0 %all-to-all-start = ((s32[64,1,32]{2,1,0:T(1,128)}), s32[64,1,32]{2,1,0:T(1,128)S(1)}, u32[]{:S(2)}, u32[]{:S(2)}) async-start(s32[64,1,32]{2,1,0:T(1,128)} %bitcast.22), calls=%async_computation | async-start | bytes 65536 | tf_op jit(solution)/shard_map/all_to_all | solution.py:376
  18.7 0.2 fusion.11
  18.9 0.1 multiply_reduce_fusion.6
  19.0 0.2 convolution_add_fusion.1
  19.9 0.3 fusion.48
  20.4 0.2 reshape.520
  20.6 0.2 stack.30
  20.8 0.1 multiply_reduce_fusion.1
  21.0 0.2 concatenate.29
  21.3 4.9 %all-to-all-done = s32[64,1,32]{2,1,0:T(1,128)S(1)} async-done(((s32[64,1,32]{2,1,0:T(1,128)}), s32[64,1,32]{2,1,0:T(1,128)S(1)}, u32[]{:S(2)}, u32[]{:S(2)}) %all-to-all-start) | async-done | bytes 8224 | tf_op jit(solution)/shard_map/all_to_all | solution.py:376
  26.2 0.5 broadcast.804
  26.7 0.7 reduce.13
  27.5 3.6 %fusion.1 = f32[27,2048]{1,0:T(8,128)S(1)} fusion(s32[2048]{0:T(1024)S(1)} %eq.47, bf16[9,2048]{1,0:T(8,128)(2,1)S(1)} %get-tuple-element.103, bf16[9,2048]{1,0:T(8,128)(2,1)S(1)} %get-tuple-element.104, bf16[9,2048]{1,0:T(8,128)(2,1)S(1)} %get-tuple-element.102), kind=kOutput, calls=%fused_computation.2 | convolution fusion | flops 231018496 | bytes 339968 | tf_op jit(solution)/shard_map/dot_general | solution.py:324
  31.2 0.1 reshape.522
  31.3 0.2 copy.159
  31.5 0.9 reshape.565
  32.3 5.5 %all-to-all-start.1 = ((f32[64,1,288]{2,1,0:T(1,128)}), f32[64,1,288]{2,1,0:T(1,128)S(1)}, u32[]{:S(2)}, u32[]{:S(2)}) async-start(f32[64,1,288]{2,1,0:T(1,128)} %reshape.565), calls=%async_computation.1 | async-start | bytes 196608 | tf_op jit(solution)/shard_map/all_to_all | solution.py:379
  37.9 0.5 pad_bitcast_fusion.bg_ref
  39.3 0.2 copy.75
  39.5 0.8 pad_convert_fusion.target_ref
  40.3 6.9 %all-to-all-done.1 = f32[64,1,288]{2,1,0:T(1,128)S(1)} async-done(((f32[64,1,288]{2,1,0:T(1,128)}), f32[64,1,288]{2,1,0:T(1,128)S(1)}, u32[]{:S(2)}, u32[]{:S(2)}) %all-to-all-start.1) | async-done | bytes 73760 | tf_op jit(solution)/shard_map/all_to_all | solution.py:379
  47.2 0.5 broadcast.810
  47.8 0.8 reduce.14
  48.6 0.1 reshape.566
  48.9 0.2 reshape.523
  49.1 1.8 %fusion.5 = f32[27,1024]{1,0:T(8,128)S(1)} fusion(s32[1024]{0:T(1024)S(1)} %multiply_add_fusion.7, bf16[9,2048]{1,0:T(8,128)(2,1)S(1)} %get-tuple-element.100, bf16[9,2048]{1,0:T(8,128)(2,1)S(1)} %get-tuple-element.101, bf16[9,2048]{1,0:T(8,128)(2,1)S(1)} %get-tuple-element.99), kind=kOutput, calls=%fused_computation.7 | convolution fusion | flops 115675136 | bytes 225280 | tf_op jit(solution)/shard_map/dot_general | solution.py:324
  50.9 0.7 maximum_bitcast_fusion.entry_ref
  51.6 11.9 %shard_map.138 = (f32[1,1024,8]{2,1,0:T(8,128)}, f32[1,16,1024]{2,1,0:T(8,128)}) custom-call(s32[1]{0:T(128)} %bitcast.426.counts_ref, s32[1]{0:T(128)} %bitcast.1.tiles_ref, f32[1,16,1024]{2,1,0:T(8,128)} %maximum_bitcast_fusion.entry_ref, f32[1,1024,8]{2,1,0:T(8,128)} %pad_convert_fusion.target_ref, f32[1,8]{1,0:T(1,128)} %pad_bitcast_fusion.bg_ref), custom_call_target="tpu_custom_call" | custom-call | tf_op jit(solution)/shard_map/pallas_call | solution.py:293
  63.5 0.9 fusion.144
  64.4 1.0 slice_bitcast_fusion.8
  65.5 1.7 %fusion.4 = f32[27,2048]{1,0:T(8,128)S(1)} fusion(s32[1024]{0:T(1024)S(1)} %multiply_add_fusion.7, bf16[9,1024]{1,0:T(8,128)(2,1)S(1)} %get-tuple-element.116, bf16[9,1024]{1,0:T(8,128)(2,1)S(1)} %get-tuple-element.117, bf16[9,1024]{1,0:T(8,128)(2,1)S(1)} %get-tuple-element.115), kind=kOutput, calls=%fused_computation.6 | convolution fusion | flops 115509248 | bytes 280576 | tf_op jit(solution)/shard_map/dot_general | solution.py:324
  67.3 0.1 reshape.524
  67.4 0.2 copy.158
  67.6 0.9 reshape.567
  68.5 13.1 %all-to-all-start.2 = ((f32[64,1,288]{2,1,0:T(1,128)}), f32[64,1,288]{2,1,0:T(1,128)S(1)}, u32[]{:S(2)}, u32[]{:S(2)}) async-start(f32[64,1,288]{2,1,0:T(1,128)} %reshape.567), calls=%async_computation.2 | async-start | bytes 196608 | tf_op jit(solution)/shard_map/all_to_all | solution.py:412
  81.6 0.7 copy.90
  82.4 8.6 %all-to-all-done.2 = f32[64,1,288]{2,1,0:T(1,128)S(1)} async-done(((f32[64,1,288]{2,1,0:T(1,128)}), f32[64,1,288]{2,1,0:T(1,128)S(1)}, u32[]{:S(2)}, u32[]{:S(2)}) %all-to-all-start.2) | async-done | bytes 73760 | tf_op jit(solution)/shard_map/all_to_all | solution.py:412
  91.0 0.8 reduce.15
  91.8 0.1 reshape.568
  92.0 0.2 reshape.525
  92.2 3.3 %fusion = f32[27,2048]{1,0:T(8,128)S(1)} fusion(s32[2048]{0:T(1024)S(1)} %eq.47, bf16[9,2048]{1,0:T(8,128)(2,1)S(1)} %get-tuple-element.95, bf16[9,2048]{1,0:T(8,128)(2,1)S(1)} %get-tuple-element.96, bf16[9,2048]{1,0:T(8,128)(2,1)S(1)} %get-tuple-element.94), kind=kOutput, calls=%fused_computation.1 | convolution fusion | flops 231018496 | bytes 339968 | tf_op jit(solution)/shard_map/dot_general | solution.py:324
  95.7 13.6 %all_gather.3 = f32[4,145,128]{2,1,0:T(8,128)S(1)} all-gather(f32[1,145,128]{2,1,0:T(8,128)S(1)} %fusion.50), channel_id=1, replica_groups=mesh['tiles'=64,'views'=4] {'views'}, dimensions={0}, use_global_device_ids=true | all-gather | bytes 371200 | tf_op jit(solution)/shard_map/all_gather | solution.py:415
  109.6 0.3 convolution_add_fusion
  109.9 0.5 fusion.45
  110.4 0.1 multiply_reduce_fusion.5
  110.9 1.3 %multiply_reduce_fusion.2 = (f32[4,3,2048]{2,1,0:T(4,128)S(1)}, f32[4,3,3,2048]{3,1,2,0:T(4,128)S(1)}) fusion(f32[3,3,2048]{2,0,1:T(4,128)S(1)} %copy.85, f32[4,3,3,2048]{3,0,2,1:T(4,128)S(1)} %pad_add_fusion, f32[4,3,3]{2,1,0:T(4,128)S(1)} %reshape.528), kind=kOutput, calls=%fused_computation.30 | convolution fusion | flops 2777088 | bytes 762000 | tf_op jit(solution)/shard_map/vmap(transpose(jvp(ik,kjg->ijg)))/dot_general | solution.py:87
  112.2 0.2 copy_multiply_fusion
  112.7 0.2 fusion.169
  113.0 0.1 fusion.37
  113.7 0.7 broadcast_multiply_fusion
  114.3 0.1 add_add_fusion.5
  114.6 0.1 add_add_fusion.4
  114.7 0.2 fusion.42
  115.0 0.4 fusion.34
  115.5 0.1 fusion.38
  115.7 0.1 fusion.36
  115.8 0.2 fusion.77
  116.1 0.9 add_reduce_fusion
  117.0 1.3 %divide_subtract_fusion = (f32[59,2048]{1,0:T(8,128)}, f32[59,2048]{1,0:T(8,128)}, f32[59,2048]{1,0:T(8,128)}) fusion(f32[59,2048]{1,0:T(8,128)S(1)} %copy-done.1, f32[59]{0:T(128)S(1)} %copy-done.6, f32[59,2048]{1,0:T(8,128)S(1)} %add_reduce_fusion, f32[59,2048]{1,0:T(8,128)S(1)} %copy-done.2, f32[59,2048]{1,0:T(8,128)S(1)} %copy-done.3), kind=kLoop, calls=%fused_computation.25 | loop fusion | flops 1329152 | bytes 3383532 | tf_op jit(solution)/shard_map/sub | solution.py:335
  (115 shorter events, 4.0 us)
Async XLA Ops:
  0.6 17.7 %copy-start = (f32[16,12]{1,0:T(8,128)S(1)}, f32[16,12]{1,0:T(8,128)}, u32[]{:S(2)}) copy-start(f32[16,12]{1,0:T(8,128)} %param.15) | copy-start | bytes 2308
  0.6 17.8 %copy-start.1 = (f32[59,2048]{1,0:T(8,128)S(1)}, f32[59,2048]{1,0:T(8,128)}, u32[]{:S(2)}) copy-start(f32[59,2048]{1,0:T(8,128)} %param.11) | copy-start | bytes 1449988
  5.7 20.6 %all-to-all-start = ((s32[64,1,32]{2,1,0:T(1,128)}), s32[64,1,32]{2,1,0:T(1,128)S(1)}, u32[]{:S(2)}, u32[]{:S(2)}) async-start(s32[64,1,32]{2,1,0:T(1,128)} %bitcast.22), calls=%async_computation | async-start | bytes 65536 | tf_op jit(solution)/shard_map/all_to_all | solution.py:376
  31.1 6.8 %copy-start.7 = (f32[3]{0:T(128)S(1)}, f32[3]{0:T(128)}, u32[]{:S(2)}) copy-start(f32[3]{0:T(128)} %param.21) | copy-start | bytes 40
  31.1 8.2 %copy-start.5 = (bf16[1,1,3,1024]{3,2,1,0:T(4,128)(2,1)S(1)}, bf16[1,1,3,1024]{3,2,1,0:T(4,128)(2,1)}, u32[]{:S(2)}) copy-start(bf16[1,1,3,1024]{3,2,1,0:T(4,128)(2,1)} %param.20) | copy-start | bytes 18436
  32.3 14.9 %all-to-all-start.1 = ((f32[64,1,288]{2,1,0:T(1,128)}), f32[64,1,288]{2,1,0:T(1,128)S(1)}, u32[]{:S(2)}, u32[]{:S(2)}) async-start(f32[64,1,288]{2,1,0:T(1,128)} %reshape.565), calls=%async_computation.1 | async-start | bytes 196608 | tf_op jit(solution)/shard_map/all_to_all | solution.py:379
  67.2 14.3 %copy-start.4 = (f32[1,1024,8]{2,1,0:T(8,128)S(1)}, f32[1,1024,8]{2,1,0:T(8,128)}, u32[]{:S(2)}) copy-start(f32[1,1024,8]{2,1,0:T(8,128)} %get-tuple-element.6) | copy-start | bytes 98308
  68.5 22.5 %all-to-all-start.2 = ((f32[64,1,288]{2,1,0:T(1,128)}), f32[64,1,288]{2,1,0:T(1,128)S(1)}, u32[]{:S(2)}, u32[]{:S(2)}) async-start(f32[64,1,288]{2,1,0:T(1,128)} %reshape.567), calls=%async_computation.2 | async-start | bytes 196608 | tf_op jit(solution)/shard_map/all_to_all | solution.py:412
  115.8 1.2 %copy-start.2 = (f32[59,2048]{1,0:T(8,128)S(1)}, f32[59,2048]{1,0:T(8,128)}, u32[]{:S(2)}) copy-start(f32[59,2048]{1,0:T(8,128)} %param.12) | copy-start | bytes 1449988
  115.8 1.2 %copy-start.3 = (f32[59,2048]{1,0:T(8,128)S(1)}, f32[59,2048]{1,0:T(8,128)}, u32[]{:S(2)}) copy-start(f32[59,2048]{1,0:T(8,128)} %param.13) | copy-start | bytes 1449988
  115.8 1.2 %copy-start.6 = (f32[59]{0:T(128)S(1)}, f32[59]{0:T(128)}, u32[]{:S(2)}) copy-start(f32[59]{0:T(128)} %param.14) | copy-start | bytes 712

commit v9 on v8

--- a/solution.py
+++ b/solution.py
@@ -202,7 +202,7 @@
 
 
 def render_kernel(
-    counts_ref, tiles_ref, entry_ref, target_ref, bg_ref, image_ref, sums_ref, trans_ref, fall_ref, *, tile_cols
+    counts_ref, tiles_ref, entry_ref, target_ref, bg_ref, image_ref, sums_ref, trans_ref, fall_ref, inv_ref, *, tile_cols
 ):
     t = pl.program_id(0)
     count = counts_ref[t]
@@ -229,12 +229,13 @@
         power = -0.5 * (blk[2:3] * dx * dx + 2.0 * blk[3:4] * dx * dy + blk[4:5] * dy * dy)
         falloff = jnp.exp(power)
         alpha = jnp.where(live, blk[5:6] * falloff, 0.0)
-        log_keep = jnp.log1p(-alpha)
+        log_keep = jnp.log(1.0 - alpha)
         cum = split_cumsum(log_keep, upper)
         trans = jnp.exp(log_total + cum - log_keep)
         weight = trans * alpha
         trans_ref[:, pl.ds(start, KB)] = trans
         fall_ref[:, pl.ds(start, KB)] = falloff
+        inv_ref[:, pl.ds(start, KB)] = jnp.exp(-log_keep)
         return (
             log_total + cum[:, KB - 1 : KB],
             red + weight * blk[8:9],
@@ -266,7 +267,7 @@
         weight = trans * alpha
         along = resid_r * blk[8:9] + resid_g * blk[9:10] + resid_b * blk[10:11]
         running = prefix + split_cumsum(weight * along, upper)
-        d_alpha = jnp.where(live, trans * along - (dot_total - running) / (1.0 - alpha), 0.0)
+        d_alpha = jnp.where(live, trans * along - (dot_total - running) * inv_ref[:, pl.ds(start, KB)], 0.0)
         d_power = d_alpha * alpha
         x_term = d_power * dx
         y_term = d_power * dy
@@ -309,6 +310,7 @@
             jax.ShapeDtypeStruct((n, 16, LIST), jnp.float32),
         ],
         scratch_shapes=[
+            pltpu.VMEM((PIXELS, LIST), jnp.float32),
             pltpu.VMEM((PIXELS, LIST), jnp.float32),
             pltpu.VMEM((PIXELS, LIST), jnp.float32),
         ],

time: 120 us -> 119 us (level)
  starting transfers between devices: 30.6 us -> 26.3 us
  Pallas kernels: 11.9 us -> 15.4 us
    all_to_all x1, starting transfers between devices: 13.1 us -> 8.8 us  [body(): lax.all_to_all(grad_send, 'tiles', split_axis=1, concat_axis=1, tiled=True)]
    pallas_call x1, Pallas kernels: 11.9 us -> 15.4 us  [render_tiles(): pl.pallas_call(partial(render_kernel, tile_cols=tile_cols), grid=(n,), in...]
where the time goes in v9:
time: 119 us; the launch traced here: 117 us
  starting transfers between devices  26.3 us (22%)
  waiting for transfers between devices  20.4 us (17%)
  other arithmetic  15.4 us (13%)
  matrix products  15.4 us (13%)
  Pallas kernels  15.4 us (13%)
  blocking collectives  13.2 us (11%)
  local copies, waits for them, and re-layouts  8.2 us (7%)
  between operations  2.76 us (2%)
    pallas_call x1, Pallas kernels, render_tiles(): pl.pallas_call(partial(render_kernel, tile_cols=tile_cols), grid=(n,), in...  15.4 us
    all_gather x1, blocking collectives, body(): lax.all_gather(payload.reshape(-1, 128), 'views', axis=0, tiled=False)  13.2 us
    dot_general x5, matrix products, select_rows(): lax.dot_general(pieces, chosen, (((1,), (contract,)), ((), ())), preferre...  12 us
    all_to_all x1, starting transfers between devices, body(): lax.all_to_all(asked_for, 'tiles', split_axis=0, concat_axis=0, tiled=True)  12 us
    all_to_all x1, starting transfers between devices, body(): lax.all_to_all(grad_send, 'tiles', split_axis=1, concat_axis=1, tiled=True)  8.8 us
    all_to_all x1, waiting for transfers between devices, body(): lax.all_to_all(grad_send, 'tiles', split_axis=1, concat_axis=1, tiled=True)  8.61 us
    all_to_all x1, waiting for transfers between devices, body(): lax.all_to_all(served, 'tiles', split_axis=1, concat_axis=1, tiled=True)  6.94 us
    all_to_all x1, starting transfers between devices, body(): lax.all_to_all(served, 'tiles', split_axis=1, concat_axis=1, tiled=True)  5.52 us
  transfers between devices with their start and end apart: 3, of which 3 were waited for; matrix products, arithmetic and copies ran while one was open for 4% of the time, Pallas kernels for 0%

profile of v9, /device:TPU:2, one launch (start us, length us, event | category | flops | bytes accessed | tf_op | source)
XLA Modules:
  0.0 117.2 jit_solution(2629248843614829512)
XLA Ops:
  0.7 1.3 %convert_reduce_fusion = s32[1024]{0:T(1024)S(1)} fusion(s32[1024]{0:T(1024)} %bitcast.472), kind=kLoop, calls=%fused_computation.12 | loop fusion | flops 5241856 | bytes 8192 | tf_op jit(solution)/shard_map/reduce_sum | solution.py:370
  1.9 0.7 multiply_add_fusion.7
  2.6 0.7 reduce-precision_convert_fusion.9
  3.3 1.6 %fusion.6 = f32[3,2048]{1,0:T(4,128)S(1)} fusion(s32[1024]{0:T(1024)S(1)} %multiply_add_fusion.7, bf16[1,1024]{1,0:T(2,128)(2,1)S(1)} %get-tuple-element.164, bf16[1,1024]{1,0:T(2,128)(2,1)S(1)} %get-tuple-element.165, bf16[1,1024]{1,0:T(2,128)(2,1)S(1)} %get-tuple-element.163), kind=kOutput, calls=%fused_computation.8 | convolution fusion | flops 14698496 | bytes 34816 | tf_op jit(solution)/shard_map/dot_general | solution.py:326
  5.0 0.7 all_to_all.12
  5.7 12.0 %all-to-all-start = ((s32[64,1,32]{2,1,0:T(1,128)}), s32[64,1,32]{2,1,0:T(1,128)S(1)}, u32[]{:S(2)}, u32[]{:S(2)}) async-start(s32[64,1,32]{2,1,0:T(1,128)} %bitcast.22), calls=%async_computation | async-start | bytes 65536 | tf_op jit(solution)/shard_map/all_to_all | solution.py:378
  18.7 0.2 fusion.11
  18.9 0.1 multiply_reduce_fusion.6
  19.0 0.2 convolution_add_fusion.1
  19.9 0.3 fusion.48
  20.4 0.2 reshape.520
  20.6 0.2 stack.30
  20.8 0.1 multiply_reduce_fusion.1
  21.0 0.2 concatenate.29
  21.3 4.9 %all-to-all-done = s32[64,1,32]{2,1,0:T(1,128)S(1)} async-done(((s32[64,1,32]{2,1,0:T(1,128)}), s32[64,1,32]{2,1,0:T(1,128)S(1)}, u32[]{:S(2)}, u32[]{:S(2)}) %all-to-all-start) | async-done | bytes 8224 | tf_op jit(solution)/shard_map/all_to_all | solution.py:378
  26.2 0.5 broadcast.804
  26.7 0.7 reduce.13
  27.5 3.6 %fusion.1 = f32[27,2048]{1,0:T(8,128)S(1)} fusion(s32[2048]{0:T(1024)S(1)} %eq.47, bf16[9,2048]{1,0:T(8,128)(2,1)S(1)} %get-tuple-element.103, bf16[9,2048]{1,0:T(8,128)(2,1)S(1)} %get-tuple-element.104, bf16[9,2048]{1,0:T(8,128)(2,1)S(1)} %get-tuple-element.102), kind=kOutput, calls=%fused_computation.2 | convolution fusion | flops 231018496 | bytes 339968 | tf_op jit(solution)/shard_map/dot_general | solution.py:326
  31.2 0.1 reshape.522
  31.3 0.2 copy.159
  31.5 0.9 reshape.565
  32.3 5.5 %all-to-all-start.1 = ((f32[64,1,288]{2,1,0:T(1,128)}), f32[64,1,288]{2,1,0:T(1,128)S(1)}, u32[]{:S(2)}, u32[]{:S(2)}) async-start(f32[64,1,288]{2,1,0:T(1,128)} %reshape.565), calls=%async_computation.1 | async-start | bytes 196608 | tf_op jit(solution)/shard_map/all_to_all | solution.py:381
  37.9 0.5 pad_bitcast_fusion.bg_ref
  39.3 0.2 copy.75
  39.5 0.8 pad_convert_fusion.target_ref
  40.3 6.9 %all-to-all-done.1 = f32[64,1,288]{2,1,0:T(1,128)S(1)} async-done(((f32[64,1,288]{2,1,0:T(1,128)}), f32[64,1,288]{2,1,0:T(1,128)S(1)}, u32[]{:S(2)}, u32[]{:S(2)}) %all-to-all-start.1) | async-done | bytes 73760 | tf_op jit(solution)/shard_map/all_to_all | solution.py:381
  47.2 0.5 broadcast.810
  47.8 0.8 reduce.14
  48.6 0.1 reshape.566
  48.9 0.2 reshape.523
  49.1 1.8 %fusion.5 = f32[27,1024]{1,0:T(8,128)S(1)} fusion(s32[1024]{0:T(1024)S(1)} %multiply_add_fusion.7, bf16[9,2048]{1,0:T(8,128)(2,1)S(1)} %get-tuple-element.100, bf16[9,2048]{1,0:T(8,128)(2,1)S(1)} %get-tuple-element.101, bf16[9,2048]{1,0:T(8,128)(2,1)S(1)} %get-tuple-element.99), kind=kOutput, calls=%fused_computation.7 | convolution fusion | flops 115675136 | bytes 225280 | tf_op jit(solution)/shard_map/dot_general | solution.py:326
  50.9 0.7 maximum_bitcast_fusion.entry_ref
  51.6 15.4 %shard_map.138 = (f32[1,1024,8]{2,1,0:T(8,128)}, f32[1,16,1024]{2,1,0:T(8,128)}) custom-call(s32[1]{0:T(128)} %bitcast.426.counts_ref, s32[1]{0:T(128)} %bitcast.1.tiles_ref, f32[1,16,1024]{2,1,0:T(8,128)} %maximum_bitcast_fusion.entry_ref, f32[1,1024,8]{2,1,0:T(8,128)} %pad_convert_fusion.target_ref, f32[1,8]{1,0:T(1,128)} %pad_bitcast_fusion.bg_ref), custom_call_target="tpu_custom_call" | custom-call | tf_op jit(solution)/shard_map/pallas_call | solution.py:294
  67.1 0.9 fusion.144
  67.9 1.0 slice_bitcast_fusion.8
  69.0 1.7 %fusion.4 = f32[27,2048]{1,0:T(8,128)S(1)} fusion(s32[1024]{0:T(1024)S(1)} %multiply_add_fusion.7, bf16[9,1024]{1,0:T(8,128)(2,1)S(1)} %get-tuple-element.116, bf16[9,1024]{1,0:T(8,128)(2,1)S(1)} %get-tuple-element.117, bf16[9,1024]{1,0:T(8,128)(2,1)S(1)} %get-tuple-element.115), kind=kOutput, calls=%fused_computation.6 | convolution fusion | flops 115509248 | bytes 280576 | tf_op jit(solution)/shard_map/dot_general | solution.py:326
  70.8 0.1 reshape.524
  70.9 0.2 copy.158
  71.1 0.9 reshape.567
  72.0 8.8 %all-to-all-start.2 = ((f32[64,1,288]{2,1,0:T(1,128)}), f32[64,1,288]{2,1,0:T(1,128)S(1)}, u32[]{:S(2)}, u32[]{:S(2)}) async-start(f32[64,1,288]{2,1,0:T(1,128)} %reshape.567), calls=%async_computation.2 | async-start | bytes 196608 | tf_op jit(solution)/shard_map/all_to_all | solution.py:414
  80.8 0.7 copy.90
  81.6 8.6 %all-to-all-done.2 = f32[64,1,288]{2,1,0:T(1,128)S(1)} async-done(((f32[64,1,288]{2,1,0:T(1,128)}), f32[64,1,288]{2,1,0:T(1,128)S(1)}, u32[]{:S(2)}, u32[]{:S(2)}) %all-to-all-start.2) | async-done | bytes 73760 | tf_op jit(solution)/shard_map/all_to_all | solution.py:414
  90.2 0.8 reduce.15
  91.0 0.1 reshape.568
  91.3 0.2 reshape.525
  91.5 3.3 %fusion = f32[27,2048]{1,0:T(8,128)S(1)} fusion(s32[2048]{0:T(1024)S(1)} %eq.47, bf16[9,2048]{1,0:T(8,128)(2,1)S(1)} %get-tuple-element.95, bf16[9,2048]{1,0:T(8,128)(2,1)S(1)} %get-tuple-element.96, bf16[9,2048]{1,0:T(8,128)(2,1)S(1)} %get-tuple-element.94), kind=kOutput, calls=%fused_computation.1 | convolution fusion | flops 231018496 | bytes 339968 | tf_op jit(solution)/shard_map/dot_general | solution.py:326
  94.9 13.2 %all_gather.3 = f32[4,145,128]{2,1,0:T(8,128)S(1)} all-gather(f32[1,145,128]{2,1,0:T(8,128)S(1)} %fusion.50), channel_id=1, replica_groups=mesh['tiles'=64,'views'=4] {'views'}, dimensions={0}, use_global_device_ids=true | all-gather | bytes 371200 | tf_op jit(solution)/shard_map/all_gather | solution.py:417
  108.5 0.3 convolution_add_fusion
  108.8 0.5 fusion.45
  109.3 0.1 multiply_reduce_fusion.5
  109.7 1.3 %multiply_reduce_fusion.2 = (f32[4,3,2048]{2,1,0:T(4,128)S(1)}, f32[4,3,3,2048]{3,1,2,0:T(4,128)S(1)}) fusion(f32[3,3,2048]{2,0,1:T(4,128)S(1)} %copy.85, f32[4,3,3,2048]{3,0,2,1:T(4,128)S(1)} %pad_add_fusion, f32[4,3,3]{2,1,0:T(4,128)S(1)} %reshape.528), kind=kOutput, calls=%fused_computation.30 | convolution fusion | flops 2777088 | bytes 762000 | tf_op jit(solution)/shard_map/vmap(transpose(jvp(ik,kjg->ijg)))/dot_general | solution.py:87
  111.1 0.2 copy_multiply_fusion
  111.6 0.2 fusion.169
  111.8 0.1 fusion.37
  112.5 0.7 broadcast_multiply_fusion
  113.2 0.1 add_add_fusion.5
  113.4 0.1 add_add_fusion.4
  113.6 0.2 fusion.42
  113.9 0.4 fusion.34
  114.4 0.1 fusion.38
  114.5 0.1 fusion.36
  114.7 0.2 fusion.77
  114.9 0.9 add_reduce_fusion
  115.9 1.3 %divide_subtract_fusion = (f32[59,2048]{1,0:T(8,128)}, f32[59,2048]{1,0:T(8,128)}, f32[59,2048]{1,0:T(8,128)}) fusion(f32[59,2048]{1,0:T(8,128)S(1)} %copy-done.1, f32[59]{0:T(128)S(1)} %copy-done.6, f32[59,2048]{1,0:T(8,128)S(1)} %add_reduce_fusion, f32[59,2048]{1,0:T(8,128)S(1)} %copy-done.2, f32[59,2048]{1,0:T(8,128)S(1)} %copy-done.3), kind=kLoop, calls=%fused_computation.25 | loop fusion | flops 1329152 | bytes 3383532 | tf_op jit(solution)/shard_map/sub | solution.py:337
  (115 shorter events, 4.0 us)
Async XLA Ops:
  0.6 17.7 %copy-start = (f32[16,12]{1,0:T(8,128)S(1)}, f32[16,12]{1,0:T(8,128)}, u32[]{:S(2)}) copy-start(f32[16,12]{1,0:T(8,128)} %param.15) | copy-start | bytes 2308
  0.6 17.8 %copy-start.1 = (f32[59,2048]{1,0:T(8,128)S(1)}, f32[59,2048]{1,0:T(8,128)}, u32[]{:S(2)}) copy-start(f32[59,2048]{1,0:T(8,128)} %param.11) | copy-start | bytes 1449988
  5.7 20.6 %all-to-all-start = ((s32[64,1,32]{2,1,0:T(1,128)}), s32[64,1,32]{2,1,0:T(1,128)S(1)}, u32[]{:S(2)}, u32[]{:S(2)}) async-start(s32[64,1,32]{2,1,0:T(1,128)} %bitcast.22), calls=%async_computation | async-start | bytes 65536 | tf_op jit(solution)/shard_map/all_to_all | solution.py:378
  31.1 6.8 %copy-start.7 = (f32[3]{0:T(128)S(1)}, f32[3]{0:T(128)}, u32[]{:S(2)}) copy-start(f32[3]{0:T(128)} %param.21) | copy-start | bytes 40
  31.1 8.2 %copy-start.5 = (bf16[1,1,3,1024]{3,2,1,0:T(4,128)(2,1)S(1)}, bf16[1,1,3,1024]{3,2,1,0:T(4,128)(2,1)}, u32[]{:S(2)}) copy-start(bf16[1,1,3,1024]{3,2,1,0:T(4,128)(2,1)} %param.20) | copy-start | bytes 18436
  32.3 14.9 %all-to-all-start.1 = ((f32[64,1,288]{2,1,0:T(1,128)}), f32[64,1,288]{2,1,0:T(1,128)S(1)}, u32[]{:S(2)}, u32[]{:S(2)}) async-start(f32[64,1,288]{2,1,0:T(1,128)} %reshape.565), calls=%async_computation.1 | async-start | bytes 196608 | tf_op jit(solution)/shard_map/all_to_all | solution.py:381
  70.8 10.0 %copy-start.4 = (f32[1,1024,8]{2,1,0:T(8,128)S(1)}, f32[1,1024,8]{2,1,0:T(8,128)}, u32[]{:S(2)}) copy-start(f32[1,1024,8]{2,1,0:T(8,128)} %get-tuple-element.6) | copy-start | bytes 98308
  72.0 18.2 %all-to-all-start.2 = ((f32[64,1,288]{2,1,0:T(1,128)}), f32[64,1,288]{2,1,0:T(1,128)S(1)}, u32[]{:S(2)}, u32[]{:S(2)}) async-start(f32[64,1,288]{2,1,0:T(1,128)} %reshape.567), calls=%async_computation.2 | async-start | bytes 196608 | tf_op jit(solution)/shard_map/all_to_all | solution.py:414
  114.7 1.2 %copy-start.2 = (f32[59,2048]{1,0:T(8,128)S(1)}, f32[59,2048]{1,0:T(8,128)}, u32[]{:S(2)}) copy-start(f32[59,2048]{1,0:T(8,128)} %param.12) | copy-start | bytes 1449988
  114.7 1.2 %copy-start.3 = (f32[59,2048]{1,0:T(8,128)S(1)}, f32[59,2048]{1,0:T(8,128)}, u32[]{:S(2)}) copy-start(f32[59,2048]{1,0:T(8,128)} %param.13) | copy-start | bytes 1449988
  114.7 1.2 %copy-start.6 = (f32[59]{0:T(128)S(1)}, f32[59]{0:T(128)}, u32[]{:S(2)}) copy-start(f32[59]{0:T(128)} %param.14) | copy-start | bytes 712
